TPU v7x, 256 devices: a whole 4x4x8 slice. The times are simulated.
256 devices in a mesh: seq: 32 (over z, y), head: 8 (over x, core).
Axes of the slice: x: 4, y: 4, z: 8, core: 2. Of those that a mesh axis runs over, the one named last changes fastest.
Arguments:
- query_proj: bfloat16 [8192, 2048], P('seq', 'head'), may hold values from -40 to 40
- key_proj: bfloat16 [8192, 2048], P('seq', 'head'), may hold values from -40 to 40
- value_proj: bfloat16 [8192, 4096], P('seq', 'head'), may hold values from -40 to 40
- gate_proj: bfloat16 [8192, 4096], P('seq', 'head'), may hold values from -6 to 6
- strength: float32 [32, 8192], P('head', 'seq'), may hold values from 0 to 2, as said below
- log_decay: float32 [32, 8192], P('head', 'seq'), may hold values from -1 to 0, as said below
- conv_query: bfloat16 [4, 2048], P(None, 'head'), may hold values from -3 to 3
- conv_key: bfloat16 [4, 2048], P(None, 'head'), may hold values from -3 to 3
- conv_value: bfloat16 [4, 4096], P(None, 'head'), may hold values from -3 to 3
- norm_gain: bfloat16 [128], replicated, may hold values from 0.099609375 to 1.8984375
- out_weight: bfloat16 [4096, 2048], P('head'), may hold values from -0.09375 to 0.09375
Outputs:
- layer_out: bfloat16 [8192, 2048], P(('seq', 'head'))
Inputs may be any that keep to these rules, and one draw needn't show every extreme that they name: `strength`: strictly inside the range. `log_decay`: strictly below the upper end.
All inputs are finite; a program needn't handle non-finite values.
Results may differ from a plain program's by a relative error of at most 0.014.
Values may be sent and summed in bfloat16 or wider, within the bound.
No kernel may reach another device: no remote copies, remote signals or barrier semaphores. Data moves between devices by JAX's collectives and lax.ppermute only.
A program may use at most 64 MiB of HBM per device.

v0:
```python
import jax
import jax.numpy as jnp
from jax import lax
from jax.sharding import PartitionSpec as P

DK = 128
DV = 128
SPAN = 128


epsilon = 1e-06
highest = lax.Precision.HIGHEST


def shifted(array, axis, by):
    length = lax.axis_size(axis)
    pairs = [(i, i + by) for i in range(length) if 0 <= i + by < length]
    return lax.ppermute(array, axis, pairs)


def conv_silu(signal, before, weights):
    length = signal.shape[0]
    padded = jnp.concatenate([before, signal], axis=0).astype(jnp.float32)
    conv_taps = weights.astype(jnp.float32)
    summed = jnp.zeros(signal.shape, jnp.float32)
    for offset in range(conv_taps.shape[0]):
        summed = summed + conv_taps[offset] * padded[offset : offset + length]
    return jax.nn.silu(summed)


def apply_map(matrix, state_now):
    return jnp.einsum("hrke,hrev->hrkv", matrix, state_now, precision=highest)


def shards(
    query_proj,
    key_proj,
    value_proj,
    gate_proj,
    strength,
    log_decay,
    conv_query,
    conv_key,
    conv_value,
    norm_gain,
    out_weight,
):
    local_rows = query_proj.shape[0]
    rim_width = conv_query.shape[0] - 1
    before_query, before_key, before_value = shifted(
        (
            query_proj[local_rows - rim_width :],
            key_proj[local_rows - rim_width :],
            value_proj[local_rows - rim_width :],
        ),
        "seq",
        1,
    )
    key_heads = key_proj.shape[1] // DK
    value_heads = value_proj.shape[1] // DV
    ratio_heads = value_heads // key_heads
    spans = local_rows // SPAN
    queries = conv_silu(query_proj, before_query, conv_query)
    key_rows = conv_silu(key_proj, before_key, conv_key).reshape(local_rows, key_heads, DK)
    key_rows = key_rows / jnp.sqrt(jnp.sum(key_rows * key_rows, axis=-1, keepdims=True) + epsilon)
    values = conv_silu(value_proj, before_value, conv_value)
    query_blocks = queries.reshape(spans, SPAN, key_heads, DK).transpose(2, 0, 1, 3)[:, None]
    key_blocks = key_rows.reshape(spans, SPAN, key_heads, DK).transpose(2, 0, 1, 3)[:, None]
    value_blocks = values.reshape(spans, SPAN, key_heads, ratio_heads, DV).transpose(2, 3, 0, 1, 4)
    strength_blocks = strength.reshape(key_heads, ratio_heads, spans, SPAN)
    decay_blocks = log_decay.reshape(key_heads, ratio_heads, spans, SPAN)
    cumulative = jnp.cumsum(decay_blocks, axis=-1)
    positions = jnp.arange(SPAN)
    inclusive = positions[:, None] >= positions[None, :]
    strictly = positions[:, None] > positions[None, :]
    log_gaps = cumulative[..., :, None] - cumulative[..., None, :]
    decays = jnp.where(inclusive, jnp.exp(jnp.where(inclusive, log_gaps, 0.0)), 0.0)
    key_key = jnp.einsum("hxnck,hxnek->hxnce", key_blocks, key_blocks, precision=highest)
    query_key = jnp.einsum("hxnck,hxnek->hxnce", query_blocks, key_blocks, precision=highest)
    lower_part = jnp.where(strictly, strength_blocks[..., None] * decays * key_key, 0.0)
    system = lower_part + jnp.eye(SPAN, dtype=jnp.float32)
    right_side = jnp.concatenate(
        [
            strength_blocks[..., None] * value_blocks,
            (strength_blocks * jnp.exp(cumulative))[..., None] * key_blocks,
        ],
        axis=-1,
    )
    solved = lax.linalg.triangular_solve(
        system, right_side, left_side=True, lower=True, unit_diagonal=True
    )
    value_part = solved[..., :DV]
    key_part = solved[..., DV:]
    attention = decays * query_key
    local_out = jnp.einsum("hrnce,hrnev->hrncv", attention, value_part, precision=highest)
    coupling = jnp.exp(cumulative)[..., None] * query_blocks - jnp.einsum(
        "hrnce,hrnek->hrnck", attention, key_part, precision=highest
    )
    span_end = cumulative[..., -1:]
    scaled_keys = jnp.exp(span_end - cumulative)[..., None] * key_blocks
    transit = jnp.exp(span_end)[..., None] * jnp.eye(DK, dtype=jnp.float32) - jnp.einsum(
        "hrnck,hrnce->hrnke", scaled_keys, key_part, precision=highest
    )
    inject = jnp.einsum("hrnck,hrncv->hrnkv", scaled_keys, value_part, precision=highest)
    transit_seq = jnp.moveaxis(transit, 2, 0)
    inject_seq = jnp.moveaxis(inject, 2, 0)
    identity = jnp.broadcast_to(jnp.eye(DK, dtype=jnp.float32), (key_heads, ratio_heads, DK, DK))
    zero_state = jnp.zeros((key_heads, ratio_heads, DK, DV), jnp.float32)

    def sweep_spans(carried, span_in):
        prefix, state_now = carried
        transit_now, inject_now = span_in
        return (
            (apply_map(transit_now, prefix), apply_map(transit_now, state_now) + inject_now),
            None,
        )

    (total_map, local_end), ignored = lax.scan(
        sweep_spans, (identity, zero_state), (transit_seq, inject_seq)
    )

    def relay_step(hop_index, state_now):
        return shifted(apply_map(total_map, state_now) + local_end, "seq", 1)

    incoming = lax.fori_loop(0, lax.axis_size("seq") - 1, relay_step, zero_state)

    def replay(state_now, span_in):
        transit_now, inject_now, coupling_now, local_now = span_in
        span_out = (
            jnp.einsum("hrck,hrkv->hrcv", coupling_now, state_now, precision=highest) + local_now
        )
        return (apply_map(transit_now, state_now) + inject_now, span_out)

    ignored_state, outputs = lax.scan(
        replay,
        incoming,
        (transit_seq, inject_seq, jnp.moveaxis(coupling, 2, 0), jnp.moveaxis(local_out, 2, 0)),
    )
    core_out = jnp.moveaxis(outputs, 0, 2)
    core_out = core_out.transpose(2, 3, 0, 1, 4).reshape(local_rows, value_heads, DV)
    gate_values = gate_proj.astype(jnp.float32).reshape(local_rows, value_heads, DV)
    scale_rows = lax.rsqrt(jnp.mean(core_out * core_out, axis=-1, keepdims=True) + epsilon)
    normed = core_out * scale_rows * norm_gain.astype(jnp.float32) * jax.nn.silu(gate_values)
    hidden = normed.reshape(local_rows, value_heads * DV).astype(jnp.bfloat16)
    return lax.psum_scatter(
        jnp.dot(hidden, out_weight, preferred_element_type=jnp.float32).astype(jnp.bfloat16),
        "head",
        scatter_dimension=0,
        tiled=True,
    )


def solution(mesh):
    placed = (
        P("seq", "head"),
        P("seq", "head"),
        P("seq", "head"),
        P("seq", "head"),
        P("head", "seq"),
        P("head", "seq"),
        P(None, "head"),
        P(None, "head"),
        P(None, "head"),
        P(),
        P("head", None),
    )
    return jax.shard_map(
        shards, mesh=mesh, in_specs=placed, out_specs=P(("seq", "head"), None), check_vma=False
    )
```

profile of v0, /device:TPU:128, one launch (start us, length us, event | category | flops | bytes accessed | tf_op | source)
XLA Modules:
  0.0 605.2 jit_solution(14393865314700446362)
XLA Ops:
  36.8 80.1 %custom-call.3 = f32[2,2,2,1,128,128]{4,5,3,2,1,0:T(8,128)} custom-call(f32[2,2,2,1,128,128]{5,4,3,2,1,0:T(8,128)} %select_add_fusion), custom_call_target="InvertDiagBlocksLowerTriangular" | custom-call | tf_op jit(solution)/shard_map/triangular_solve | solution.py:89
  135.5 415.6 %while.38 = (s32[]{:T(128)}, f32[2,2,128,128]{3,2,1,0:T(8,128)S(1)}, f32[2,2,128,128]{3,2,1,0:T(8,128)S(1)}, f32[2,2,128,128]{3,2,1,0:T(8,128)S(1)}) while((s32[]{:T(128)}, f32[2,2,128,128]{3,2,1,0:T(8,128)S(1)}, f32[2,2,128,128]{3,2,1,0:T(8,128)S(1)}, f32[2,2,128,128]{3,2,1,0:T(8,128)S(1)}) %tuple.82), condition=%wide.region_5.6_spmd.clone, body=%wide.region_4.5_spmd.sunk.clone | while | flops 100728832 | bytes 2097245 | solution.py:125
  139.2 10.0 %collective-permute-done = f32[2,2,128,128]{3,2,1,0:T(8,128)S(1)} collective-permute-done((f32[2,2,128,128]{3,2,1,0:T(8,128)}, f32[2,2,128,128]{3,2,1,0:T(8,128)S(1)}, u32[]{:S(2)}, u32[]{:S(2)}) %collective-permute-start) | collective-permute-done | bytes 262176 | tf_op jit(solution)/shard_map/while/body/eval_jaxpr/ppermute | solution.py:18
  152.3 9.9 %collective-permute-done = f32[2,2,128,128]{3,2,1,0:T(8,128)S(1)} collective-permute-done((f32[2,2,128,128]{3,2,1,0:T(8,128)}, f32[2,2,128,128]{3,2,1,0:T(8,128)S(1)}, u32[]{:S(2)}, u32[]{:S(2)}) %collective-permute-start) | collective-permute-done | bytes 262176 | tf_op jit(solution)/shard_map/while/body/eval_jaxpr/ppermute | solution.py:18
  178.0 9.9 %collective-permute-done = f32[2,2,128,128]{3,2,1,0:T(8,128)S(1)} collective-permute-done((f32[2,2,128,128]{3,2,1,0:T(8,128)}, f32[2,2,128,128]{3,2,1,0:T(8,128)S(1)}, u32[]{:S(2)}, u32[]{:S(2)}) %collective-permute-start) | collective-permute-done | bytes 262176 | tf_op jit(solution)/shard_map/while/body/eval_jaxpr/ppermute | solution.py:18
  229.6 10.7 %collective-permute-done = f32[2,2,128,128]{3,2,1,0:T(8,128)S(1)} collective-permute-done((f32[2,2,128,128]{3,2,1,0:T(8,128)}, f32[2,2,128,128]{3,2,1,0:T(8,128)S(1)}, u32[]{:S(2)}, u32[]{:S(2)}) %collective-permute-start) | collective-permute-done | bytes 262176 | tf_op jit(solution)/shard_map/while/body/eval_jaxpr/ppermute | solution.py:18
  243.2 11.8 %collective-permute-done = f32[2,2,128,128]{3,2,1,0:T(8,128)S(1)} collective-permute-done((f32[2,2,128,128]{3,2,1,0:T(8,128)}, f32[2,2,128,128]{3,2,1,0:T(8,128)S(1)}, u32[]{:S(2)}, u32[]{:S(2)}) %collective-permute-start) | collective-permute-done | bytes 262176 | tf_op jit(solution)/shard_map/while/body/eval_jaxpr/ppermute | solution.py:18
  258.1 12.4 %collective-permute-done = f32[2,2,128,128]{3,2,1,0:T(8,128)S(1)} collective-permute-done((f32[2,2,128,128]{3,2,1,0:T(8,128)}, f32[2,2,128,128]{3,2,1,0:T(8,128)S(1)}, u32[]{:S(2)}, u32[]{:S(2)}) %collective-permute-start) | collective-permute-done | bytes 262176 | tf_op jit(solution)/shard_map/while/body/eval_jaxpr/ppermute | solution.py:18
  273.5 11.5 %collective-permute-done = f32[2,2,128,128]{3,2,1,0:T(8,128)S(1)} collective-permute-done((f32[2,2,128,128]{3,2,1,0:T(8,128)}, f32[2,2,128,128]{3,2,1,0:T(8,128)S(1)}, u32[]{:S(2)}, u32[]{:S(2)}) %collective-permute-start) | collective-permute-done | bytes 262176 | tf_op jit(solution)/shard_map/while/body/eval_jaxpr/ppermute | solution.py:18
  288.0 10.7 %collective-permute-done = f32[2,2,128,128]{3,2,1,0:T(8,128)S(1)} collective-permute-done((f32[2,2,128,128]{3,2,1,0:T(8,128)}, f32[2,2,128,128]{3,2,1,0:T(8,128)S(1)}, u32[]{:S(2)}, u32[]{:S(2)}) %collective-permute-start) | collective-permute-done | bytes 262176 | tf_op jit(solution)/shard_map/while/body/eval_jaxpr/ppermute | solution.py:18
  314.6 9.9 %collective-permute-done = f32[2,2,128,128]{3,2,1,0:T(8,128)S(1)} collective-permute-done((f32[2,2,128,128]{3,2,1,0:T(8,128)}, f32[2,2,128,128]{3,2,1,0:T(8,128)S(1)}, u32[]{:S(2)}, u32[]{:S(2)}) %collective-permute-start) | collective-permute-done | bytes 262176 | tf_op jit(solution)/shard_map/while/body/eval_jaxpr/ppermute | solution.py:18
  327.5 9.9 %collective-permute-done = f32[2,2,128,128]{3,2,1,0:T(8,128)S(1)} collective-permute-done((f32[2,2,128,128]{3,2,1,0:T(8,128)}, f32[2,2,128,128]{3,2,1,0:T(8,128)S(1)}, u32[]{:S(2)}, u32[]{:S(2)}) %collective-permute-start) | collective-permute-done | bytes 262176 | tf_op jit(solution)/shard_map/while/body/eval_jaxpr/ppermute | solution.py:18
  340.3 9.9 %collective-permute-done = f32[2,2,128,128]{3,2,1,0:T(8,128)S(1)} collective-permute-done((f32[2,2,128,128]{3,2,1,0:T(8,128)}, f32[2,2,128,128]{3,2,1,0:T(8,128)S(1)}, u32[]{:S(2)}, u32[]{:S(2)}) %collective-permute-start) | collective-permute-done | bytes 262176 | tf_op jit(solution)/shard_map/while/body/eval_jaxpr/ppermute | solution.py:18
  366.1 9.9 %collective-permute-done = f32[2,2,128,128]{3,2,1,0:T(8,128)S(1)} collective-permute-done((f32[2,2,128,128]{3,2,1,0:T(8,128)}, f32[2,2,128,128]{3,2,1,0:T(8,128)S(1)}, u32[]{:S(2)}, u32[]{:S(2)}) %collective-permute-start) | collective-permute-done | bytes 262176 | tf_op jit(solution)/shard_map/while/body/eval_jaxpr/ppermute | solution.py:18
  379.0 10.7 %collective-permute-done = f32[2,2,128,128]{3,2,1,0:T(8,128)S(1)} collective-permute-done((f32[2,2,128,128]{3,2,1,0:T(8,128)}, f32[2,2,128,128]{3,2,1,0:T(8,128)S(1)}, u32[]{:S(2)}, u32[]{:S(2)}) %collective-permute-start) | collective-permute-done | bytes 262176 | tf_op jit(solution)/shard_map/while/body/eval_jaxpr/ppermute | solution.py:18
  392.7 11.8 %collective-permute-done = f32[2,2,128,128]{3,2,1,0:T(8,128)S(1)} collective-permute-done((f32[2,2,128,128]{3,2,1,0:T(8,128)}, f32[2,2,128,128]{3,2,1,0:T(8,128)S(1)}, u32[]{:S(2)}, u32[]{:S(2)}) %collective-permute-start) | collective-permute-done | bytes 262176 | tf_op jit(solution)/shard_map/while/body/eval_jaxpr/ppermute | solution.py:18
  407.6 12.4 %collective-permute-done = f32[2,2,128,128]{3,2,1,0:T(8,128)S(1)} collective-permute-done((f32[2,2,128,128]{3,2,1,0:T(8,128)}, f32[2,2,128,128]{3,2,1,0:T(8,128)S(1)}, u32[]{:S(2)}, u32[]{:S(2)}) %collective-permute-start) | collective-permute-done | bytes 262176 | tf_op jit(solution)/shard_map/while/body/eval_jaxpr/ppermute | solution.py:18
  422.9 11.5 %collective-permute-done = f32[2,2,128,128]{3,2,1,0:T(8,128)S(1)} collective-permute-done((f32[2,2,128,128]{3,2,1,0:T(8,128)}, f32[2,2,128,128]{3,2,1,0:T(8,128)S(1)}, u32[]{:S(2)}, u32[]{:S(2)}) %collective-permute-start) | collective-permute-done | bytes 262176 | tf_op jit(solution)/shard_map/while/body/eval_jaxpr/ppermute | solution.py:18
  437.4 10.6 %collective-permute-done = f32[2,2,128,128]{3,2,1,0:T(8,128)S(1)} collective-permute-done((f32[2,2,128,128]{3,2,1,0:T(8,128)}, f32[2,2,128,128]{3,2,1,0:T(8,128)S(1)}, u32[]{:S(2)}, u32[]{:S(2)}) %collective-permute-start) | collective-permute-done | bytes 262176 | tf_op jit(solution)/shard_map/while/body/eval_jaxpr/ppermute | solution.py:18
  464.0 9.9 %collective-permute-done = f32[2,2,128,128]{3,2,1,0:T(8,128)S(1)} collective-permute-done((f32[2,2,128,128]{3,2,1,0:T(8,128)}, f32[2,2,128,128]{3,2,1,0:T(8,128)S(1)}, u32[]{:S(2)}, u32[]{:S(2)}) %collective-permute-start) | collective-permute-done | bytes 262176 | tf_op jit(solution)/shard_map/while/body/eval_jaxpr/ppermute | solution.py:18
  502.6 9.9 %collective-permute-done = f32[2,2,128,128]{3,2,1,0:T(8,128)S(1)} collective-permute-done((f32[2,2,128,128]{3,2,1,0:T(8,128)}, f32[2,2,128,128]{3,2,1,0:T(8,128)S(1)}, u32[]{:S(2)}, u32[]{:S(2)}) %collective-permute-start) | collective-permute-done | bytes 262176 | tf_op jit(solution)/shard_map/while/body/eval_jaxpr/ppermute | solution.py:18
  515.5 9.9 %collective-permute-done = f32[2,2,128,128]{3,2,1,0:T(8,128)S(1)} collective-permute-done((f32[2,2,128,128]{3,2,1,0:T(8,128)}, f32[2,2,128,128]{3,2,1,0:T(8,128)S(1)}, u32[]{:S(2)}, u32[]{:S(2)}) %collective-permute-start) | collective-permute-done | bytes 262176 | tf_op jit(solution)/shard_map/while/body/eval_jaxpr/ppermute | solution.py:18
  541.3 9.9 %collective-permute-done = f32[2,2,128,128]{3,2,1,0:T(8,128)S(1)} collective-permute-done((f32[2,2,128,128]{3,2,1,0:T(8,128)}, f32[2,2,128,128]{3,2,1,0:T(8,128)S(1)}, u32[]{:S(2)}, u32[]{:S(2)}) %collective-permute-start) | collective-permute-done | bytes 262176 | tf_op jit(solution)/shard_map/while/body/eval_jaxpr/ppermute | solution.py:18
  564.6 33.8 %reduce-scatter.2.cloned.1.call-done = bf16[32,2048]{1,0:T(8,128)(2,1)} async-done(((bf16[256,2048]{1,0:T(8,128)(2,1)}), bf16[32,2048]{1,0:T(8,128)(2,1)}) %reduce-scatter.2.cloned.1.call-update) | async-done | bytes 131088 | tf_op jit(solution)/shard_map/reduce_scatter | solution.py:145
  (160 shorter events, 265.0 us)
Async XLA Ops:
  6.5 591.8 %reduce-scatter.2.cloned.1.call-start = ((), (), s32[]{:S(2)}) async-start(), calls=%async_computation.1 | async-start | bytes 1179648 | tf_op jit(solution)/shard_map/reduce_scatter | solution.py:145
  7.4 21.3 %collective-permute-start.1 = (bf16[3,256]{1,0:T(4,128)(2,1)S(1)}, bf16[3,256]{1,0:T(4,128)(2,1)S(1)}, u32[]{:S(2)}, u32[]{:S(2)}) collective-permute-start(bf16[3,256]{1,0:T(4,128)(2,1)S(1)} %slice.96), channel_id=1, source_target_pairs={{0,8},{8,16},{16,24},{24,32},{32,40},{40,48},{48,56},{56,64},{64,7... | collective-permute-start | bytes 4616 | tf_op jit(solution)/shard_map/ppermute | solution.py:18
  12.2 104.7 %collective-permute-start.2 = (bf16[3,512]{1,0:T(4,128)(2,1)}, bf16[3,512]{1,0:T(4,128)(2,1)}, u32[]{:S(2)}, u32[]{:S(2)}) collective-permute-start(bf16[3,512]{1,0:T(4,128)(2,1)} %slice.105), channel_id=1, source_target_pairs={{0,8},{8,16},{16,24},{24,32},{32,40},{40,48},{48,56},{56,64},{64,7... | collective-permute-start | bytes 9224 | tf_op jit(solution)/shard_map/ppermute | solution.py:18
  16.9 14.5 %collective-permute-start.3 = (bf16[3,256]{1,0:T(4,128)(2,1)}, bf16[3,256]{1,0:T(4,128)(2,1)}, u32[]{:S(2)}, u32[]{:S(2)}) collective-permute-start(bf16[3,256]{1,0:T(4,128)(2,1)} %slice.116), channel_id=1, source_target_pairs={{0,8},{8,16},{16,24},{24,32},{32,40},{40,48},{48,56},{56,64},{64,7... | collective-permute-start | bytes 4616 | tf_op jit(solution)/shard_map/ppermute | solution.py:18
  136.6 12.6 %collective-permute-start = (f32[2,2,128,128]{3,2,1,0:T(8,128)}, f32[2,2,128,128]{3,2,1,0:T(8,128)S(1)}, u32[]{:S(2)}, u32[]{:S(2)}) collective-permute-start(f32[2,2,128,128]{3,2,1,0:T(8,128)} %convolution_add_fusion.10), channel_id=1, source_target_pairs={{0,8},{8,16},{16,24},{24,32},{32,40},{40,48},{48,56},{56,64},{64,7... | collective-permute-start | bytes 786440 | tf_op jit(solution)/shard_map/while/body/eval_jaxpr/ppermute | solution.py:18
  150.3 11.8 %collective-permute-start = (f32[2,2,128,128]{3,2,1,0:T(8,128)}, f32[2,2,128,128]{3,2,1,0:T(8,128)S(1)}, u32[]{:S(2)}, u32[]{:S(2)}) collective-permute-start(f32[2,2,128,128]{3,2,1,0:T(8,128)} %convolution_add_fusion.10), channel_id=1, source_target_pairs={{0,8},{8,16},{16,24},{24,32},{32,40},{40,48},{48,56},{56,64},{64,7... | collective-permute-start | bytes 786440 | tf_op jit(solution)/shard_map/while/body/eval_jaxpr/ppermute | solution.py:18
  163.2 11.8 %collective-permute-start = (f32[2,2,128,128]{3,2,1,0:T(8,128)}, f32[2,2,128,128]{3,2,1,0:T(8,128)S(1)}, u32[]{:S(2)}, u32[]{:S(2)}) collective-permute-start(f32[2,2,128,128]{3,2,1,0:T(8,128)} %convolution_add_fusion.10), channel_id=1, source_target_pairs={{0,8},{8,16},{16,24},{24,32},{32,40},{40,48},{48,56},{56,64},{64,7... | collective-permute-start | bytes 786440 | tf_op jit(solution)/shard_map/while/body/eval_jaxpr/ppermute | solution.py:18
  176.1 11.8 %collective-permute-start = (f32[2,2,128,128]{3,2,1,0:T(8,128)}, f32[2,2,128,128]{3,2,1,0:T(8,128)S(1)}, u32[]{:S(2)}, u32[]{:S(2)}) collective-permute-start(f32[2,2,128,128]{3,2,1,0:T(8,128)} %convolution_add_fusion.10), channel_id=1, source_target_pairs={{0,8},{8,16},{16,24},{24,32},{32,40},{40,48},{48,56},{56,64},{64,7... | collective-permute-start | bytes 786440 | tf_op jit(solution)/shard_map/while/body/eval_jaxpr/ppermute | solution.py:18
  189.0 11.8 %collective-permute-start = (f32[2,2,128,128]{3,2,1,0:T(8,128)}, f32[2,2,128,128]{3,2,1,0:T(8,128)S(1)}, u32[]{:S(2)}, u32[]{:S(2)}) collective-permute-start(f32[2,2,128,128]{3,2,1,0:T(8,128)} %convolution_add_fusion.10), channel_id=1, source_target_pairs={{0,8},{8,16},{16,24},{24,32},{32,40},{40,48},{48,56},{56,64},{64,7... | collective-permute-start | bytes 786440 | tf_op jit(solution)/shard_map/while/body/eval_jaxpr/ppermute | solution.py:18
  201.9 11.8 %collective-permute-start = (f32[2,2,128,128]{3,2,1,0:T(8,128)}, f32[2,2,128,128]{3,2,1,0:T(8,128)S(1)}, u32[]{:S(2)}, u32[]{:S(2)}) collective-permute-start(f32[2,2,128,128]{3,2,1,0:T(8,128)} %convolution_add_fusion.10), channel_id=1, source_target_pairs={{0,8},{8,16},{16,24},{24,32},{32,40},{40,48},{48,56},{56,64},{64,7... | collective-permute-start | bytes 786440 | tf_op jit(solution)/shard_map/while/body/eval_jaxpr/ppermute | solution.py:18
  214.8 11.8 %collective-permute-start = (f32[2,2,128,128]{3,2,1,0:T(8,128)}, f32[2,2,128,128]{3,2,1,0:T(8,128)S(1)}, u32[]{:S(2)}, u32[]{:S(2)}) collective-permute-start(f32[2,2,128,128]{3,2,1,0:T(8,128)} %convolution_add_fusion.10), channel_id=1, source_target_pairs={{0,8},{8,16},{16,24},{24,32},{32,40},{40,48},{48,56},{56,64},{64,7... | collective-permute-start | bytes 786440 | tf_op jit(solution)/shard_map/while/body/eval_jaxpr/ppermute | solution.py:18
  227.6 12.6 %collective-permute-start = (f32[2,2,128,128]{3,2,1,0:T(8,128)}, f32[2,2,128,128]{3,2,1,0:T(8,128)S(1)}, u32[]{:S(2)}, u32[]{:S(2)}) collective-permute-start(f32[2,2,128,128]{3,2,1,0:T(8,128)} %convolution_add_fusion.10), channel_id=1, source_target_pairs={{0,8},{8,16},{16,24},{24,32},{32,40},{40,48},{48,56},{56,64},{64,7... | collective-permute-start | bytes 786440 | tf_op jit(solution)/shard_map/while/body/eval_jaxpr/ppermute | solution.py:18
  241.3 13.7 %collective-permute-start = (f32[2,2,128,128]{3,2,1,0:T(8,128)}, f32[2,2,128,128]{3,2,1,0:T(8,128)S(1)}, u32[]{:S(2)}, u32[]{:S(2)}) collective-permute-start(f32[2,2,128,128]{3,2,1,0:T(8,128)} %convolution_add_fusion.10), channel_id=1, source_target_pairs={{0,8},{8,16},{16,24},{24,32},{32,40},{40,48},{48,56},{56,64},{64,7... | collective-permute-start | bytes 786440 | tf_op jit(solution)/shard_map/while/body/eval_jaxpr/ppermute | solution.py:18
  256.2 14.3 %collective-permute-start = (f32[2,2,128,128]{3,2,1,0:T(8,128)}, f32[2,2,128,128]{3,2,1,0:T(8,128)S(1)}, u32[]{:S(2)}, u32[]{:S(2)}) collective-permute-start(f32[2,2,128,128]{3,2,1,0:T(8,128)} %convolution_add_fusion.10), channel_id=1, source_target_pairs={{0,8},{8,16},{16,24},{24,32},{32,40},{40,48},{48,56},{56,64},{64,7... | collective-permute-start | bytes 786440 | tf_op jit(solution)/shard_map/while/body/eval_jaxpr/ppermute | solution.py:18
  271.6 13.4 %collective-permute-start = (f32[2,2,128,128]{3,2,1,0:T(8,128)}, f32[2,2,128,128]{3,2,1,0:T(8,128)S(1)}, u32[]{:S(2)}, u32[]{:S(2)}) collective-permute-start(f32[2,2,128,128]{3,2,1,0:T(8,128)} %convolution_add_fusion.10), channel_id=1, source_target_pairs={{0,8},{8,16},{16,24},{24,32},{32,40},{40,48},{48,56},{56,64},{64,7... | collective-permute-start | bytes 786440 | tf_op jit(solution)/shard_map/while/body/eval_jaxpr/ppermute | solution.py:18
  286.1 12.6 %collective-permute-start = (f32[2,2,128,128]{3,2,1,0:T(8,128)}, f32[2,2,128,128]{3,2,1,0:T(8,128)S(1)}, u32[]{:S(2)}, u32[]{:S(2)}) collective-permute-start(f32[2,2,128,128]{3,2,1,0:T(8,128)} %convolution_add_fusion.10), channel_id=1, source_target_pairs={{0,8},{8,16},{16,24},{24,32},{32,40},{40,48},{48,56},{56,64},{64,7... | collective-permute-start | bytes 786440 | tf_op jit(solution)/shard_map/while/body/eval_jaxpr/ppermute | solution.py:18
  299.8 11.8 %collective-permute-start = (f32[2,2,128,128]{3,2,1,0:T(8,128)}, f32[2,2,128,128]{3,2,1,0:T(8,128)S(1)}, u32[]{:S(2)}, u32[]{:S(2)}) collective-permute-start(f32[2,2,128,128]{3,2,1,0:T(8,128)} %convolution_add_fusion.10), channel_id=1, source_target_pairs={{0,8},{8,16},{16,24},{24,32},{32,40},{40,48},{48,56},{56,64},{64,7... | collective-permute-start | bytes 786440 | tf_op jit(solution)/shard_map/while/body/eval_jaxpr/ppermute | solution.py:18
  325.5 11.8 %collective-permute-start = (f32[2,2,128,128]{3,2,1,0:T(8,128)}, f32[2,2,128,128]{3,2,1,0:T(8,128)S(1)}, u32[]{:S(2)}, u32[]{:S(2)}) collective-permute-start(f32[2,2,128,128]{3,2,1,0:T(8,128)} %convolution_add_fusion.10), channel_id=1, source_target_pairs={{0,8},{8,16},{16,24},{24,32},{32,40},{40,48},{48,56},{56,64},{64,7... | collective-permute-start | bytes 786440 | tf_op jit(solution)/shard_map/while/body/eval_jaxpr/ppermute | solution.py:18
  377.1 12.6 %collective-permute-start = (f32[2,2,128,128]{3,2,1,0:T(8,128)}, f32[2,2,128,128]{3,2,1,0:T(8,128)S(1)}, u32[]{:S(2)}, u32[]{:S(2)}) collective-permute-start(f32[2,2,128,128]{3,2,1,0:T(8,128)} %convolution_add_fusion.10), channel_id=1, source_target_pairs={{0,8},{8,16},{16,24},{24,32},{32,40},{40,48},{48,56},{56,64},{64,7... | collective-permute-start | bytes 786440 | tf_op jit(solution)/shard_map/while/body/eval_jaxpr/ppermute | solution.py:18
  390.8 13.8 %collective-permute-start = (f32[2,2,128,128]{3,2,1,0:T(8,128)}, f32[2,2,128,128]{3,2,1,0:T(8,128)S(1)}, u32[]{:S(2)}, u32[]{:S(2)}) collective-permute-start(f32[2,2,128,128]{3,2,1,0:T(8,128)} %convolution_add_fusion.10), channel_id=1, source_target_pairs={{0,8},{8,16},{16,24},{24,32},{32,40},{40,48},{48,56},{56,64},{64,7... | collective-permute-start | bytes 786440 | tf_op jit(solution)/shard_map/while/body/eval_jaxpr/ppermute | solution.py:18
  405.6 14.3 %collective-permute-start = (f32[2,2,128,128]{3,2,1,0:T(8,128)}, f32[2,2,128,128]{3,2,1,0:T(8,128)S(1)}, u32[]{:S(2)}, u32[]{:S(2)}) collective-permute-start(f32[2,2,128,128]{3,2,1,0:T(8,128)} %convolution_add_fusion.10), channel_id=1, source_target_pairs={{0,8},{8,16},{16,24},{24,32},{32,40},{40,48},{48,56},{56,64},{64,7... | collective-permute-start | bytes 786440 | tf_op jit(solution)/shard_map/while/body/eval_jaxpr/ppermute | solution.py:18
  421.0 13.4 %collective-permute-start = (f32[2,2,128,128]{3,2,1,0:T(8,128)}, f32[2,2,128,128]{3,2,1,0:T(8,128)S(1)}, u32[]{:S(2)}, u32[]{:S(2)}) collective-permute-start(f32[2,2,128,128]{3,2,1,0:T(8,128)} %convolution_add_fusion.10), channel_id=1, source_target_pairs={{0,8},{8,16},{16,24},{24,32},{32,40},{40,48},{48,56},{56,64},{64,7... | collective-permute-start | bytes 786440 | tf_op jit(solution)/shard_map/while/body/eval_jaxpr/ppermute | solution.py:18
  435.5 12.6 %collective-permute-start = (f32[2,2,128,128]{3,2,1,0:T(8,128)}, f32[2,2,128,128]{3,2,1,0:T(8,128)S(1)}, u32[]{:S(2)}, u32[]{:S(2)}) collective-permute-start(f32[2,2,128,128]{3,2,1,0:T(8,128)} %convolution_add_fusion.10), channel_id=1, source_target_pairs={{0,8},{8,16},{16,24},{24,32},{32,40},{40,48},{48,56},{56,64},{64,7... | collective-permute-start | bytes 786440 | tf_op jit(solution)/shard_map/while/body/eval_jaxpr/ppermute | solution.py:18
  500.7 11.8 %collective-permute-start = (f32[2,2,128,128]{3,2,1,0:T(8,128)}, f32[2,2,128,128]{3,2,1,0:T(8,128)S(1)}, u32[]{:S(2)}, u32[]{:S(2)}) collective-permute-start(f32[2,2,128,128]{3,2,1,0:T(8,128)} %convolution_add_fusion.10), channel_id=1, source_target_pairs={{0,8},{8,16},{16,24},{24,32},{32,40},{40,48},{48,56},{56,64},{64,7... | collective-permute-start | bytes 786440 | tf_op jit(solution)/shard_map/while/body/eval_jaxpr/ppermute | solution.py:18
  (16 other events, 778.3 us)
Sparse Core Ops, SparseCore 0:
  564.7 33.5 reduce-scatter.1
where the time goes:
time: 608 us; the launch traced here: 605 us
  waiting for transfers between devices  355 us (58%)
  other arithmetic  93.4 us (15%)
  starting transfers between devices  69.9 us (11%)
  matrix products  56.1 us (9%)
  local copies, waits for them, and re-layouts  16 us (3%)
  between operations  13.7 us (2%)
    ppermute x34, waiting for transfers between devices, shifted(): return lax.ppermute(array, axis, pairs)  321 us
    another operation x5, other arithmetic, shards(): lax.linalg.triangular_solve(system, right_side, left_side=True, lower=Tru...  82.8 us
    ppermute x34, starting transfers between devices, shifted(): return lax.ppermute(array, axis, pairs)  69.9 us
    dot_general x37, matrix products, apply_map(): return jnp.einsum('hrke,hrev->hrkv', matrix, state_now, precision=highest)  40.1 us
    reduce_scatter x1, waiting for transfers between devices, shards(): lax.psum_scatter(jnp.dot(hidden, out_weight, preferred_element_type=jnp.f...  33.8 us
  transfers between devices with their start and end apart: 35, of which 32 were waited for; matrix products, arithmetic and copies ran while one was open for 16% of the time, Pallas kernels for 0%

commit v1 on v0

--- a/solution.py
+++ b/solution.py
@@ -119,10 +119,22 @@
         sweep_spans, (identity, zero_state), (transit_seq, inject_seq)
     )
 
-    def relay_step(hop_index, state_now):
-        return shifted(apply_map(total_map, state_now) + local_end, "seq", 1)
-
-    incoming = lax.fori_loop(0, lax.axis_size("seq") - 1, relay_step, zero_state)
+    seq_size = lax.axis_size("seq")
+    seq_index = lax.axis_index("seq")
+    prefix_map, prefix_end = total_map, local_end
+    distance = 1
+    while distance < seq_size:
+        if 2 * distance < seq_size:
+            earlier_map, earlier_end = shifted((prefix_map, prefix_end), "seq", distance)
+            prefix_end = apply_map(prefix_map, earlier_end) + prefix_end
+            prefix_map = jnp.where(
+                seq_index >= distance, apply_map(prefix_map, earlier_map), prefix_map
+            )
+        else:
+            earlier_end = shifted(prefix_end, "seq", distance)
+            prefix_end = apply_map(prefix_map, earlier_end) + prefix_end
+        distance *= 2
+    incoming = shifted(prefix_end, "seq", 1)
 
     def replay(state_now, span_in):
         transit_now, inject_now, coupling_now, local_now = span_in

time: 608 us -> 272 us (0.45)
  waiting for transfers between devices: 355 us -> 89.4 us
  starting transfers between devices: 69.9 us -> 33.3 us
  matrix products: 56.1 us -> 30.2 us
  other arithmetic: 93.4 us -> 87.2 us
    ppermute x34 -> x13, waiting for transfers between devices: 321 us -> 55.6 us  [shifted(): return lax.ppermute(array, axis, pairs)]
    ppermute x34 -> x13, starting transfers between devices: 69.9 us -> 33.3 us  [shifted(): return lax.ppermute(array, axis, pairs)]
    dot_general x37 -> x15, matrix products: 40.1 us -> 15.3 us  [apply_map(): return jnp.einsum('hrke,hrev->hrkv', matrix, state_now, precision=highest)]
  transfers between devices with their start and end apart: 35 -> 14, of which waited for: 32 -> 11; matrix products, arithmetic and copies ran while one was open for 16% -> 45% of each run, Pallas kernels for 0% -> 0%
where the time goes in v1:
time: 272 us; the launch traced here: 270 us
  waiting for transfers between devices  89.4 us (33%)
  other arithmetic  87.2 us (32%)
  starting transfers between devices  33.3 us (12%)
  matrix products  30.2 us (11%)
  local copies, waits for them, and re-layouts  15.7 us (6%)
  between operations  13.9 us (5%)
    another operation x5, other arithmetic, shards(): lax.linalg.triangular_solve(system, right_side, left_side=True, lower=Tru...  79.7 us
    ppermute x13, waiting for transfers between devices, shifted(): return lax.ppermute(array, axis, pairs)  55.6 us
    reduce_scatter x1, waiting for transfers between devices, shards(): lax.psum_scatter(jnp.dot(hidden, out_weight, preferred_element_type=jnp.f...  33.8 us
    ppermute x13, starting transfers between devices, shifted(): return lax.ppermute(array, axis, pairs)  33.3 us
    dot_general x15, matrix products, apply_map(): return jnp.einsum('hrke,hrev->hrkv', matrix, state_now, precision=highest)  15.3 us
  transfers between devices with their start and end apart: 14, of which 11 were waited for; matrix products, arithmetic and copies ran while one was open for 45% of the time, Pallas kernels for 0%

profile of v1, /device:TPU:128, one launch (start us, length us, event | category | flops | bytes accessed | tf_op | source)
XLA Modules:
  0.0 269.8 jit_solution(7779524585369142471)
XLA Ops:
  7.4 3.5 %collective-permute-start.1 = (bf16[3,512]{1,0:T(4,128)(2,1)S(1)}, bf16[3,512]{1,0:T(4,128)(2,1)S(1)}, u32[]{:S(2)}, u32[]{:S(2)}) collective-permute-start(bf16[3,512]{1,0:T(4,128)(2,1)S(1)} %slice.105), channel_id=1, source_target_pairs={{0,8},{8,16},{16,24},{24,32},{32,40},{40,48},{48,56},{56,64},{64,7... | collective-permute-start | bytes 9224 | tf_op jit(solution)/shard_map/ppermute | solution.py:18
  11.6 3.5 %collective-permute-start = (bf16[3,256]{1,0:T(4,128)(2,1)S(1)}, bf16[3,256]{1,0:T(4,128)(2,1)S(1)}, u32[]{:S(2)}, u32[]{:S(2)}) collective-permute-start(bf16[3,256]{1,0:T(4,128)(2,1)S(1)} %slice.96), channel_id=1, source_target_pairs={{0,8},{8,16},{16,24},{24,32},{32,40},{40,48},{48,56},{56,64},{64,7... | collective-permute-start | bytes 4616 | tf_op jit(solution)/shard_map/ppermute | solution.py:18
  15.7 3.2 %collective-permute-start.12 = (bf16[3,256]{1,0:T(4,128)(2,1)S(1)}, bf16[3,256]{1,0:T(4,128)(2,1)S(1)}, u32[]{:S(2)}, u32[]{:S(2)}) collective-permute-start(bf16[3,256]{1,0:T(4,128)(2,1)S(1)} %slice.116), channel_id=1, source_target_pairs={{0,8},{8,16},{16,24},{24,32},{32,40},{40,48},{48,56},{56,64},{64,7... | collective-permute-start | bytes 4616 | tf_op jit(solution)/shard_map/ppermute | solution.py:18
  27.4 79.3 %custom-call.3 = f32[2,2,2,1,128,128]{4,5,3,2,1,0:T(8,128)} custom-call(f32[2,2,2,1,128,128]{5,4,3,2,1,0:T(8,128)S(1)} %select_add_fusion), custom_call_target="InvertDiagBlocksLowerTriangular" | custom-call | tf_op jit(solution)/shard_map/triangular_solve | solution.py:89
  112.7 8.2 %while.28 = (s32[]{:T(128)}, f32[2,2,128,128]{3,2,1,0:T(8,128)}, f32[2,2,128,128]{3,2,1,0:T(8,128)}, f32[2,2,2,128,128]{4,3,2,1,0:T(8,128)S(1)}, f32[2,2,2,128,128]{4,3,2,1,0:T(8,128)S(1)}) while((s32[]{:T(128)}, f32[2,2,128,128]{3,2,1,0:T(8,128)}, f32[2,2,128,128]{3,2,1,0:T(8,128)}, ...), condition=%wide.region_3.4_spmd.clone.clone, body=%wide.region_2.3_spmd.clone.sunk.clone | while | flops 201457664 | bytes 2885202 | solution.py:118
  120.9 2.6 collective-permute-start.6
  123.5 3.5 %collective-permute-start.2 = (f32[2,2,128,128]{3,2,1,0:T(8,128)}, f32[2,2,128,128]{3,2,1,0:T(8,128)S(1)}, u32[]{:S(2)}, u32[]{:S(2)}) collective-permute-start(f32[2,2,128,128]{3,2,1,0:T(8,128)} %get-tuple-element.70), channel_id=1, source_target_pairs={{0,8},{8,16},{16,24},{24,32},{32,40},{40,48},{48,56},{56,64},{64,7... | collective-permute-start | bytes 786440 | tf_op jit(solution)/shard_map/ppermute | solution.py:18
  127.0 8.5 %collective-permute-done.6 = f32[2,2,128,128]{3,2,1,0:T(8,128)S(1)} collective-permute-done((f32[2,2,128,128]{3,2,1,0:T(8,128)}, f32[2,2,128,128]{3,2,1,0:T(8,128)S(1)}, u32[]{:S(2)}, u32[]{:S(2)}) %collective-permute-start.6) | collective-permute-done | bytes 262176 | tf_op jit(solution)/shard_map/ppermute | solution.py:18
  136.9 1.9 collective-permute-start.7
  140.6 2.1 convolution_select_fusion.3
  142.7 3.9 %collective-permute-start.3 = (f32[2,2,128,128]{3,2,1,0:T(8,128)}, f32[2,2,128,128]{3,2,1,0:T(8,128)}, u32[]{:S(2)}, u32[]{:S(2)}) collective-permute-start(f32[2,2,128,128]{3,2,1,0:T(8,128)} %convolution_select_fusion.3), channel_id=1, source_target_pairs={{0,16},{8,24},{16,32},{24,40},{32,48},{40,56},{48,64},{56,72},{64,... | collective-permute-start | bytes 786440 | tf_op jit(solution)/shard_map/ppermute | solution.py:18
  146.6 3.2 %collective-permute-done.7 = f32[2,2,128,128]{3,2,1,0:T(8,128)S(1)} collective-permute-done((f32[2,2,128,128]{3,2,1,0:T(8,128)S(1)}, f32[2,2,128,128]{3,2,1,0:T(8,128)S(1)}, u32[]{:S(2)}, u32[]{:S(2)}) %collective-permute-start.7) | collective-permute-done | bytes 262176 | tf_op jit(solution)/shard_map/ppermute | solution.py:18
  149.9 2.0 convolution_add_fusion.6
  151.9 2.2 collective-permute-start.8
  159.1 2.1 collective-permute-start.4
  161.1 6.3 %collective-permute-done.8 = f32[2,2,128,128]{3,2,1,0:T(8,128)} collective-permute-done((f32[2,2,128,128]{3,2,1,0:T(8,128)}, f32[2,2,128,128]{3,2,1,0:T(8,128)}, u32[]{:S(2)}, u32[]{:S(2)}) %collective-permute-start.8) | collective-permute-done | bytes 262176 | tf_op jit(solution)/shard_map/ppermute | solution.py:18
  168.8 1.9 collective-permute-start.9
  175.3 18.7 %collective-permute-done.9 = f32[2,2,128,128]{3,2,1,0:T(8,128)S(1)} collective-permute-done((f32[2,2,128,128]{3,2,1,0:T(8,128)S(1)}, f32[2,2,128,128]{3,2,1,0:T(8,128)S(1)}, u32[]{:S(2)}, u32[]{:S(2)}) %collective-permute-start.9) | collective-permute-done | bytes 262176 | tf_op jit(solution)/shard_map/ppermute | solution.py:18
  198.7 7.8 %collective-permute-done.10 = f32[2,2,128,128]{3,2,1,0:T(8,128)S(1)} collective-permute-done((f32[2,2,128,128]{3,2,1,0:T(8,128)S(1)}, f32[2,2,128,128]{3,2,1,0:T(8,128)S(1)}, u32[]{:S(2)}, u32[]{:S(2)}) %collective-permute-start.10) | collective-permute-done | bytes 262176 | tf_op jit(solution)/shard_map/ppermute | solution.py:18
  210.5 8.0 %collective-permute-done.11 = f32[2,2,128,128]{3,2,1,0:T(8,128)S(1)} collective-permute-done((f32[2,2,128,128]{3,2,1,0:T(8,128)S(1)}, f32[2,2,128,128]{3,2,1,0:T(8,128)S(1)}, u32[]{:S(2)}, u32[]{:S(2)}) %collective-permute-start.11) | collective-permute-done | bytes 262176 | tf_op jit(solution)/shard_map/ppermute | solution.py:18
  218.5 5.2 %while.27 = (s32[]{:T(128)}, f32[2,2,128,128]{3,2,1,0:T(8,128)S(1)}, f32[2,2,2,128,128]{4,3,2,1,0:T(8,128)}, f32[2,2,2,128,128]{4,3,2,1,0:T(8,128)S(1)}, f32[2,2...) while((s32[]{:T(128)}, ...), condition=%wide.region_5.6_spmd.clone, body=%wide.region_4.5_spmd.sunk.clone | while | flops 201457664 | bytes 2623573 | solution.py:146
  218.5 2.2 fusion.128
  221.1 2.1 fusion.128
  229.2 33.8 %reduce-scatter.2.cloned.1.call-done = bf16[32,2048]{1,0:T(8,128)(2,1)} async-done(((bf16[256,2048]{1,0:T(8,128)(2,1)}), bf16[32,2048]{1,0:T(8,128)(2,1)}) %reduce-scatter.2.cloned.1.call-update) | async-done | bytes 131088 | tf_op jit(solution)/shard_map/reduce_scatter | solution.py:157
  (104 shorter events, 53.6 us)
Async XLA Ops:
  6.5 220.8 %copy-start = (bf16[512,2048]{1,0:T(8,128)(2,1)S(1)}, bf16[512,2048]{1,0:T(8,128)(2,1)}, u32[]{:S(2)}) copy-start(bf16[512,2048]{1,0:T(8,128)(2,1)} %param.25) | copy-start | bytes 6291460
  6.5 256.4 %reduce-scatter.2.cloned.1.call-start = ((), (), s32[]{:S(2)}) async-start(), calls=%async_computation.1 | async-start | bytes 1179648 | tf_op jit(solution)/shard_map/reduce_scatter | solution.py:157
  7.4 99.3 %collective-permute-start.1 = (bf16[3,512]{1,0:T(4,128)(2,1)S(1)}, bf16[3,512]{1,0:T(4,128)(2,1)S(1)}, u32[]{:S(2)}, u32[]{:S(2)}) collective-permute-start(bf16[3,512]{1,0:T(4,128)(2,1)S(1)} %slice.105), channel_id=1, source_target_pairs={{0,8},{8,16},{16,24},{24,32},{32,40},{40,48},{48,56},{56,64},{64,7... | collective-permute-start | bytes 9224 | tf_op jit(solution)/shard_map/ppermute | solution.py:18
  11.6 12.7 %collective-permute-start = (bf16[3,256]{1,0:T(4,128)(2,1)S(1)}, bf16[3,256]{1,0:T(4,128)(2,1)S(1)}, u32[]{:S(2)}, u32[]{:S(2)}) collective-permute-start(bf16[3,256]{1,0:T(4,128)(2,1)S(1)} %slice.96), channel_id=1, source_target_pairs={{0,8},{8,16},{16,24},{24,32},{32,40},{40,48},{48,56},{56,64},{64,7... | collective-permute-start | bytes 4616 | tf_op jit(solution)/shard_map/ppermute | solution.py:18
  15.7 123.1 %collective-permute-start.12 = (bf16[3,256]{1,0:T(4,128)(2,1)S(1)}, bf16[3,256]{1,0:T(4,128)(2,1)S(1)}, u32[]{:S(2)}, u32[]{:S(2)}) collective-permute-start(bf16[3,256]{1,0:T(4,128)(2,1)S(1)} %slice.116), channel_id=1, source_target_pairs={{0,8},{8,16},{16,24},{24,32},{32,40},{40,48},{48,56},{56,64},{64,7... | collective-permute-start | bytes 4616 | tf_op jit(solution)/shard_map/ppermute | solution.py:18
  25.4 81.2 %copy-start.7 = (bf16[256,512]{1,0:T(8,128)(2,1)S(1)}, bf16[256,512]{1,0:T(8,128)(2,1)}, u32[]{:S(2)}) copy-start(bf16[256,512]{1,0:T(8,128)(2,1)} %param.17) | copy-start | bytes 786436
  26.4 84.3 %copy-start.1 = (f32[2,2,128,128]{3,2,1,0:T(8,128)}, f32[2,2,128,128]{3,2,1,0:T(8,128)S(1)}, u32[]{:S(2)}) copy-start(f32[2,2,128,128]{3,2,1,0:T(8,128)S(1)} %fusion.50) | copy-start | bytes 786436
  107.4 1.0 copy-start.6
  109.5 2.4 copy-start.3
  112.7 10.9 %copy-start.8 = (bf16[4,256]{1,0:T(4,128)(2,1)S(1)}, bf16[4,256]{1,0:T(4,128)(2,1)}, u32[]{:S(2)}) copy-start(bf16[4,256]{1,0:T(4,128)(2,1)} %param.21) | copy-start | bytes 6148
  120.9 14.6 %collective-permute-start.6 = (f32[2,2,128,128]{3,2,1,0:T(8,128)}, f32[2,2,128,128]{3,2,1,0:T(8,128)S(1)}, u32[]{:S(2)}, u32[]{:S(2)}) collective-permute-start(f32[2,2,128,128]{3,2,1,0:T(8,128)} %get-tuple-element.71), channel_id=1, source_target_pairs={{0,8},{8,16},{16,24},{24,32},{32,40},{40,48},{48,56},{56,64},{64,7... | collective-permute-start | bytes 786440 | tf_op jit(solution)/shard_map/ppermute | solution.py:18
  123.5 17.0 %collective-permute-start.2 = (f32[2,2,128,128]{3,2,1,0:T(8,128)}, f32[2,2,128,128]{3,2,1,0:T(8,128)S(1)}, u32[]{:S(2)}, u32[]{:S(2)}) collective-permute-start(f32[2,2,128,128]{3,2,1,0:T(8,128)} %get-tuple-element.70), channel_id=1, source_target_pairs={{0,8},{8,16},{16,24},{24,32},{32,40},{40,48},{48,56},{56,64},{64,7... | collective-permute-start | bytes 786440 | tf_op jit(solution)/shard_map/ppermute | solution.py:18
  136.9 12.9 %collective-permute-start.7 = (f32[2,2,128,128]{3,2,1,0:T(8,128)S(1)}, f32[2,2,128,128]{3,2,1,0:T(8,128)S(1)}, u32[]{:S(2)}, u32[]{:S(2)}) collective-permute-start(f32[2,2,128,128]{3,2,1,0:T(8,128)S(1)} %convolution_add_fusion.7), channel_id=1, source_target_pairs={{0,16},{8,24},{16,32},{24,40},{32,48},{40,56},{48,64},{56,72},{64,... | collective-permute-start | bytes 786440 | tf_op jit(solution)/shard_map/ppermute | solution.py:18
  142.7 14.8 %collective-permute-start.3 = (f32[2,2,128,128]{3,2,1,0:T(8,128)}, f32[2,2,128,128]{3,2,1,0:T(8,128)}, u32[]{:S(2)}, u32[]{:S(2)}) collective-permute-start(f32[2,2,128,128]{3,2,1,0:T(8,128)} %convolution_select_fusion.3), channel_id=1, source_target_pairs={{0,16},{8,24},{16,32},{24,40},{32,48},{40,56},{48,64},{56,72},{64,... | collective-permute-start | bytes 786440 | tf_op jit(solution)/shard_map/ppermute | solution.py:18
  151.9 18.9 %copy-start.2 = (f32[2,2,128,128]{3,2,1,0:T(8,128)S(1)}, f32[2,2,128,128]{3,2,1,0:T(8,128)}, u32[]{:S(2)}) copy-start(f32[2,2,128,128]{3,2,1,0:T(8,128)} %copy-done.1) | copy-start | bytes 786436
  151.9 15.5 %collective-permute-start.8 = (f32[2,2,128,128]{3,2,1,0:T(8,128)}, f32[2,2,128,128]{3,2,1,0:T(8,128)}, u32[]{:S(2)}, u32[]{:S(2)}) collective-permute-start(f32[2,2,128,128]{3,2,1,0:T(8,128)} %convolution_add_fusion.6), channel_id=1, source_target_pairs={{0,32},{8,40},{16,48},{24,56},{32,64},{40,72},{48,80},{56,88},{64,... | collective-permute-start | bytes 786440 | tf_op jit(solution)/shard_map/ppermute | solution.py:18
  156.8 15.6 %copy-start.5 = (f32[2,128,2,128]{3,2,1,0:T(2,128)S(1)}, f32[2,128,2,128]{3,2,1,0:T(2,128)}, u32[]{:S(2)}) copy-start(f32[2,128,2,128]{3,2,1,0:T(2,128)} %reshape.131) | copy-start | bytes 786436
  159.1 36.6 %copy-start.4 = (f32[2,2,2,128,256]{4,3,2,1,0:T(8,128)S(1)}, f32[2,2,2,128,256]{4,3,2,1,0:T(8,128)}, u32[]{:S(2)}) copy-start(f32[2,2,2,128,256]{4,3,2,1,0:T(8,128)} %copy-done.3) | copy-start | bytes 3145732
  159.1 13.9 %collective-permute-start.4 = (f32[2,2,128,128]{3,2,1,0:T(8,128)S(1)}, f32[2,2,128,128]{3,2,1,0:T(8,128)S(1)}, u32[]{:S(2)}, u32[]{:S(2)}) collective-permute-start(f32[2,2,128,128]{3,2,1,0:T(8,128)S(1)} %convolution_select_fusion.2), channel_id=1, source_target_pairs={{0,32},{8,40},{16,48},{24,56},{32,64},{40,72},{48,80},{56,88},{64,... | collective-permute-start | bytes 786440 | tf_op jit(solution)/shard_map/ppermute | solution.py:18
  168.8 25.1 %collective-permute-start.9 = (f32[2,2,128,128]{3,2,1,0:T(8,128)S(1)}, f32[2,2,128,128]{3,2,1,0:T(8,128)S(1)}, u32[]{:S(2)}, u32[]{:S(2)}) collective-permute-start(f32[2,2,128,128]{3,2,1,0:T(8,128)S(1)} %convolution_add_fusion.5), channel_id=1, source_target_pairs={{0,64},{8,72},{16,80},{24,88},{32,96},{40,104},{48,112},{56,120},{... | collective-permute-start | bytes 786440 | tf_op jit(solution)/shard_map/ppermute | solution.py:18
  173.3 24.9 %collective-permute-start.5 = (f32[2,2,128,128]{3,2,1,0:T(8,128)S(1)}, f32[2,2,128,128]{3,2,1,0:T(8,128)S(1)}, u32[]{:S(2)}, u32[]{:S(2)}) collective-permute-start(f32[2,2,128,128]{3,2,1,0:T(8,128)S(1)} %convolution_select_fusion.1), channel_id=1, source_target_pairs={{0,64},{8,72},{16,80},{24,88},{32,96},{40,104},{48,112},{56,120},{... | collective-permute-start | bytes 786440 | tf_op jit(solution)/shard_map/ppermute | solution.py:18
  194.3 12.2 %collective-permute-start.10 = (f32[2,2,128,128]{3,2,1,0:T(8,128)S(1)}, f32[2,2,128,128]{3,2,1,0:T(8,128)S(1)}, u32[]{:S(2)}, u32[]{:S(2)}) collective-permute-start(f32[2,2,128,128]{3,2,1,0:T(8,128)S(1)} %convolution_add_fusion.4), channel_id=1, source_target_pairs={{0,128},{8,136},{16,144},{24,152},{32,160},{40,168},{48,176},{56,1... | collective-permute-start | bytes 786440 | tf_op jit(solution)/shard_map/ppermute | solution.py:18
  206.9 11.6 %collective-permute-start.11 = (f32[2,2,128,128]{3,2,1,0:T(8,128)S(1)}, f32[2,2,128,128]{3,2,1,0:T(8,128)S(1)}, u32[]{:S(2)}, u32[]{:S(2)}) collective-permute-start(f32[2,2,128,128]{3,2,1,0:T(8,128)S(1)} %convolution_add_fusion.3), channel_id=1, source_target_pairs={{0,8},{8,16},{16,24},{24,32},{32,40},{40,48},{48,56},{56,64},{64,7... | collective-permute-start | bytes 786440 | tf_op jit(solution)/shard_map/ppermute | solution.py:18
  223.7 3.7 %copy-start.9 = (bf16[256,512]{1,0:T(8,128)(2,1)S(1)}, bf16[256,512]{1,0:T(8,128)(2,1)}, u32[]{:S(2)}) copy-start(bf16[256,512]{1,0:T(8,128)(2,1)} %param.18) | copy-start | bytes 786436
Sparse Core Ops, SparseCore 0:
  229.3 33.5 reduce-scatter.1

commit v2 on v1

--- a/solution.py
+++ b/solution.py
@@ -26,6 +26,27 @@
     for offset in range(conv_taps.shape[0]):
         summed = summed + conv_taps[offset] * padded[offset : offset + length]
     return jax.nn.silu(summed)
+
+
+def unit_lower_inverse(system):
+    size = system.shape[-1]
+    rows = jnp.arange(size)[:, None]
+    cols = jnp.arange(size)[None, :]
+    inverse = jnp.broadcast_to(jnp.eye(size, dtype=system.dtype), system.shape)
+    width = 1
+    while width < size:
+        same_block = (rows // (2 * width)) == (cols // (2 * width))
+        lower_half = (rows // width) > (cols // width)
+        coupling = jnp.where(same_block & lower_half, system, 0.0)
+        correction = jnp.einsum(
+            "...ij,...jk->...ik",
+            jnp.einsum("...ij,...jk->...ik", inverse, coupling, precision=highest),
+            inverse,
+            precision=highest,
+        )
+        inverse = jnp.where(same_block & lower_half, -correction, inverse)
+        width *= 2
+    return inverse
 
 
 def apply_map(matrix, state_now):
@@ -86,8 +107,8 @@
         ],
         axis=-1,
     )
-    solved = lax.linalg.triangular_solve(
-        system, right_side, left_side=True, lower=True, unit_diagonal=True
+    solved = jnp.einsum(
+        "...ij,...jk->...ik", unit_lower_inverse(system), right_side, precision=highest
     )
     value_part = solved[..., :DV]
     key_part = solved[..., DV:]

time: 272 us -> 210 us (0.77)
  other arithmetic: 87.2 us -> 9.64 us
  matrix products: 30.2 us -> 42.9 us
    another operation x5 -> x0, other arithmetic: 79.7 us -> none  [shards(): lax.linalg.triangular_solve(system, right_side, left_side=True, lower=Tru...]
    dot_general x0 -> x15, matrix products: none -> 12.8 us  [the longest x7 6.22 us: unit_lower_inverse(): jnp.einsum('...ij,...jk->...ik', inverse, coupling, precision=highest)]
  transfers between devices with their start and end apart: 14 -> 14, of which waited for: 11 -> 11; matrix products, arithmetic and copies ran while one was open for 45% -> 27% of each run, Pallas kernels for 0% -> 0%
where the time goes in v2:
time: 210 us; the launch traced here: 207 us
  waiting for transfers between devices  89.5 us (43%)
  matrix products  42.9 us (20%)
  starting transfers between devices  33.4 us (16%)
  local copies, waits for them, and re-layouts  17.7 us (8%)
  between operations  14 us (7%)
  other arithmetic  9.64 us (5%)
    ppermute x13, waiting for transfers between devices, shifted(): return lax.ppermute(array, axis, pairs)  55.7 us
    reduce_scatter x1, waiting for transfers between devices, shards(): lax.psum_scatter(jnp.dot(hidden, out_weight, preferred_element_type=jnp.f...  33.8 us
    ppermute x13, starting transfers between devices, shifted(): return lax.ppermute(array, axis, pairs)  33.4 us
    dot_general x15, matrix products, apply_map(): return jnp.einsum('hrke,hrev->hrkv', matrix, state_now, precision=highest)  15.3 us
    dot_general x7, matrix products, unit_lower_inverse(): jnp.einsum('...ij,...jk->...ik', inverse, coupling, precision=highest)  6.22 us
    dot_general x7, matrix products, unit_lower_inverse(): jnp.einsum('...ij,...jk->...ik', jnp.einsum('...ij,...jk->...ik', inverse...  5.5 us
    dot_general x2, matrix products, replay(): jnp.einsum('hrck,hrkv->hrcv', coupling_now, state_now, precision=highest)  4.27 us
  transfers between devices with their start and end apart: 14, of which 11 were waited for; matrix products, arithmetic and copies ran while one was open for 27% of the time, Pallas kernels for 0%

profile of v2, /device:TPU:128, one launch (start us, length us, event | category | flops | bytes accessed | tf_op | source)
XLA Modules:
  0.0 207.2 jit_solution(15228104535174269580)
XLA Ops:
  7.4 3.5 %collective-permute-start = (bf16[3,256]{1,0:T(4,128)(2,1)S(1)}, bf16[3,256]{1,0:T(4,128)(2,1)S(1)}, u32[]{:S(2)}, u32[]{:S(2)}) collective-permute-start(bf16[3,256]{1,0:T(4,128)(2,1)S(1)} %slice.92), channel_id=1, source_target_pairs={{0,8},{8,16},{16,24},{24,32},{32,40},{40,48},{48,56},{56,64},{64,7... | collective-permute-start | bytes 4616 | tf_op jit(solution)/shard_map/ppermute | solution.py:18
  11.6 3.5 %collective-permute-start.1 = (bf16[3,512]{1,0:T(4,128)(2,1)S(1)}, bf16[3,512]{1,0:T(4,128)(2,1)S(1)}, u32[]{:S(2)}, u32[]{:S(2)}) collective-permute-start(bf16[3,512]{1,0:T(4,128)(2,1)S(1)} %slice.101), channel_id=1, source_target_pairs={{0,8},{8,16},{16,24},{24,32},{32,40},{40,48},{48,56},{56,64},{64,7... | collective-permute-start | bytes 9224 | tf_op jit(solution)/shard_map/ppermute | solution.py:18
  15.7 3.2 %collective-permute-start.12 = (bf16[3,256]{1,0:T(4,128)(2,1)S(1)}, bf16[3,256]{1,0:T(4,128)(2,1)S(1)}, u32[]{:S(2)}, u32[]{:S(2)}) collective-permute-start(bf16[3,256]{1,0:T(4,128)(2,1)S(1)} %slice.112), channel_id=1, source_target_pairs={{0,8},{8,16},{16,24},{24,32},{32,40},{40,48},{48,56},{56,64},{64,7... | collective-permute-start | bytes 4616 | tf_op jit(solution)/shard_map/ppermute | solution.py:18
  40.3 2.2 %reshape.586 = f32[2,128,2,2,128]{4,3,2,1,0:T(2,128)} reshape(f32[256,512]{1,0:T(8,128)} %divide_multiply_fusion) | data formatting | bytes 1048576 | tf_op jit(solution)/shard_map/reshape | solution.py:90
  48.2 8.2 %while.28 = (s32[]{:T(128)}, f32[2,2,128,128]{3,2,1,0:T(8,128)}, f32[2,2,128,128]{3,2,1,0:T(8,128)}, f32[2,2,2,128,128]{4,3,2,1,0:T(8,128)S(1)}, f32[2,2,2,128,128]{4,3,2,1,0:T(8,128)S(1)}) while((s32[]{:T(128)}, f32[2,2,128,128]{3,2,1,0:T(8,128)}, f32[2,2,128,128]{3,2,1,0:T(8,128)}, ...), condition=%wide.region_3.4_spmd.clone.clone, body=%wide.region_2.3_spmd.clone.sunk.clone | while | flops 201457664 | bytes 2885202 | solution.py:139
  56.4 2.6 %collective-permute-start.6 = (f32[2,2,128,128]{3,2,1,0:T(8,128)}, f32[2,2,128,128]{3,2,1,0:T(8,128)S(1)}, u32[]{:S(2)}, u32[]{:S(2)}) collective-permute-start(f32[2,2,128,128]{3,2,1,0:T(8,128)} %get-tuple-element.71), channel_id=1, source_target_pairs={{0,8},{8,16},{16,24},{24,32},{32,40},{40,48},{48,56},{56,64},{64,7... | collective-permute-start | bytes 786440 | tf_op jit(solution)/shard_map/ppermute | solution.py:18
  59.0 3.5 %collective-permute-start.2 = (f32[2,2,128,128]{3,2,1,0:T(8,128)}, f32[2,2,128,128]{3,2,1,0:T(8,128)S(1)}, u32[]{:S(2)}, u32[]{:S(2)}) collective-permute-start(f32[2,2,128,128]{3,2,1,0:T(8,128)} %get-tuple-element.70), channel_id=1, source_target_pairs={{0,8},{8,16},{16,24},{24,32},{32,40},{40,48},{48,56},{56,64},{64,7... | collective-permute-start | bytes 786440 | tf_op jit(solution)/shard_map/ppermute | solution.py:18
  62.5 8.5 %collective-permute-done.6 = f32[2,2,128,128]{3,2,1,0:T(8,128)S(1)} collective-permute-done((f32[2,2,128,128]{3,2,1,0:T(8,128)}, f32[2,2,128,128]{3,2,1,0:T(8,128)S(1)}, u32[]{:S(2)}, u32[]{:S(2)}) %collective-permute-start.6) | collective-permute-done | bytes 262176 | tf_op jit(solution)/shard_map/ppermute | solution.py:18
  76.1 2.1 %convolution_select_fusion.3 = f32[2,2,128,128]{3,2,1,0:T(8,128)} fusion(f32[2,2,128,128]{3,2,1,0:T(8,128)} %get-tuple-element.70, f32[2,2,128,128]{3,2,1,0:T(8,128)S(1)} %collective-permute-done.2, pred[]{:T(512)S(6)} %ge.26), kind=kOutput, calls=%fused_computation.46 | convolution fusion | flops 100728832 | bytes 786433 | tf_op jit(solution)/shard_map/hrke,hrev->hrkv/dot_general | solution.py:53
  78.2 3.9 %collective-permute-start.3 = (f32[2,2,128,128]{3,2,1,0:T(8,128)}, f32[2,2,128,128]{3,2,1,0:T(8,128)}, u32[]{:S(2)}, u32[]{:S(2)}) collective-permute-start(f32[2,2,128,128]{3,2,1,0:T(8,128)} %convolution_select_fusion.3), channel_id=1, source_target_pairs={{0,16},{8,24},{16,32},{24,40},{32,48},{40,56},{48,64},{56,72},{64,... | collective-permute-start | bytes 786440 | tf_op jit(solution)/shard_map/ppermute | solution.py:18
  82.1 3.3 %collective-permute-done.7 = f32[2,2,128,128]{3,2,1,0:T(8,128)S(1)} collective-permute-done((f32[2,2,128,128]{3,2,1,0:T(8,128)S(1)}, f32[2,2,128,128]{3,2,1,0:T(8,128)S(1)}, u32[]{:S(2)}, u32[]{:S(2)}) %collective-permute-start.7) | collective-permute-done | bytes 262176 | tf_op jit(solution)/shard_map/ppermute | solution.py:18
  85.4 2.1 convolution_add_fusion.6
  87.4 2.0 collective-permute-start.8
  94.5 2.1 collective-permute-start.4
  96.6 6.4 %collective-permute-done.8 = f32[2,2,128,128]{3,2,1,0:T(8,128)} collective-permute-done((f32[2,2,128,128]{3,2,1,0:T(8,128)}, f32[2,2,128,128]{3,2,1,0:T(8,128)}, u32[]{:S(2)}, u32[]{:S(2)}) %collective-permute-start.8) | collective-permute-done | bytes 262176 | tf_op jit(solution)/shard_map/ppermute | solution.py:18
  110.8 18.7 %collective-permute-done.9 = f32[2,2,128,128]{3,2,1,0:T(8,128)S(1)} collective-permute-done((f32[2,2,128,128]{3,2,1,0:T(8,128)S(1)}, f32[2,2,128,128]{3,2,1,0:T(8,128)S(1)}, u32[]{:S(2)}, u32[]{:S(2)}) %collective-permute-start.9) | collective-permute-done | bytes 262176 | tf_op jit(solution)/shard_map/ppermute | solution.py:18
  134.3 7.8 %collective-permute-done.10 = f32[2,2,128,128]{3,2,1,0:T(8,128)S(1)} collective-permute-done((f32[2,2,128,128]{3,2,1,0:T(8,128)S(1)}, f32[2,2,128,128]{3,2,1,0:T(8,128)S(1)}, u32[]{:S(2)}, u32[]{:S(2)}) %collective-permute-start.10) | collective-permute-done | bytes 262176 | tf_op jit(solution)/shard_map/ppermute | solution.py:18
  142.5 2.1 %collective-permute-start.11 = (f32[2,2,128,128]{3,2,1,0:T(8,128)S(1)}, f32[2,2,128,128]{3,2,1,0:T(8,128)S(1)}, u32[]{:S(2)}, u32[]{:S(2)}) collective-permute-start(f32[2,2,128,128]{3,2,1,0:T(8,128)S(1)} %convolution_add_fusion.3), channel_id=1, source_target_pairs={{0,8},{8,16},{16,24},{24,32},{32,40},{40,48},{48,56},{56,64},{64,7... | collective-permute-start | bytes 786440 | tf_op jit(solution)/shard_map/ppermute | solution.py:18
  146.3 7.8 %collective-permute-done.11 = f32[2,2,128,128]{3,2,1,0:T(8,128)S(1)} collective-permute-done((f32[2,2,128,128]{3,2,1,0:T(8,128)S(1)}, f32[2,2,128,128]{3,2,1,0:T(8,128)S(1)}, u32[]{:S(2)}, u32[]{:S(2)}) %collective-permute-start.11) | collective-permute-done | bytes 262176 | tf_op jit(solution)/shard_map/ppermute | solution.py:18
  154.1 5.1 %while.27 = (s32[]{:T(128)}, f32[2,2,128,128]{3,2,1,0:T(8,128)S(1)}, f32[2,2,2,128,128]{4,3,2,1,0:T(8,128)}, f32[2,2,2,128,128]{4,3,2,1,0:T(8,128)S(1)}, f32[2,2...) while((s32[]{:T(128)}, ...), condition=%wide.region_5.6_spmd.clone, body=%wide.region_4.5_spmd.sunk.clone | while | flops 201457664 | bytes 2623573 | solution.py:167
  154.1 2.1 %fusion.238 = f32[2,2,2,128,128]{4,3,2,1,0:T(8,128)} fusion(f32[2,2,2,128,128]{4,3,2,1,0:T(8,128)} %get-tuple-element.315, s32[]{:T(128)S(6)} %copy.90, f32[2,2,128,128]{3,2,1,0:T(8,128)S(1)} %copy.101, f32[2,2,2,128,128]{4,3,0,2,1:T(8,128)} %get-tuple-element.326, f32[2,2,2,128,128]{4,3,0,2,1:T(8,128)} %get-tuple-element.325), kind=kOutput, calls=%fused_computation.2.clone.1.clone | convolution fusion | flops 100728832 | bytes 1049600 | tf_op jit(solution)/shard_map/while/body/eval_jaxpr/hrck,hrkv->hrcv/dot_general | solution.py:163
  156.7 2.1 %fusion.238 = f32[2,2,2,128,128]{4,3,2,1,0:T(8,128)} fusion(f32[2,2,2,128,128]{4,3,2,1,0:T(8,128)} %get-tuple-element.315, s32[]{:T(128)S(6)} %copy.90, f32[2,2,128,128]{3,2,1,0:T(8,128)S(1)} %copy.101, f32[2,2,2,128,128]{4,3,0,2,1:T(8,128)} %get-tuple-element.326, f32[2,2,2,128,128]{4,3,0,2,1:T(8,128)} %get-tuple-element.325), kind=kOutput, calls=%fused_computation.2.clone.1.clone | convolution fusion | flops 100728832 | bytes 1049600 | tf_op jit(solution)/shard_map/while/body/eval_jaxpr/hrck,hrkv->hrcv/dot_general | solution.py:163
  163.7 2.8 %convolution_convert_fusion = bf16[256,2048]{1,0:T(8,128)(2,1)} fusion(bf16[512,2048]{1,0:T(8,128)(2,1)S(1)} %copy-done, bf16[256,512]{1,0:T(8,128)(2,1)S(1)} %copy-done.9, f32[256,512]{1,0:T(8,128)} %reshape.588, f32[32,8,4,128]{3,2,1,0:T(4,128)S(1)} %bitcast.158, f32[512]{0:T(512)S(1)} %broadcast_bitcast_fusion), kind=kOutput, calls=%fused_computation.22 | convolution fusion | flops 538574848 | bytes 4458496 | tf_op jit(solution)/shard_map/dot_general | solution.py:179
  166.6 33.8 %reduce-scatter.2.cloned.1.call-done = bf16[32,2048]{1,0:T(8,128)(2,1)} async-done(((bf16[256,2048]{1,0:T(8,128)(2,1)}), bf16[32,2048]{1,0:T(8,128)(2,1)}) %reduce-scatter.2.cloned.1.call-update) | async-done | bytes 131088 | tf_op jit(solution)/shard_map/reduce_scatter | solution.py:178
  (119 shorter events, 67.1 us)
Async XLA Ops:
  6.5 157.2 %copy-start = (bf16[512,2048]{1,0:T(8,128)(2,1)S(1)}, bf16[512,2048]{1,0:T(8,128)(2,1)}, u32[]{:S(2)}) copy-start(bf16[512,2048]{1,0:T(8,128)(2,1)} %param.25) | copy-start | bytes 6291460
  6.5 193.8 %reduce-scatter.2.cloned.1.call-start = ((), (), s32[]{:S(2)}) async-start(), calls=%async_computation.1 | async-start | bytes 1179648 | tf_op jit(solution)/shard_map/reduce_scatter | solution.py:178
  7.4 17.1 %collective-permute-start = (bf16[3,256]{1,0:T(4,128)(2,1)S(1)}, bf16[3,256]{1,0:T(4,128)(2,1)S(1)}, u32[]{:S(2)}, u32[]{:S(2)}) collective-permute-start(bf16[3,256]{1,0:T(4,128)(2,1)S(1)} %slice.92), channel_id=1, source_target_pairs={{0,8},{8,16},{16,24},{24,32},{32,40},{40,48},{48,56},{56,64},{64,7... | collective-permute-start | bytes 4616 | tf_op jit(solution)/shard_map/ppermute | solution.py:18
  11.6 27.5 %collective-permute-start.1 = (bf16[3,512]{1,0:T(4,128)(2,1)S(1)}, bf16[3,512]{1,0:T(4,128)(2,1)S(1)}, u32[]{:S(2)}, u32[]{:S(2)}) collective-permute-start(bf16[3,512]{1,0:T(4,128)(2,1)S(1)} %slice.101), channel_id=1, source_target_pairs={{0,8},{8,16},{16,24},{24,32},{32,40},{40,48},{48,56},{56,64},{64,7... | collective-permute-start | bytes 9224 | tf_op jit(solution)/shard_map/ppermute | solution.py:18
  15.7 58.6 %collective-permute-start.12 = (bf16[3,256]{1,0:T(4,128)(2,1)S(1)}, bf16[3,256]{1,0:T(4,128)(2,1)S(1)}, u32[]{:S(2)}, u32[]{:S(2)}) collective-permute-start(bf16[3,256]{1,0:T(4,128)(2,1)S(1)} %slice.112), channel_id=1, source_target_pairs={{0,8},{8,16},{16,24},{24,32},{32,40},{40,48},{48,56},{56,64},{64,7... | collective-permute-start | bytes 4616 | tf_op jit(solution)/shard_map/ppermute | solution.py:18
  26.6 18.5 %copy-start.1 = (f32[2,2,128,128]{3,2,1,0:T(8,128)}, f32[2,2,128,128]{3,2,1,0:T(8,128)S(1)}, u32[]{:S(2)}) copy-start(f32[2,2,128,128]{3,2,1,0:T(8,128)S(1)} %fusion.71) | copy-start | bytes 786436
  36.5 2.6 %copy-start.7 = (bf16[256,512]{1,0:T(8,128)(2,1)S(1)}, bf16[256,512]{1,0:T(8,128)(2,1)}, u32[]{:S(2)}) copy-start(bf16[256,512]{1,0:T(8,128)(2,1)} %param.17) | copy-start | bytes 786436
  40.3 3.7 %copy-start.6 = (f32[2,2,2,128,128]{4,3,2,1,0:T(8,128)S(1)}, f32[2,2,2,128,128]{4,3,2,1,0:T(8,128)}, u32[]{:S(2)}) copy-start(f32[2,2,2,128,128]{4,3,2,1,0:T(8,128)} %fusion.21) | copy-start | bytes 1572868
  45.1 3.1 %copy-start.3 = (f32[2,2,2,128,256]{4,3,2,1,0:T(8,128)}, f32[2,2,2,128,256]{4,3,2,1,0:T(8,128)S(1)}, u32[]{:S(2)}) copy-start(f32[2,2,2,128,256]{4,3,2,1,0:T(8,128)S(1)} %fusion.28) | copy-start | bytes 3145732
  48.2 10.8 %copy-start.8 = (bf16[4,256]{1,0:T(4,128)(2,1)S(1)}, bf16[4,256]{1,0:T(4,128)(2,1)}, u32[]{:S(2)}) copy-start(bf16[4,256]{1,0:T(4,128)(2,1)} %param.21) | copy-start | bytes 6148
  56.4 14.6 %collective-permute-start.6 = (f32[2,2,128,128]{3,2,1,0:T(8,128)}, f32[2,2,128,128]{3,2,1,0:T(8,128)S(1)}, u32[]{:S(2)}, u32[]{:S(2)}) collective-permute-start(f32[2,2,128,128]{3,2,1,0:T(8,128)} %get-tuple-element.71), channel_id=1, source_target_pairs={{0,8},{8,16},{16,24},{24,32},{32,40},{40,48},{48,56},{56,64},{64,7... | collective-permute-start | bytes 786440 | tf_op jit(solution)/shard_map/ppermute | solution.py:18
  59.0 17.0 %collective-permute-start.2 = (f32[2,2,128,128]{3,2,1,0:T(8,128)}, f32[2,2,128,128]{3,2,1,0:T(8,128)S(1)}, u32[]{:S(2)}, u32[]{:S(2)}) collective-permute-start(f32[2,2,128,128]{3,2,1,0:T(8,128)} %get-tuple-element.70), channel_id=1, source_target_pairs={{0,8},{8,16},{16,24},{24,32},{32,40},{40,48},{48,56},{56,64},{64,7... | collective-permute-start | bytes 786440 | tf_op jit(solution)/shard_map/ppermute | solution.py:18
  72.4 13.0 %collective-permute-start.7 = (f32[2,2,128,128]{3,2,1,0:T(8,128)S(1)}, f32[2,2,128,128]{3,2,1,0:T(8,128)S(1)}, u32[]{:S(2)}, u32[]{:S(2)}) collective-permute-start(f32[2,2,128,128]{3,2,1,0:T(8,128)S(1)} %convolution_add_fusion.7), channel_id=1, source_target_pairs={{0,16},{8,24},{16,32},{24,40},{32,48},{40,56},{48,64},{56,72},{64,... | collective-permute-start | bytes 786440 | tf_op jit(solution)/shard_map/ppermute | solution.py:18
  78.2 14.8 %collective-permute-start.3 = (f32[2,2,128,128]{3,2,1,0:T(8,128)}, f32[2,2,128,128]{3,2,1,0:T(8,128)}, u32[]{:S(2)}, u32[]{:S(2)}) collective-permute-start(f32[2,2,128,128]{3,2,1,0:T(8,128)} %convolution_select_fusion.3), channel_id=1, source_target_pairs={{0,16},{8,24},{16,32},{24,40},{32,48},{40,56},{48,64},{56,72},{64,... | collective-permute-start | bytes 786440 | tf_op jit(solution)/shard_map/ppermute | solution.py:18
  87.4 18.9 %copy-start.2 = (f32[2,2,128,128]{3,2,1,0:T(8,128)S(1)}, f32[2,2,128,128]{3,2,1,0:T(8,128)}, u32[]{:S(2)}) copy-start(f32[2,2,128,128]{3,2,1,0:T(8,128)} %copy-done.1) | copy-start | bytes 786436
  87.4 15.5 %collective-permute-start.8 = (f32[2,2,128,128]{3,2,1,0:T(8,128)}, f32[2,2,128,128]{3,2,1,0:T(8,128)}, u32[]{:S(2)}, u32[]{:S(2)}) collective-permute-start(f32[2,2,128,128]{3,2,1,0:T(8,128)} %convolution_add_fusion.6), channel_id=1, source_target_pairs={{0,32},{8,40},{16,48},{24,56},{32,64},{40,72},{48,80},{56,88},{64,... | collective-permute-start | bytes 786440 | tf_op jit(solution)/shard_map/ppermute | solution.py:18
  92.1 15.8 %copy-start.5 = (f32[2,128,2,128]{3,2,1,0:T(2,128)S(1)}, f32[2,128,2,128]{3,2,1,0:T(2,128)}, u32[]{:S(2)}) copy-start(f32[2,128,2,128]{3,2,1,0:T(2,128)} %reshape.587) | copy-start | bytes 786436
  94.5 36.7 %copy-start.4 = (f32[2,2,2,128,256]{4,3,2,1,0:T(8,128)S(1)}, f32[2,2,2,128,256]{4,3,2,1,0:T(8,128)}, u32[]{:S(2)}) copy-start(f32[2,2,2,128,256]{4,3,2,1,0:T(8,128)} %copy-done.3) | copy-start | bytes 3145732
  94.5 13.9 %collective-permute-start.4 = (f32[2,2,128,128]{3,2,1,0:T(8,128)S(1)}, f32[2,2,128,128]{3,2,1,0:T(8,128)S(1)}, u32[]{:S(2)}, u32[]{:S(2)}) collective-permute-start(f32[2,2,128,128]{3,2,1,0:T(8,128)S(1)} %convolution_select_fusion.2), channel_id=1, source_target_pairs={{0,32},{8,40},{16,48},{24,56},{32,64},{40,72},{48,80},{56,88},{64,... | collective-permute-start | bytes 786440 | tf_op jit(solution)/shard_map/ppermute | solution.py:18
  104.4 25.2 %collective-permute-start.9 = (f32[2,2,128,128]{3,2,1,0:T(8,128)S(1)}, f32[2,2,128,128]{3,2,1,0:T(8,128)S(1)}, u32[]{:S(2)}, u32[]{:S(2)}) collective-permute-start(f32[2,2,128,128]{3,2,1,0:T(8,128)S(1)} %convolution_add_fusion.5), channel_id=1, source_target_pairs={{0,64},{8,72},{16,80},{24,88},{32,96},{40,104},{48,112},{56,120},{... | collective-permute-start | bytes 786440 | tf_op jit(solution)/shard_map/ppermute | solution.py:18
  108.9 25.0 %collective-permute-start.5 = (f32[2,2,128,128]{3,2,1,0:T(8,128)S(1)}, f32[2,2,128,128]{3,2,1,0:T(8,128)S(1)}, u32[]{:S(2)}, u32[]{:S(2)}) collective-permute-start(f32[2,2,128,128]{3,2,1,0:T(8,128)S(1)} %convolution_select_fusion.1), channel_id=1, source_target_pairs={{0,64},{8,72},{16,80},{24,88},{32,96},{40,104},{48,112},{56,120},{... | collective-permute-start | bytes 786440 | tf_op jit(solution)/shard_map/ppermute | solution.py:18
  129.9 12.2 %collective-permute-start.10 = (f32[2,2,128,128]{3,2,1,0:T(8,128)S(1)}, f32[2,2,128,128]{3,2,1,0:T(8,128)S(1)}, u32[]{:S(2)}, u32[]{:S(2)}) collective-permute-start(f32[2,2,128,128]{3,2,1,0:T(8,128)S(1)} %convolution_add_fusion.4), channel_id=1, source_target_pairs={{0,128},{8,136},{16,144},{24,152},{32,160},{40,168},{48,176},{56,1... | collective-permute-start | bytes 786440 | tf_op jit(solution)/shard_map/ppermute | solution.py:18
  142.5 11.6 %collective-permute-start.11 = (f32[2,2,128,128]{3,2,1,0:T(8,128)S(1)}, f32[2,2,128,128]{3,2,1,0:T(8,128)S(1)}, u32[]{:S(2)}, u32[]{:S(2)}) collective-permute-start(f32[2,2,128,128]{3,2,1,0:T(8,128)S(1)} %convolution_add_fusion.3), channel_id=1, source_target_pairs={{0,8},{8,16},{16,24},{24,32},{32,40},{40,48},{48,56},{56,64},{64,7... | collective-permute-start | bytes 786440 | tf_op jit(solution)/shard_map/ppermute | solution.py:18
  159.2 4.5 %copy-start.9 = (bf16[256,512]{1,0:T(8,128)(2,1)S(1)}, bf16[256,512]{1,0:T(8,128)(2,1)}, u32[]{:S(2)}) copy-start(bf16[256,512]{1,0:T(8,128)(2,1)} %param.18) | copy-start | bytes 786436
Sparse Core Ops, SparseCore 0:
  166.7 33.5 reduce-scatter.1

commit v3 on v2

--- a/solution.py
+++ b/solution.py
@@ -146,7 +146,9 @@
     distance = 1
     while distance < seq_size:
         if 2 * distance < seq_size:
-            earlier_map, earlier_end = shifted((prefix_map, prefix_end), "seq", distance)
+            earlier_map, earlier_end = shifted(
+                jnp.stack([prefix_map, prefix_end]), "seq", distance
+            )
             prefix_end = apply_map(prefix_map, earlier_end) + prefix_end
             prefix_map = jnp.where(
                 seq_index >= distance, apply_map(prefix_map, earlier_map), prefix_map
@@ -175,12 +177,17 @@
     scale_rows = lax.rsqrt(jnp.mean(core_out * core_out, axis=-1, keepdims=True) + epsilon)
     normed = core_out * scale_rows * norm_gain.astype(jnp.float32) * jax.nn.silu(gate_values)
     hidden = normed.reshape(local_rows, value_heads * DV).astype(jnp.bfloat16)
-    return lax.psum_scatter(
-        jnp.dot(hidden, out_weight, preferred_element_type=jnp.float32).astype(jnp.bfloat16),
+    partial_sum = jnp.dot(hidden, out_weight, preferred_element_type=jnp.float32).astype(
+        jnp.bfloat16
+    )
+    head_size = lax.axis_size("head")
+    pieces = lax.all_to_all(
+        partial_sum.reshape(head_size, local_rows // head_size, partial_sum.shape[1]),
         "head",
-        scatter_dimension=0,
-        tiled=True,
-    )
+        0,
+        0,
+    )
+    return jnp.sum(pieces.astype(jnp.float32), axis=0).astype(jnp.bfloat16)
 
 
 def solution(mesh):

time: 210 us -> 202 us (0.962)
  the two profiles are of different devices: /device:TPU:128 before, /device:TPU:192 now
where the time goes in v3:
time: 202 us; the launch traced here: 200 us
  waiting for transfers between devices  79.3 us (39%)
  matrix products  43.9 us (22%)
  starting transfers between devices  21.6 us (11%)
  blocking collectives  20 us (10%)
  local copies, waits for them, and re-layouts  18.8 us (9%)
  other arithmetic  15.6 us (8%)
    ppermute x9, waiting for transfers between devices, shifted(): return lax.ppermute(array, axis, pairs)  79.3 us
    ppermute x9, starting transfers between devices, shifted(): return lax.ppermute(array, axis, pairs)  21.6 us
    all_to_all x1, blocking collectives, shards(): lax.all_to_all(partial_sum.reshape(head_size, local_rows // head_size, pa...  20 us
    dot_general x15, matrix products, apply_map(): return jnp.einsum('hrke,hrev->hrkv', matrix, state_now, precision=highest)  15.8 us
    dot_general x7, matrix products, unit_lower_inverse(): jnp.einsum('...ij,...jk->...ik', inverse, coupling, precision=highest)  6.96 us
    dot_general x7, matrix products, unit_lower_inverse(): jnp.einsum('...ij,...jk->...ik', jnp.einsum('...ij,...jk->...ik', inverse...  6.23 us
    another operation x4, other arithmetic, shards(): jnp.stack([prefix_map, prefix_end])  4.32 us
    dot_general x2, matrix products, replay(): jnp.einsum('hrck,hrkv->hrcv', coupling_now, state_now, precision=highest)  4.29 us
  transfers between devices with their start and end apart: 9, of which 6 were waited for; matrix products, arithmetic and copies ran while one was open for 20% of the time, Pallas kernels for 0%

profile of v3, /device:TPU:192, one launch (start us, length us, event | category | flops | bytes accessed | tf_op | source)
XLA Modules:
  0.0 200.2 jit_solution(10911658109493588217)
XLA Ops:
  0.8 3.5 %collective-permute-start = (bf16[3,256]{1,0:T(4,128)(2,1)S(1)}, bf16[3,256]{1,0:T(4,128)(2,1)S(1)}, u32[]{:S(2)}, u32[]{:S(2)}) collective-permute-start(bf16[3,256]{1,0:T(4,128)(2,1)S(1)} %slice.92), channel_id=1, source_target_pairs={{0,8},{8,16},{16,24},{24,32},{32,40},{40,48},{48,56},{56,64},{64,7... | collective-permute-start | bytes 4616 | tf_op jit(solution)/shard_map/ppermute | solution.py:18
  5.6 3.5 %collective-permute-start.1 = (bf16[3,512]{1,0:T(4,128)(2,1)}, bf16[3,512]{1,0:T(4,128)(2,1)}, u32[]{:S(2)}, u32[]{:S(2)}) collective-permute-start(bf16[3,512]{1,0:T(4,128)(2,1)} %slice.101), channel_id=1, source_target_pairs={{0,8},{8,16},{16,24},{24,32},{32,40},{40,48},{48,56},{56,64},{64,7... | collective-permute-start | bytes 9224 | tf_op jit(solution)/shard_map/ppermute | solution.py:18
  31.4 1.6 fusion.21
  35.0 2.2 %reshape.589 = f32[2,128,2,2,128]{4,3,2,1,0:T(2,128)} reshape(f32[256,512]{1,0:T(8,128)} %divide_multiply_fusion) | data formatting | bytes 1048576 | tf_op jit(solution)/shard_map/reshape | solution.py:90
  42.2 5.0 %while.28 = (s32[]{:T(128)}, f32[2,2,128,128]{3,2,1,0:T(8,128)S(1)}, f32[2,2,128,128]{3,2,1,0:T(8,128)}, f32[2,2,2,128,128]{4,3,2,1,0:T(8,128)S(1)}, f32[2,2,2,128,128]{4,3,2,1,0:T(8,128)S(1)}) while((s32[]{:T(128)}, f32[2,2,128,128]{3,2,1,0:T(8,128)S(1)}, f32[2,2,128,128]{3,2,1,0:T(8,128)}, ...), condition=%wide.region_3.4_spmd.clone.clone, body=%wide.region_2.3_spmd.clone.sunk.clone | while | flops 201457664 | bytes 2884683 | solution.py:139
  47.2 1.8 pad_maximum_fusion
  49.0 3.2 %collective-permute-start.2 = (f32[2,2,2,128,128]{4,3,2,1,0:T(8,128)}, f32[2,2,2,128,128]{4,3,2,1,0:T(8,128)}, u32[]{:S(2)}, u32[]{:S(2)}) collective-permute-start(f32[2,2,2,128,128]{4,3,2,1,0:T(8,128)} %pad_maximum_fusion), channel_id=1, source_target_pairs={{0,8},{8,16},{16,24},{24,32},{32,40},{40,48},{48,56},{56,64},{64,7... | collective-permute-start | bytes 1572872 | tf_op jit(solution)/shard_map/ppermute | solution.py:18
  52.2 14.2 %collective-permute-done.2 = f32[2,2,2,128,128]{4,3,2,1,0:T(8,128)} collective-permute-done((f32[2,2,2,128,128]{4,3,2,1,0:T(8,128)}, f32[2,2,2,128,128]{4,3,2,1,0:T(8,128)}, u32[]{:S(2)}, u32[]{:S(2)}) %collective-permute-start.2) | collective-permute-done | bytes 524320 | tf_op jit(solution)/shard_map/ppermute | solution.py:18
  70.8 1.9 collective-permute-start.3
  72.8 14.9 %collective-permute-done.3 = f32[2,2,2,128,128]{4,3,2,1,0:T(8,128)} collective-permute-done((f32[2,2,2,128,128]{4,3,2,1,0:T(8,128)}, f32[2,2,2,128,128]{4,3,2,1,0:T(8,128)}, u32[]{:S(2)}, u32[]{:S(2)}) %collective-permute-start.3) | collective-permute-done | bytes 524320 | tf_op jit(solution)/shard_map/ppermute | solution.py:18
  91.7 2.9 %collective-permute-start.4 = (f32[2,2,2,128,128]{4,3,2,1,0:T(8,128)}, f32[2,2,2,128,128]{4,3,2,1,0:T(8,128)}, u32[]{:S(2)}, u32[]{:S(2)}) collective-permute-start(f32[2,2,2,128,128]{4,3,2,1,0:T(8,128)} %pad_maximum_fusion.2), channel_id=1, source_target_pairs={{0,32},{8,40},{16,48},{24,56},{32,64},{40,72},{48,80},{56,88},{64,... | collective-permute-start | bytes 1572872 | tf_op jit(solution)/shard_map/ppermute | solution.py:18
  95.3 1.9 collective-permute-start.8
  97.3 8.0 %collective-permute-done.4 = f32[2,2,2,128,128]{4,3,2,1,0:T(8,128)} collective-permute-done((f32[2,2,2,128,128]{4,3,2,1,0:T(8,128)}, f32[2,2,2,128,128]{4,3,2,1,0:T(8,128)}, u32[]{:S(2)}, u32[]{:S(2)}) %collective-permute-start.4) | collective-permute-done | bytes 524320 | tf_op jit(solution)/shard_map/ppermute | solution.py:18
  111.2 1.8 reshape.590
  115.7 20.7 %collective-permute-done.5 = f32[2,2,2,128,128]{4,3,2,1,0:T(8,128)} collective-permute-done((f32[2,2,2,128,128]{4,3,2,1,0:T(8,128)}, f32[2,2,2,128,128]{4,3,2,1,0:T(8,128)}, u32[]{:S(2)}, u32[]{:S(2)}) %collective-permute-start.5) | collective-permute-done | bytes 524320 | tf_op jit(solution)/shard_map/ppermute | solution.py:18
  142.2 13.7 %collective-permute-done.6 = f32[2,2,128,128]{3,2,1,0:T(8,128)S(1)} collective-permute-done((f32[2,2,128,128]{3,2,1,0:T(8,128)S(1)}, f32[2,2,128,128]{3,2,1,0:T(8,128)S(1)}, u32[]{:S(2)}, u32[]{:S(2)}) %collective-permute-start.6) | collective-permute-done | bytes 262176 | tf_op jit(solution)/shard_map/ppermute | solution.py:18
  156.3 2.1 %collective-permute-start.7 = (f32[2,2,128,128]{3,2,1,0:T(8,128)S(1)}, f32[2,2,128,128]{3,2,1,0:T(8,128)S(1)}, u32[]{:S(2)}, u32[]{:S(2)}) collective-permute-start(f32[2,2,128,128]{3,2,1,0:T(8,128)S(1)} %convolution_add_fusion.3), channel_id=1, source_target_pairs={{0,8},{8,16},{16,24},{24,32},{32,40},{40,48},{48,56},{56,64},{64,7... | collective-permute-start | bytes 786440 | tf_op jit(solution)/shard_map/ppermute | solution.py:18
  158.5 1.6 fusion.19
  160.1 7.8 %collective-permute-done.7 = f32[2,2,128,128]{3,2,1,0:T(8,128)S(1)} collective-permute-done((f32[2,2,128,128]{3,2,1,0:T(8,128)S(1)}, f32[2,2,128,128]{3,2,1,0:T(8,128)S(1)}, u32[]{:S(2)}, u32[]{:S(2)}) %collective-permute-start.7) | collective-permute-done | bytes 262176 | tf_op jit(solution)/shard_map/ppermute | solution.py:18
  167.9 5.2 %while.27 = (s32[]{:T(128)}, f32[2,2,128,128]{3,2,1,0:T(8,128)S(1)}, f32[2,2,2,128,128]{4,3,2,1,0:T(8,128)}, f32[2,2,2,128,128]{4,3,2,1,0:T(8,128)S(1)}, f32[2,2...) while((s32[]{:T(128)}, ...), condition=%wide.region_5.6_spmd.clone, body=%wide.region_4.5_spmd.sunk.clone | while | flops 201457664 | bytes 2623565 | solution.py:169
  167.9 2.1 %fusion.230 = f32[2,2,2,128,128]{4,3,2,1,0:T(8,128)} fusion(f32[2,2,2,128,128]{4,3,2,1,0:T(8,128)} %get-tuple-element.315, s32[]{:T(128)} %get-tuple-element.313, f32[2,2,128,128]{3,2,1,0:T(8,128)S(1)} %copy.101, f32[2,2,2,128,128]{4,3,0,2,1:T(8,128)} %get-tuple-element.326, f32[2,2,2,128,128]{4,3,0,2,1:T(8,128)} %get-tuple-element.325), kind=kOutput, calls=%fused_computation.2.clone.1.clone | convolution fusion | flops 100728832 | bytes 1049600 | tf_op jit(solution)/shard_map/while/body/eval_jaxpr/hrck,hrkv->hrcv/dot_general | solution.py:165
  170.5 2.1 %fusion.230 = f32[2,2,2,128,128]{4,3,2,1,0:T(8,128)} fusion(f32[2,2,2,128,128]{4,3,2,1,0:T(8,128)} %get-tuple-element.315, s32[]{:T(128)} %get-tuple-element.313, f32[2,2,128,128]{3,2,1,0:T(8,128)S(1)} %copy.101, f32[2,2,2,128,128]{4,3,0,2,1:T(8,128)} %get-tuple-element.326, f32[2,2,2,128,128]{4,3,0,2,1:T(8,128)} %get-tuple-element.325), kind=kOutput, calls=%fused_computation.2.clone.1.clone | convolution fusion | flops 100728832 | bytes 1049600 | tf_op jit(solution)/shard_map/while/body/eval_jaxpr/hrck,hrkv->hrcv/dot_general | solution.py:165
  177.6 1.8 convolution_convert_fusion
  179.4 20.0 %all_to_all.5 = bf16[8,32,2048]{2,1,0:T(8,128)(2,1)S(1)} all-to-all(bf16[8,32,2048]{2,1,0:T(8,128)(2,1)S(1)} %bitcast.191), channel_id=1, replica_groups=mesh['seq'=32,'head'=8] {'head'}, dimensions={0} | all-to-all | bytes 2097152 | tf_op jit(solution)/shard_map/all_to_all | solution.py:184
  (148 shorter events, 65.7 us)
Async XLA Ops:
  0.0 177.5 %copy-start = (bf16[512,2048]{1,0:T(8,128)(2,1)S(1)}, bf16[512,2048]{1,0:T(8,128)(2,1)}, u32[]{:S(2)}) copy-start(bf16[512,2048]{1,0:T(8,128)(2,1)} %param.25) | copy-start | bytes 6291460
  0.8 16.1 %collective-permute-start = (bf16[3,256]{1,0:T(4,128)(2,1)S(1)}, bf16[3,256]{1,0:T(4,128)(2,1)S(1)}, u32[]{:S(2)}, u32[]{:S(2)}) collective-permute-start(bf16[3,256]{1,0:T(4,128)(2,1)S(1)} %slice.92), channel_id=1, source_target_pairs={{0,8},{8,16},{16,24},{24,32},{32,40},{40,48},{48,56},{56,64},{64,7... | collective-permute-start | bytes 4616 | tf_op jit(solution)/shard_map/ppermute | solution.py:18
  5.6 27.4 %collective-permute-start.1 = (bf16[3,512]{1,0:T(4,128)(2,1)}, bf16[3,512]{1,0:T(4,128)(2,1)}, u32[]{:S(2)}, u32[]{:S(2)}) collective-permute-start(bf16[3,512]{1,0:T(4,128)(2,1)} %slice.101), channel_id=1, source_target_pairs={{0,8},{8,16},{16,24},{24,32},{32,40},{40,48},{48,56},{56,64},{64,7... | collective-permute-start | bytes 9224 | tf_op jit(solution)/shard_map/ppermute | solution.py:18
  18.8 3.8 %copy-start.16 = (pred[128,128]{1,0:T(8,128)(4,1)S(1)}, pred[128,128]{1,0:T(8,128)(4,1)}, u32[]{:S(2)}) copy-start(pred[128,128]{1,0:T(8,128)(4,1)} %get-tuple-element.177) | copy-start | bytes 49156
  18.8 3.8 %copy-start.18 = (pred[128,128]{1,0:T(8,128)(4,1)S(1)}, pred[128,128]{1,0:T(8,128)(4,1)}, u32[]{:S(2)}) copy-start(pred[128,128]{1,0:T(8,128)(4,1)} %get-tuple-element.186) | copy-start | bytes 49156
  19.0 20.8 %copy-start.1 = (f32[2,2,128,128]{3,2,1,0:T(8,128)}, f32[2,2,128,128]{3,2,1,0:T(8,128)S(1)}, u32[]{:S(2)}) copy-start(f32[2,2,128,128]{3,2,1,0:T(8,128)S(1)} %fusion.71) | copy-start | bytes 786436
  30.5 3.3 %copy-start.20 = (f32[1,512]{1,0:T(1,128)S(1)}, f32[1,512]{1,0:T(1,128)}, u32[]{:S(2)}) copy-start(f32[1,512]{1,0:T(1,128)} %get-tuple-element.160) | copy-start | bytes 6148
  33.0 4.2 %copy-start.17 = (f32[2,2,2,128]{3,2,1,0:T(2,128)S(1)}, f32[2,2,2,128]{3,2,1,0:T(2,128)}, u32[]{:S(2)}) copy-start(f32[2,2,2,128]{3,2,1,0:T(2,128)} %get-tuple-element.158) | copy-start | bytes 12292
  35.0 3.8 %copy-start.11 = (f32[2,2,2,128,128]{4,3,2,1,0:T(8,128)S(1)}, f32[2,2,2,128,128]{4,3,2,1,0:T(8,128)}, u32[]{:S(2)}) copy-start(f32[2,2,2,128,128]{4,3,2,1,0:T(8,128)} %fusion.21) | copy-start | bytes 1572868
  49.0 17.4 %collective-permute-start.2 = (f32[2,2,2,128,128]{4,3,2,1,0:T(8,128)}, f32[2,2,2,128,128]{4,3,2,1,0:T(8,128)}, u32[]{:S(2)}, u32[]{:S(2)}) collective-permute-start(f32[2,2,2,128,128]{4,3,2,1,0:T(8,128)} %pad_maximum_fusion), channel_id=1, source_target_pairs={{0,8},{8,16},{16,24},{24,32},{32,40},{40,48},{48,56},{56,64},{64,7... | collective-permute-start | bytes 1572872 | tf_op jit(solution)/shard_map/ppermute | solution.py:18
  69.3 27.9 %copy-start.26 = (bf16[128]{0:T(256)(128)(2,1)S(1)}, bf16[128]{0:T(256)(128)(2,1)}, u32[]{:S(2)}) copy-start(bf16[128]{0:T(256)(128)(2,1)} %param.24) | copy-start | bytes 772
  69.3 28.0 %copy-start.24 = (bf16[4,256]{1,0:T(4,128)(2,1)S(1)}, bf16[4,256]{1,0:T(4,128)(2,1)}, u32[]{:S(2)}) copy-start(bf16[4,256]{1,0:T(4,128)(2,1)} %param.21) | copy-start | bytes 6148
  70.8 16.8 %collective-permute-start.3 = (f32[2,2,2,128,128]{4,3,2,1,0:T(8,128)}, f32[2,2,2,128,128]{4,3,2,1,0:T(8,128)}, u32[]{:S(2)}, u32[]{:S(2)}) collective-permute-start(f32[2,2,2,128,128]{4,3,2,1,0:T(8,128)} %pad_maximum_fusion.1), channel_id=1, source_target_pairs={{0,16},{8,24},{16,32},{24,40},{32,48},{40,56},{48,64},{56,72},{64,... | collective-permute-start | bytes 1572872 | tf_op jit(solution)/shard_map/ppermute | solution.py:18
  91.7 13.6 %collective-permute-start.4 = (f32[2,2,2,128,128]{4,3,2,1,0:T(8,128)}, f32[2,2,2,128,128]{4,3,2,1,0:T(8,128)}, u32[]{:S(2)}, u32[]{:S(2)}) collective-permute-start(f32[2,2,2,128,128]{4,3,2,1,0:T(8,128)} %pad_maximum_fusion.2), channel_id=1, source_target_pairs={{0,32},{8,40},{16,48},{24,56},{32,64},{40,72},{48,80},{56,88},{64,... | collective-permute-start | bytes 1572872 | tf_op jit(solution)/shard_map/ppermute | solution.py:18
  95.3 15.0 %collective-permute-start.8 = (bf16[3,256]{1,0:T(4,128)(2,1)S(1)}, bf16[3,256]{1,0:T(4,128)(2,1)S(1)}, u32[]{:S(2)}, u32[]{:S(2)}) collective-permute-start(bf16[3,256]{1,0:T(4,128)(2,1)S(1)} %slice.112), channel_id=1, source_target_pairs={{0,8},{8,16},{16,24},{24,32},{32,40},{40,48},{48,56},{56,64},{64,7... | collective-permute-start | bytes 4616 | tf_op jit(solution)/shard_map/ppermute | solution.py:18
  97.2 13.1 %copy-start.13 = (bf16[256,256]{1,0:T(8,128)(2,1)S(1)}, bf16[256,256]{1,0:T(8,128)(2,1)}, u32[]{:S(2)}) copy-start(bf16[256,256]{1,0:T(8,128)(2,1)} %param.15) | copy-start | bytes 393220
  106.7 3.6 %copy-start.9 = (f32[2,2,128,128]{3,2,1,0:T(8,128)}, f32[2,2,128,128]{3,2,1,0:T(8,128)S(1)}, u32[]{:S(2)}) copy-start(f32[2,2,128,128]{3,2,1,0:T(8,128)S(1)} %convolution_add_fusion.5) | copy-start | bytes 786436
  108.1 6.0 %copy-start.2 = (f32[2,2,128,128]{3,2,1,0:T(8,128)S(1)}, f32[2,2,128,128]{3,2,1,0:T(8,128)}, u32[]{:S(2)}) copy-start(f32[2,2,128,128]{3,2,1,0:T(8,128)} %copy-done.1) | copy-start | bytes 786436
  109.0 27.4 %collective-permute-start.5 = (f32[2,2,2,128,128]{4,3,2,1,0:T(8,128)}, f32[2,2,2,128,128]{4,3,2,1,0:T(8,128)}, u32[]{:S(2)}, u32[]{:S(2)}) collective-permute-start(f32[2,2,2,128,128]{4,3,2,1,0:T(8,128)} %pad_maximum_fusion.3), channel_id=1, source_target_pairs={{0,64},{8,72},{16,80},{24,88},{32,96},{40,104},{48,112},{56,120},{... | collective-permute-start | bytes 1572872 | tf_op jit(solution)/shard_map/ppermute | solution.py:18
  113.0 26.2 %copy-start.4 = (f32[2,2,2,128,256]{4,3,2,1,0:T(8,128)S(1)}, f32[2,2,2,128,256]{4,3,2,1,0:T(8,128)}, u32[]{:S(2)}) copy-start(f32[2,2,2,128,256]{4,3,2,1,0:T(8,128)} %copy-done.3) | copy-start | bytes 3145732
  113.0 27.8 %copy-start.6 = (f32[2,2,128,128]{3,2,1,0:T(8,128)S(1)}, f32[2,2,128,128]{3,2,1,0:T(8,128)}, u32[]{:S(2)}) copy-start(f32[2,2,128,128]{3,2,1,0:T(8,128)} %copy-done.5) | copy-start | bytes 786436
  137.9 18.0 %collective-permute-start.6 = (f32[2,2,128,128]{3,2,1,0:T(8,128)S(1)}, f32[2,2,128,128]{3,2,1,0:T(8,128)S(1)}, u32[]{:S(2)}, u32[]{:S(2)}) collective-permute-start(f32[2,2,128,128]{3,2,1,0:T(8,128)S(1)} %convolution_add_fusion.4), channel_id=1, source_target_pairs={{0,128},{8,136},{16,144},{24,152},{32,160},{40,168},{48,176},{56,1... | collective-permute-start | bytes 786440 | tf_op jit(solution)/shard_map/ppermute | solution.py:18
  156.3 11.6 %collective-permute-start.7 = (f32[2,2,128,128]{3,2,1,0:T(8,128)S(1)}, f32[2,2,128,128]{3,2,1,0:T(8,128)S(1)}, u32[]{:S(2)}, u32[]{:S(2)}) collective-permute-start(f32[2,2,128,128]{3,2,1,0:T(8,128)S(1)} %convolution_add_fusion.3), channel_id=1, source_target_pairs={{0,8},{8,16},{16,24},{24,32},{32,40},{40,48},{48,56},{56,64},{64,7... | collective-permute-start | bytes 786440 | tf_op jit(solution)/shard_map/ppermute | solution.py:18
  173.0 4.5 %copy-start.25 = (bf16[256,512]{1,0:T(8,128)(2,1)S(1)}, bf16[256,512]{1,0:T(8,128)(2,1)}, u32[]{:S(2)}) copy-start(bf16[256,512]{1,0:T(8,128)(2,1)} %param.18) | copy-start | bytes 786436
  (12 other events, 29.3 us)

commit v4 on v3

v4 whole, which is shorter than its diff:
```python
import jax
import jax.numpy as jnp
from jax import lax
from jax.sharding import PartitionSpec as P

DK = 128
DV = 128
SPAN = 128


epsilon = 1e-06
highest = lax.Precision.HIGHEST


def shifted(array, axis, by):
    length = lax.axis_size(axis)
    pairs = [(i, i + by) for i in range(length) if 0 <= i + by < length]
    return lax.ppermute(array, axis, pairs)


def conv_silu(signal, before, weights):
    length = signal.shape[0]
    padded = jnp.concatenate([before, signal], axis=0).astype(jnp.float32)
    conv_taps = weights.astype(jnp.float32)
    summed = jnp.zeros(signal.shape, jnp.float32)
    for offset in range(conv_taps.shape[0]):
        summed = summed + conv_taps[offset] * padded[offset : offset + length]
    return jax.nn.silu(summed)


def unit_lower_inverse(system):
    size = system.shape[-1]
    rows = jnp.arange(size)[:, None]
    cols = jnp.arange(size)[None, :]
    inverse = jnp.broadcast_to(jnp.eye(size, dtype=system.dtype), system.shape)
    width = 1
    while width < size:
        same_block = (rows // (2 * width)) == (cols // (2 * width))
        lower_half = (rows // width) > (cols // width)
        coupling = jnp.where(same_block & lower_half, system, 0.0)
        correction = jnp.einsum(
            "...ij,...jk->...ik",
            jnp.einsum("...ij,...jk->...ik", inverse, coupling, precision=highest),
            inverse,
            precision=highest,
        )
        inverse = jnp.where(same_block & lower_half, -correction, inverse)
        width *= 2
    return inverse


def apply_map(matrix, state_now):
    return jnp.einsum("hrke,hrev->hrkv", matrix, state_now, precision=highest)


def recurrence(query_blocks, key_blocks, value_blocks, strength_blocks, decay_blocks):
    key_heads, ratio_heads = value_blocks.shape[:2]
    cumulative = jnp.cumsum(decay_blocks, axis=-1)
    positions = jnp.arange(SPAN)
    inclusive = positions[:, None] >= positions[None, :]
    strictly = positions[:, None] > positions[None, :]
    log_gaps = cumulative[..., :, None] - cumulative[..., None, :]
    decays = jnp.where(inclusive, jnp.exp(jnp.where(inclusive, log_gaps, 0.0)), 0.0)
    key_key = jnp.einsum("hxnck,hxnek->hxnce", key_blocks, key_blocks, precision=highest)
    query_key = jnp.einsum("hxnck,hxnek->hxnce", query_blocks, key_blocks, precision=highest)
    lower_part = jnp.where(strictly, strength_blocks[..., None] * decays * key_key, 0.0)
    system = lower_part + jnp.eye(SPAN, dtype=jnp.float32)
    right_side = jnp.concatenate(
        [
            strength_blocks[..., None] * value_blocks,
            (strength_blocks * jnp.exp(cumulative))[..., None] * key_blocks,
        ],
        axis=-1,
    )
    solved = jnp.einsum(
        "...ij,...jk->...ik", unit_lower_inverse(system), right_side, precision=highest
    )
    value_part = solved[..., :DV]
    key_part = solved[..., DV:]
    attention = decays * query_key
    local_out = jnp.einsum("hrnce,hrnev->hrncv", attention, value_part, precision=highest)
    coupling = jnp.exp(cumulative)[..., None] * query_blocks - jnp.einsum(
        "hrnce,hrnek->hrnck", attention, key_part, precision=highest
    )
    span_end = cumulative[..., -1:]
    scaled_keys = jnp.exp(span_end - cumulative)[..., None] * key_blocks
    transit = jnp.exp(span_end)[..., None] * jnp.eye(DK, dtype=jnp.float32) - jnp.einsum(
        "hrnck,hrnce->hrnke", scaled_keys, key_part, precision=highest
    )
    inject = jnp.einsum("hrnck,hrncv->hrnkv", scaled_keys, value_part, precision=highest)
    transit_seq = jnp.moveaxis(transit, 2, 0)
    inject_seq = jnp.moveaxis(inject, 2, 0)
    identity = jnp.broadcast_to(jnp.eye(DK, dtype=jnp.float32), (key_heads, ratio_heads, DK, DK))
    zero_state = jnp.zeros((key_heads, ratio_heads, DK, DV), jnp.float32)

    def sweep_spans(carried, span_in):
        prefix, state_now = carried
        transit_now, inject_now = span_in
        return (
            (apply_map(transit_now, prefix), apply_map(transit_now, state_now) + inject_now),
            None,
        )

    (total_map, local_end), ignored = lax.scan(
        sweep_spans, (identity, zero_state), (transit_seq, inject_seq)
    )

    seq_size = lax.axis_size("seq")
    seq_index = lax.axis_index("seq")
    prefix_map, prefix_end = total_map, local_end
    distance = 1
    while distance < seq_size:
        if 2 * distance < seq_size:
            earlier_map, earlier_end = shifted(
                jnp.stack([prefix_map, prefix_end]), "seq", distance
            )
            prefix_end = apply_map(prefix_map, earlier_end) + prefix_end
            prefix_map = jnp.where(
                seq_index >= distance, apply_map(prefix_map, earlier_map), prefix_map
            )
        else:
            earlier_end = shifted(prefix_end, "seq", distance)
            prefix_end = apply_map(prefix_map, earlier_end) + prefix_end
        distance *= 2
    incoming = shifted(prefix_end, "seq", 1)

    def replay(state_now, span_in):
        transit_now, inject_now, coupling_now, local_now = span_in
        span_out = (
            jnp.einsum("hrck,hrkv->hrcv", coupling_now, state_now, precision=highest) + local_now
        )
        return (apply_map(transit_now, state_now) + inject_now, span_out)

    ignored_state, outputs = lax.scan(
        replay,
        incoming,
        (transit_seq, inject_seq, jnp.moveaxis(coupling, 2, 0), jnp.moveaxis(local_out, 2, 0)),
    )
    return outputs


def shards(
    query_proj,
    key_proj,
    value_proj,
    gate_proj,
    strength,
    log_decay,
    conv_query,
    conv_key,
    conv_value,
    norm_gain,
    out_weight,
):
    local_rows = query_proj.shape[0]
    rim_width = conv_query.shape[0] - 1
    before_query, before_key, before_value = shifted(
        (
            query_proj[local_rows - rim_width :],
            key_proj[local_rows - rim_width :],
            value_proj[local_rows - rim_width :],
        ),
        "seq",
        1,
    )
    key_heads = key_proj.shape[1] // DK
    value_heads = value_proj.shape[1] // DV
    ratio_heads = value_heads // key_heads
    spans = local_rows // SPAN
    queries = conv_silu(query_proj, before_query, conv_query)
    key_rows = conv_silu(key_proj, before_key, conv_key).reshape(local_rows, key_heads, DK)
    key_rows = key_rows / jnp.sqrt(jnp.sum(key_rows * key_rows, axis=-1, keepdims=True) + epsilon)
    values = conv_silu(value_proj, before_value, conv_value)
    query_blocks = queries.reshape(spans, SPAN, key_heads, DK).transpose(2, 0, 1, 3)[:, None]
    key_blocks = key_rows.reshape(spans, SPAN, key_heads, DK).transpose(2, 0, 1, 3)[:, None]
    value_blocks = values.reshape(spans, SPAN, key_heads, ratio_heads, DV).transpose(2, 3, 0, 1, 4)
    strength_blocks = strength.reshape(key_heads, ratio_heads, spans, SPAN)
    decay_blocks = log_decay.reshape(key_heads, ratio_heads, spans, SPAN)
    parts = [
        recurrence(
            query_blocks[group : group + 1],
            key_blocks[group : group + 1],
            value_blocks[group : group + 1],
            strength_blocks[group : group + 1],
            decay_blocks[group : group + 1],
        )
        for group in range(key_heads)
    ]
    outputs = jnp.concatenate(parts, axis=1)
    core_out = jnp.moveaxis(outputs, 0, 2)
    core_out = core_out.transpose(2, 3, 0, 1, 4).reshape(local_rows, value_heads, DV)
    gate_values = gate_proj.astype(jnp.float32).reshape(local_rows, value_heads, DV)
    scale_rows = lax.rsqrt(jnp.mean(core_out * core_out, axis=-1, keepdims=True) + epsilon)
    normed = core_out * scale_rows * norm_gain.astype(jnp.float32) * jax.nn.silu(gate_values)
    hidden = normed.reshape(local_rows, value_heads * DV).astype(jnp.bfloat16)
    partial_sum = jnp.dot(hidden, out_weight, preferred_element_type=jnp.float32).astype(
        jnp.bfloat16
    )
    head_size = lax.axis_size("head")
    pieces = lax.all_to_all(
        partial_sum.reshape(head_size, local_rows // head_size, partial_sum.shape[1]),
        "head",
        0,
        0,
    )
    return jnp.sum(pieces.astype(jnp.float32), axis=0).astype(jnp.bfloat16)


def solution(mesh):
    placed = (
        P("seq", "head"),
        P("seq", "head"),
        P("seq", "head"),
        P("seq", "head"),
        P("head", "seq"),
        P("head", "seq"),
        P(None, "head"),
        P(None, "head"),
        P(None, "head"),
        P(),
        P("head", None),
    )
    return jax.shard_map(
        shards, mesh=mesh, in_specs=placed, out_specs=P(("seq", "head"), None), check_vma=False
    )
```

time: 202 us -> 189 us (0.936)
  the two profiles are of different devices: /device:TPU:192 before, /device:TPU:128 now
where the time goes in v4:
time: 189 us; the launch traced here: 187 us
  matrix products  50.8 us (27%)
  waiting for transfers between devices  42.5 us (22%)
  starting transfers between devices  42.2 us (22%)
  blocking collectives  20.1 us (11%)
  local copies, waits for them, and re-layouts  17.9 us (9%)
  other arithmetic  12.1 us (6%)
    ppermute x15, waiting for transfers between devices, shifted(): return lax.ppermute(array, axis, pairs)  42.5 us
    ppermute x15, starting transfers between devices, shifted(): return lax.ppermute(array, axis, pairs)  42.2 us
    all_to_all x1, blocking collectives, shards(): lax.all_to_all(partial_sum.reshape(head_size, local_rows // head_size, pa...  20.1 us
    dot_general x30, matrix products, apply_map(): return jnp.einsum('hrke,hrev->hrkv', matrix, state_now, precision=highest)  11.1 us
    dot_general x14, matrix products, unit_lower_inverse(): jnp.einsum('...ij,...jk->...ik', inverse, coupling, precision=highest)  9.13 us
    dot_general x14, matrix products, unit_lower_inverse(): jnp.einsum('...ij,...jk->...ik', jnp.einsum('...ij,...jk->...ik', inverse...  7.67 us
    dot_general x4, matrix products, replay(): jnp.einsum('hrck,hrkv->hrcv', coupling_now, state_now, precision=highest)  6.33 us
    dot_general x2, matrix products, recurrence(): jnp.einsum('hrnce,hrnek->hrnck', attention, key_part, precision=highest)  4.51 us
  transfers between devices with their start and end apart: 15, of which 7 were waited for; matrix products, arithmetic and copies ran while one was open for 36% of the time, Pallas kernels for 0%

profile of v4, /device:TPU:128, one launch (start us, length us, event | category | flops | bytes accessed | tf_op | source)
XLA Modules:
  0.0 187.2 jit_solution(5872770656187034537)
XLA Ops:
  0.8 3.5 %collective-permute-start = (bf16[3,256]{1,0:T(4,128)(2,1)S(1)}, bf16[3,256]{1,0:T(4,128)(2,1)S(1)}, u32[]{:S(2)}, u32[]{:S(2)}) collective-permute-start(bf16[3,256]{1,0:T(4,128)(2,1)S(1)} %slice.145), channel_id=1, source_target_pairs={{0,8},{8,16},{16,24},{24,32},{32,40},{40,48},{48,56},{56,64},{64,7... | collective-permute-start | bytes 4616 | tf_op jit(solution)/shard_map/ppermute | solution.py:18
  5.6 3.5 %collective-permute-start.1 = (bf16[3,512]{1,0:T(4,128)(2,1)}, bf16[3,512]{1,0:T(4,128)(2,1)}, u32[]{:S(2)}, u32[]{:S(2)}) collective-permute-start(bf16[3,512]{1,0:T(4,128)(2,1)} %slice.156), channel_id=1, source_target_pairs={{0,8},{8,16},{16,24},{24,32},{32,40},{40,48},{48,56},{56,64},{64,7... | collective-permute-start | bytes 9224 | tf_op jit(solution)/shard_map/ppermute | solution.py:18
  9.8 3.2 %collective-permute-start.8 = (bf16[3,256]{1,0:T(4,128)(2,1)S(1)}, bf16[3,256]{1,0:T(4,128)(2,1)S(1)}, u32[]{:S(2)}, u32[]{:S(2)}) collective-permute-start(bf16[3,256]{1,0:T(4,128)(2,1)S(1)} %slice.168), channel_id=1, source_target_pairs={{0,8},{8,16},{16,24},{24,32},{32,40},{40,48},{48,56},{56,64},{64,7... | collective-permute-start | bytes 4616 | tf_op jit(solution)/shard_map/ppermute | solution.py:18
  55.5 2.6 %collective-permute-start.9 = (f32[2,1,2,128,128]{4,3,2,1,0:T(8,128)}, f32[2,1,2,128,128]{4,3,2,1,0:T(8,128)}, u32[]{:S(2)}, u32[]{:S(2)}) collective-permute-start(f32[2,1,2,128,128]{4,3,2,1,0:T(8,128)} %pad_maximum_fusion.4), channel_id=1, source_target_pairs={{0,8},{8,16},{16,24},{24,32},{32,40},{40,48},{48,56},{56,64},{64,7... | collective-permute-start | bytes 786440 | tf_op jit(solution)/shard_map/ppermute | solution.py:18
  63.3 4.2 %while.48 = (s32[]{:T(128)}, f32[1,2,128,128]{3,2,1,0:T(8,128)S(1)}, f32[1,2,128,128]{3,2,1,0:T(8,128)}, f32[2,1,2,128,128]{4,3,2,1,0:T(8,128)S(1)}, f32[2,1,2,128,128]{4,3,2,1,0:T(8,128)S(1)}, /*index=5*/s32[]{:T(128)}) while((s32[]{:T(128)}, f32[1,2,128,128]{3,2,1,0:T(8,128)S(1)}, f32[1,2,128,128]{3,2,1,0:T(8,128)}, ...), condition=%wide.region_3.4_spmd, body=%wide.region_2.3_spmd.sunk | while | flops 100696064 | bytes 1442897 | solution.py:104
  68.6 3.5 %collective-permute-start.2 = (f32[2,1,2,128,128]{4,3,2,1,0:T(8,128)S(1)}, f32[2,1,2,128,128]{4,3,2,1,0:T(8,128)S(1)}, u32[]{:S(2)}, u32[]{:S(2)}) collective-permute-start(f32[2,1,2,128,128]{4,3,2,1,0:T(8,128)S(1)} %pad_maximum_fusion), channel_id=1, source_target_pairs={{0,8},{8,16},{16,24},{24,32},{32,40},{40,48},{48,56},{56,64},{64,7... | collective-permute-start | bytes 786440 | tf_op jit(solution)/shard_map/ppermute | solution.py:18
  72.0 2.3 %fusion.40 = f32[2,1,2,128,128]{4,3,0,2,1:T(8,128)} fusion(f32[1,2,2,128,256]{4,3,2,1,0:T(8,128)} %copy-done.4, f32[2,128,128]{2,1,0:T(8,128)} %fusion.339, f32[2,128,128]{2,1,0:T(8,128)} %get-tuple-element.270, f32[2,2,128]{2,1,0:T(2,128)} %get-tuple-element.284, f32[2,2,128]{2,1,0:T(2,128)} %bitcast.532, pred[128,128]{1,0:T(8,128)(4,1)S(1)} %get-tuple-element.308), kind=kOutput, calls=%fused_computation.53 | convolution fusion | flops 101056512 | bytes 808960 | tf_op jit(solution)/shard_map/hrnce,hrnek->hrnck/dot_general | solution.py:82
  74.3 2.2 %convolution_bitcast_fusion.4 = f32[2,1,2,128,128]{4,3,0,2,1:T(8,128)} fusion(f32[1,2,2,128,256]{4,3,2,1,0:T(8,128)} %copy-done.4, f32[2,128,128]{2,1,0:T(8,128)} %fusion.339, f32[2,2,128]{2,1,0:T(2,128)} %bitcast.533, pred[128,128]{1,0:T(8,128)(4,1)S(1)} %get-tuple-element.308), kind=kOutput, calls=%fused_computation.51 | convolution fusion | flops 100925440 | bytes 675840 | tf_op jit(solution)/shard_map/hrnce,hrnev->hrncv/dot_general | solution.py:81
  76.5 2.3 %fusion.49 = f32[2,1,2,128,128]{4,3,0,2,1:T(8,128)} fusion(f32[1,2,2,128,256]{4,3,2,1,0:T(8,128)} %copy-done.2, f32[2,128,128]{2,1,0:T(8,128)} %fusion.338, f32[2,128,128]{2,1,0:T(8,128)} %get-tuple-element.269, f32[2,2,128]{2,1,0:T(2,128)} %get-tuple-element.281, f32[2,2,128]{2,1,0:T(2,128)} %bitcast.521, pred[128,128]{1,0:T(8,128)(4,1)S(1)} %get-tuple-element.308), kind=kOutput, calls=%fused_computation.73 | convolution fusion | flops 101056512 | bytes 808960 | tf_op jit(solution)/shard_map/hrnce,hrnek->hrnck/dot_general | solution.py:82
  81.2 4.8 %collective-permute-start.10 = (f32[2,1,2,128,128]{4,3,2,1,0:T(8,128)S(1)}, f32[2,1,2,128,128]{4,3,2,1,0:T(8,128)S(1)}, u32[]{:S(2)}, u32[]{:S(2)}) collective-permute-start(f32[2,1,2,128,128]{4,3,2,1,0:T(8,128)S(1)} %pad_maximum_fusion.5), channel_id=1, source_target_pairs={{0,16},{8,24},{16,32},{24,40},{32,48},{40,56},{48,64},{56,72},{64,... | collective-permute-start | bytes 786440 | tf_op jit(solution)/shard_map/ppermute | solution.py:18
  86.6 3.0 %collective-permute-start.3 = (f32[2,1,2,128,128]{4,3,2,1,0:T(8,128)S(1)}, f32[2,1,2,128,128]{4,3,2,1,0:T(8,128)S(1)}, u32[]{:S(2)}, u32[]{:S(2)}) collective-permute-start(f32[2,1,2,128,128]{4,3,2,1,0:T(8,128)S(1)} %pad_maximum_fusion.1), channel_id=1, source_target_pairs={{0,16},{8,24},{16,32},{24,40},{32,48},{40,56},{48,64},{56,72},{64,... | collective-permute-start | bytes 786440 | tf_op jit(solution)/shard_map/ppermute | solution.py:18
  89.6 4.2 %collective-permute-done.10 = f32[2,1,2,128,128]{4,3,2,1,0:T(8,128)S(1)} collective-permute-done((f32[2,1,2,128,128]{4,3,2,1,0:T(8,128)S(1)}, f32[2,1,2,128,128]{4,3,2,1,0:T(8,128)S(1)}, u32[]{:S(2)}, u32[]{:S(2)}) %collective-permute-start.10) | collective-permute-done | bytes 262176 | tf_op jit(solution)/shard_map/ppermute | solution.py:18
  96.5 3.8 %collective-permute-done.3 = f32[2,1,2,128,128]{4,3,2,1,0:T(8,128)S(1)} collective-permute-done((f32[2,1,2,128,128]{4,3,2,1,0:T(8,128)S(1)}, f32[2,1,2,128,128]{4,3,2,1,0:T(8,128)S(1)}, u32[]{:S(2)}, u32[]{:S(2)}) %collective-permute-start.3) | collective-permute-done | bytes 262176 | tf_op jit(solution)/shard_map/ppermute | solution.py:18
  102.8 2.2 %collective-permute-done.11 = f32[2,1,2,128,128]{4,3,2,1,0:T(8,128)S(1)} collective-permute-done((f32[2,1,2,128,128]{4,3,2,1,0:T(8,128)S(1)}, f32[2,1,2,128,128]{4,3,2,1,0:T(8,128)S(1)}, u32[]{:S(2)}, u32[]{:S(2)}) %collective-permute-start.11) | collective-permute-done | bytes 262176 | tf_op jit(solution)/shard_map/ppermute | solution.py:18
  105.6 2.2 %collective-permute-start.12 = (f32[2,1,2,128,128]{4,3,2,1,0:T(8,128)S(1)}, f32[2,1,2,128,128]{4,3,2,1,0:T(8,128)S(1)}, u32[]{:S(2)}, u32[]{:S(2)}) collective-permute-start(f32[2,1,2,128,128]{4,3,2,1,0:T(8,128)S(1)} %pad_maximum_fusion.7), channel_id=1, source_target_pairs={{0,64},{8,72},{16,80},{24,88},{32,96},{40,104},{48,112},{56,120},{... | collective-permute-start | bytes 786440 | tf_op jit(solution)/shard_map/ppermute | solution.py:18
  107.9 11.4 %collective-permute-done.4 = f32[2,1,2,128,128]{4,3,2,1,0:T(8,128)S(1)} collective-permute-done((f32[2,1,2,128,128]{4,3,2,1,0:T(8,128)S(1)}, f32[2,1,2,128,128]{4,3,2,1,0:T(8,128)S(1)}, u32[]{:S(2)}, u32[]{:S(2)}) %collective-permute-start.4) | collective-permute-done | bytes 262176 | tf_op jit(solution)/shard_map/ppermute | solution.py:18
  119.8 3.1 %collective-permute-start.5 = (f32[2,1,2,128,128]{4,3,2,1,0:T(8,128)S(1)}, f32[2,1,2,128,128]{4,3,2,1,0:T(8,128)S(1)}, u32[]{:S(2)}, u32[]{:S(2)}) collective-permute-start(f32[2,1,2,128,128]{4,3,2,1,0:T(8,128)S(1)} %pad_maximum_fusion.3), channel_id=1, source_target_pairs={{0,64},{8,72},{16,80},{24,88},{32,96},{40,104},{48,112},{56,120},{... | collective-permute-start | bytes 786440 | tf_op jit(solution)/shard_map/ppermute | solution.py:18
  125.7 13.4 %collective-permute-done.5 = f32[2,1,2,128,128]{4,3,2,1,0:T(8,128)S(1)} collective-permute-done((f32[2,1,2,128,128]{4,3,2,1,0:T(8,128)S(1)}, f32[2,1,2,128,128]{4,3,2,1,0:T(8,128)S(1)}, u32[]{:S(2)}, u32[]{:S(2)}) %collective-permute-start.5) | collective-permute-done | bytes 262176 | tf_op jit(solution)/shard_map/ppermute | solution.py:18
  141.6 3.1 %collective-permute-start.14 = (f32[1,2,128,128]{3,2,1,0:T(8,128)S(1)}, f32[1,2,128,128]{3,2,1,0:T(8,128)S(1)}, u32[]{:S(2)}, u32[]{:S(2)}) collective-permute-start(f32[1,2,128,128]{3,2,1,0:T(8,128)S(1)} %fusion.67), channel_id=1, source_target_pairs={{0,8},{8,16},{16,24},{24,32},{32,40},{40,48},{48,56},{56,64},{64,7... | collective-permute-start | bytes 393224 | tf_op jit(solution)/shard_map/ppermute | solution.py:18
  144.7 5.5 %collective-permute-done.6 = f32[1,2,128,128]{3,2,1,0:T(8,128)S(1)} collective-permute-done((f32[1,2,128,128]{3,2,1,0:T(8,128)S(1)}, f32[1,2,128,128]{3,2,1,0:T(8,128)S(1)}, u32[]{:S(2)}, u32[]{:S(2)}) %collective-permute-start.6) | collective-permute-done | bytes 131104 | tf_op jit(solution)/shard_map/ppermute | solution.py:18
  150.5 3.1 %collective-permute-start.7 = (f32[1,2,128,128]{3,2,1,0:T(8,128)S(1)}, f32[1,2,128,128]{3,2,1,0:T(8,128)S(1)}, u32[]{:S(2)}, u32[]{:S(2)}) collective-permute-start(f32[1,2,128,128]{3,2,1,0:T(8,128)S(1)} %fusion.62), channel_id=1, source_target_pairs={{0,8},{8,16},{16,24},{24,32},{32,40},{40,48},{48,56},{56,64},{64,7... | collective-permute-start | bytes 393224 | tf_op jit(solution)/shard_map/ppermute | solution.py:18
  154.4 4.4 %while.51 = (s32[]{:T(128)}, f32[1,2,128,128]{3,2,1,0:T(8,128)S(1)}, f32[2,1,2,128,128]{4,3,2,1,0:T(8,128)}, f32[2,1,2,128,128]{4,3,2,1,0:T(8,128)S(1)}, f32[2,1...) while((s32[]{:T(128)}, ...), condition=%wide.region_10.11_spmd, body=%wide.region_9.10_spmd.sunk | while | flops 100728832 | bytes 1312861 | solution.py:134
  160.7 3.2 %while.49 = (s32[]{:T(128)}, f32[1,2,128,128]{3,2,1,0:T(8,128)S(1)}, f32[2,1,2,128,128]{4,3,2,1,0:T(8,128)S(1)}, f32[2,1,2,128,128]{4,3,2,1,0:T(8,128)S(1)}, f32...) while((s32[]{:T(128)}, ...), condition=%wide.region_5.6_spmd, body=%wide.region_4.5_spmd.sunk | while | flops 100728832 | bytes 1312861 | solution.py:134
  166.3 20.1 %all_to_all.5 = bf16[8,32,2048]{2,1,0:T(8,128)(2,1)S(1)} all-to-all(bf16[8,32,2048]{2,1,0:T(8,128)(2,1)S(1)} %bitcast.518), channel_id=1, replica_groups=mesh['seq'=32,'head'=8] {'head'}, dimensions={0} | all-to-all | bytes 2097152 | tf_op jit(solution)/shard_map/all_to_all | solution.py:200
  (261 shorter events, 83.7 us)
Async XLA Ops:
  0.0 165.5 %copy-start = (bf16[512,2048]{1,0:T(8,128)(2,1)S(1)}, bf16[512,2048]{1,0:T(8,128)(2,1)}, u32[]{:S(2)}) copy-start(bf16[512,2048]{1,0:T(8,128)(2,1)} %param.29) | copy-start | bytes 6291460
  0.8 23.1 %collective-permute-start = (bf16[3,256]{1,0:T(4,128)(2,1)S(1)}, bf16[3,256]{1,0:T(4,128)(2,1)S(1)}, u32[]{:S(2)}, u32[]{:S(2)}) collective-permute-start(bf16[3,256]{1,0:T(4,128)(2,1)S(1)} %slice.145), channel_id=1, source_target_pairs={{0,8},{8,16},{16,24},{24,32},{32,40},{40,48},{48,56},{56,64},{64,7... | collective-permute-start | bytes 4616 | tf_op jit(solution)/shard_map/ppermute | solution.py:18
  5.6 43.5 %collective-permute-start.1 = (bf16[3,512]{1,0:T(4,128)(2,1)}, bf16[3,512]{1,0:T(4,128)(2,1)}, u32[]{:S(2)}, u32[]{:S(2)}) collective-permute-start(bf16[3,512]{1,0:T(4,128)(2,1)} %slice.156), channel_id=1, source_target_pairs={{0,8},{8,16},{16,24},{24,32},{32,40},{40,48},{48,56},{56,64},{64,7... | collective-permute-start | bytes 9224 | tf_op jit(solution)/shard_map/ppermute | solution.py:18
  9.8 16.6 %collective-permute-start.8 = (bf16[3,256]{1,0:T(4,128)(2,1)S(1)}, bf16[3,256]{1,0:T(4,128)(2,1)S(1)}, u32[]{:S(2)}, u32[]{:S(2)}) collective-permute-start(bf16[3,256]{1,0:T(4,128)(2,1)S(1)} %slice.168), channel_id=1, source_target_pairs={{0,8},{8,16},{16,24},{24,32},{32,40},{40,48},{48,56},{56,64},{64,7... | collective-permute-start | bytes 4616 | tf_op jit(solution)/shard_map/ppermute | solution.py:18
  13.0 48.3 %copy-start.5 = (f32[128,128]{1,0:T(8,128)}, f32[128,128]{1,0:T(8,128)S(1)}, u32[]{:S(2)}) copy-start(f32[128,128]{1,0:T(8,128)S(1)} %fusion.313) | copy-start | bytes 196612
  13.0 16.0 %copy-start.31 = (pred[128,128]{1,0:T(8,128)(4,1)}, pred[128,128]{1,0:T(8,128)(4,1)S(1)}, u32[]{:S(2)}) copy-start(pred[128,128]{1,0:T(8,128)(4,1)S(1)} %get-tuple-element.309) | copy-start | bytes 49156
  15.5 13.5 %copy-start.25 = (f32[2,2,128]{2,1,0:T(2,128)}, f32[2,2,128]{2,1,0:T(2,128)S(1)}, u32[]{:S(2)}) copy-start(f32[2,2,128]{2,1,0:T(2,128)S(1)} %mul.561) | copy-start | bytes 6148
  16.1 12.9 %copy-start.21 = (f32[1,2,2,128]{3,2,1,0:T(2,128)}, f32[1,2,2,128]{3,2,1,0:T(2,128)S(1)}, u32[]{:S(2)}) copy-start(f32[1,2,2,128]{3,2,1,0:T(2,128)S(1)} %reduce_window_sum.23) | copy-start | bytes 6148
  55.5 23.3 %collective-permute-start.9 = (f32[2,1,2,128,128]{4,3,2,1,0:T(8,128)}, f32[2,1,2,128,128]{4,3,2,1,0:T(8,128)}, u32[]{:S(2)}, u32[]{:S(2)}) collective-permute-start(f32[2,1,2,128,128]{4,3,2,1,0:T(8,128)} %pad_maximum_fusion.4), channel_id=1, source_target_pairs={{0,8},{8,16},{16,24},{24,32},{32,40},{40,48},{48,56},{56,64},{64,7... | collective-permute-start | bytes 786440 | tf_op jit(solution)/shard_map/ppermute | solution.py:18
  67.6 18.4 %copy-start.1 = (f32[1,2,128,128]{3,2,1,0:T(8,128)S(1)}, f32[1,2,128,128]{3,2,1,0:T(8,128)}, u32[]{:S(2)}) copy-start(f32[1,2,128,128]{3,2,1,0:T(8,128)} %get-tuple-element.136) | copy-start | bytes 393220
  68.6 17.4 %collective-permute-start.2 = (f32[2,1,2,128,128]{4,3,2,1,0:T(8,128)S(1)}, f32[2,1,2,128,128]{4,3,2,1,0:T(8,128)S(1)}, u32[]{:S(2)}, u32[]{:S(2)}) collective-permute-start(f32[2,1,2,128,128]{4,3,2,1,0:T(8,128)S(1)} %pad_maximum_fusion), channel_id=1, source_target_pairs={{0,8},{8,16},{16,24},{24,32},{32,40},{40,48},{48,56},{56,64},{64,7... | collective-permute-start | bytes 786440 | tf_op jit(solution)/shard_map/ppermute | solution.py:18
  81.2 12.6 %collective-permute-start.10 = (f32[2,1,2,128,128]{4,3,2,1,0:T(8,128)S(1)}, f32[2,1,2,128,128]{4,3,2,1,0:T(8,128)S(1)}, u32[]{:S(2)}, u32[]{:S(2)}) collective-permute-start(f32[2,1,2,128,128]{4,3,2,1,0:T(8,128)S(1)} %pad_maximum_fusion.5), channel_id=1, source_target_pairs={{0,16},{8,24},{16,32},{24,40},{32,48},{40,56},{48,64},{56,72},{64,... | collective-permute-start | bytes 786440 | tf_op jit(solution)/shard_map/ppermute | solution.py:18
  86.6 13.7 %collective-permute-start.3 = (f32[2,1,2,128,128]{4,3,2,1,0:T(8,128)S(1)}, f32[2,1,2,128,128]{4,3,2,1,0:T(8,128)S(1)}, u32[]{:S(2)}, u32[]{:S(2)}) collective-permute-start(f32[2,1,2,128,128]{4,3,2,1,0:T(8,128)S(1)} %pad_maximum_fusion.1), channel_id=1, source_target_pairs={{0,16},{8,24},{16,32},{24,40},{32,48},{40,56},{48,64},{56,72},{64,... | collective-permute-start | bytes 786440 | tf_op jit(solution)/shard_map/ppermute | solution.py:18
  94.4 28.6 %copy-start.3 = (f32[1,2,2,128,256]{4,3,2,1,0:T(8,128)S(1)}, f32[1,2,2,128,256]{4,3,2,1,0:T(8,128)}, u32[]{:S(2)}) copy-start(f32[1,2,2,128,256]{4,3,2,1,0:T(8,128)} %copy-done.2) | copy-start | bytes 1572868
  94.4 28.6 %copy-start.7 = (f32[2,128,128]{2,1,0:T(8,128)S(1)}, f32[2,128,128]{2,1,0:T(8,128)}, u32[]{:S(2)}) copy-start(f32[2,128,128]{2,1,0:T(8,128)} %fusion.338) | copy-start | bytes 393220
  94.4 28.6 %copy-start.20 = (f32[1,2,2,128]{3,2,1,0:T(2,128)S(1)}, f32[1,2,2,128]{3,2,1,0:T(2,128)}, u32[]{:S(2)}) copy-start(f32[1,2,2,128]{3,2,1,0:T(2,128)} %copy-done.18) | copy-start | bytes 6148
  94.4 10.6 %collective-permute-start.11 = (f32[2,1,2,128,128]{4,3,2,1,0:T(8,128)S(1)}, f32[2,1,2,128,128]{4,3,2,1,0:T(8,128)S(1)}, u32[]{:S(2)}, u32[]{:S(2)}) collective-permute-start(f32[2,1,2,128,128]{4,3,2,1,0:T(8,128)S(1)} %pad_maximum_fusion.6), channel_id=1, source_target_pairs={{0,32},{8,40},{16,48},{24,56},{32,64},{40,72},{48,80},{56,88},{64,... | collective-permute-start | bytes 786440 | tf_op jit(solution)/shard_map/ppermute | solution.py:18
  100.9 18.4 %collective-permute-start.4 = (f32[2,1,2,128,128]{4,3,2,1,0:T(8,128)S(1)}, f32[2,1,2,128,128]{4,3,2,1,0:T(8,128)S(1)}, u32[]{:S(2)}, u32[]{:S(2)}) collective-permute-start(f32[2,1,2,128,128]{4,3,2,1,0:T(8,128)S(1)} %pad_maximum_fusion.2), channel_id=1, source_target_pairs={{0,32},{8,40},{16,48},{24,56},{32,64},{40,72},{48,80},{56,88},{64,... | collective-permute-start | bytes 786440 | tf_op jit(solution)/shard_map/ppermute | solution.py:18
  105.6 18.6 %collective-permute-start.12 = (f32[2,1,2,128,128]{4,3,2,1,0:T(8,128)S(1)}, f32[2,1,2,128,128]{4,3,2,1,0:T(8,128)S(1)}, u32[]{:S(2)}, u32[]{:S(2)}) collective-permute-start(f32[2,1,2,128,128]{4,3,2,1,0:T(8,128)S(1)} %pad_maximum_fusion.7), channel_id=1, source_target_pairs={{0,64},{8,72},{16,80},{24,88},{32,96},{40,104},{48,112},{56,120},{... | collective-permute-start | bytes 786440 | tf_op jit(solution)/shard_map/ppermute | solution.py:18
  119.8 19.3 %collective-permute-start.5 = (f32[2,1,2,128,128]{4,3,2,1,0:T(8,128)S(1)}, f32[2,1,2,128,128]{4,3,2,1,0:T(8,128)S(1)}, u32[]{:S(2)}, u32[]{:S(2)}) collective-permute-start(f32[2,1,2,128,128]{4,3,2,1,0:T(8,128)S(1)} %pad_maximum_fusion.3), channel_id=1, source_target_pairs={{0,64},{8,72},{16,80},{24,88},{32,96},{40,104},{48,112},{56,120},{... | collective-permute-start | bytes 786440 | tf_op jit(solution)/shard_map/ppermute | solution.py:18
  124.4 16.9 %collective-permute-start.13 = (f32[1,2,128,128]{3,2,1,0:T(8,128)S(1)}, f32[1,2,128,128]{3,2,1,0:T(8,128)S(1)}, u32[]{:S(2)}, u32[]{:S(2)}) collective-permute-start(f32[1,2,128,128]{3,2,1,0:T(8,128)S(1)} %fusion.66), channel_id=1, source_target_pairs={{0,128},{8,136},{16,144},{24,152},{32,160},{40,168},{48,176},{56,1... | collective-permute-start | bytes 393224 | tf_op jit(solution)/shard_map/ppermute | solution.py:18
  139.5 10.8 %collective-permute-start.6 = (f32[1,2,128,128]{3,2,1,0:T(8,128)S(1)}, f32[1,2,128,128]{3,2,1,0:T(8,128)S(1)}, u32[]{:S(2)}, u32[]{:S(2)}) collective-permute-start(f32[1,2,128,128]{3,2,1,0:T(8,128)S(1)} %fusion.61), channel_id=1, source_target_pairs={{0,128},{8,136},{16,144},{24,152},{32,160},{40,168},{48,176},{56,1... | collective-permute-start | bytes 393224 | tf_op jit(solution)/shard_map/ppermute | solution.py:18
  141.6 12.1 %collective-permute-start.14 = (f32[1,2,128,128]{3,2,1,0:T(8,128)S(1)}, f32[1,2,128,128]{3,2,1,0:T(8,128)S(1)}, u32[]{:S(2)}, u32[]{:S(2)}) collective-permute-start(f32[1,2,128,128]{3,2,1,0:T(8,128)S(1)} %fusion.67), channel_id=1, source_target_pairs={{0,8},{8,16},{16,24},{24,32},{32,40},{40,48},{48,56},{56,64},{64,7... | collective-permute-start | bytes 393224 | tf_op jit(solution)/shard_map/ppermute | solution.py:18
  150.5 10.2 %collective-permute-start.7 = (f32[1,2,128,128]{3,2,1,0:T(8,128)S(1)}, f32[1,2,128,128]{3,2,1,0:T(8,128)S(1)}, u32[]{:S(2)}, u32[]{:S(2)}) collective-permute-start(f32[1,2,128,128]{3,2,1,0:T(8,128)S(1)} %fusion.62), channel_id=1, source_target_pairs={{0,8},{8,16},{16,24},{24,32},{32,40},{40,48},{48,56},{56,64},{64,7... | collective-permute-start | bytes 393224 | tf_op jit(solution)/shard_map/ppermute | solution.py:18
  (34 other events, 115.1 us)

commit v5 on v4

--- a/solution.py
+++ b/solution.py
@@ -112,17 +112,19 @@
     while distance < seq_size:
         if 2 * distance < seq_size:
             earlier_map, earlier_end = shifted(
-                jnp.stack([prefix_map, prefix_end]), "seq", distance
-            )
+                jnp.stack([prefix_map, prefix_end]).astype(jnp.bfloat16), "seq", distance
+            ).astype(jnp.float32)
             prefix_end = apply_map(prefix_map, earlier_end) + prefix_end
             prefix_map = jnp.where(
                 seq_index >= distance, apply_map(prefix_map, earlier_map), prefix_map
             )
         else:
-            earlier_end = shifted(prefix_end, "seq", distance)
+            earlier_end = shifted(prefix_end.astype(jnp.bfloat16), "seq", distance).astype(
+                jnp.float32
+            )
             prefix_end = apply_map(prefix_map, earlier_end) + prefix_end
         distance *= 2
-    incoming = shifted(prefix_end, "seq", 1)
+    incoming = shifted(prefix_end.astype(jnp.bfloat16), "seq", 1).astype(jnp.float32)
 
     def replay(state_now, span_in):
         transit_now, inject_now, coupling_now, local_now = span_in

time: 189 us -> 172 us (0.910)
  waiting for transfers between devices: 42.5 us -> 24.1 us
  other arithmetic: 12.1 us -> 15 us
    ppermute x15, waiting for transfers between devices: 42.5 us -> 24.1 us  [shifted(): return lax.ppermute(array, axis, pairs)]
  transfers between devices with their start and end apart: 15 -> 15, of which waited for: 7 -> 8; matrix products, arithmetic and copies ran while one was open for 36% -> 39% of each run, Pallas kernels for 0% -> 0%
where the time goes in v5:
time: 172 us; the launch traced here: 171 us
  matrix products  49 us (28%)
  starting transfers between devices  42.6 us (25%)
  waiting for transfers between devices  24.1 us (14%)
  blocking collectives  20.1 us (12%)
  local copies, waits for them, and re-layouts  18.2 us (11%)
  other arithmetic  15 us (9%)
    ppermute x15, starting transfers between devices, shifted(): return lax.ppermute(array, axis, pairs)  42.6 us
    ppermute x15, waiting for transfers between devices, shifted(): return lax.ppermute(array, axis, pairs)  24.1 us
    all_to_all x1, blocking collectives, shards(): lax.all_to_all(partial_sum.reshape(head_size, local_rows // head_size, pa...  20.1 us
    dot_general x30, matrix products, apply_map(): return jnp.einsum('hrke,hrev->hrkv', matrix, state_now, precision=highest)  10.5 us
    dot_general x14, matrix products, unit_lower_inverse(): jnp.einsum('...ij,...jk->...ik', inverse, coupling, precision=highest)  9.14 us
    dot_general x14, matrix products, unit_lower_inverse(): jnp.einsum('...ij,...jk->...ik', jnp.einsum('...ij,...jk->...ik', inverse...  7.71 us
    dot_general x4, matrix products, replay(): jnp.einsum('hrck,hrkv->hrcv', coupling_now, state_now, precision=highest)  6.2 us
    dot_general x2, matrix products, recurrence(): jnp.einsum('hrnce,hrnek->hrnck', attention, key_part, precision=highest)  4.54 us
  transfers between devices with their start and end apart: 15, of which 8 were waited for; matrix products, arithmetic and copies ran while one was open for 39% of the time, Pallas kernels for 0%

profile of v5, /device:TPU:128, one launch (start us, length us, event | category | flops | bytes accessed | tf_op | source)
XLA Modules:
  0.0 170.9 jit_solution(8968583270466734906)
XLA Ops:
  0.8 3.5 %collective-permute-start = (bf16[3,256]{1,0:T(4,128)(2,1)S(1)}, bf16[3,256]{1,0:T(4,128)(2,1)S(1)}, u32[]{:S(2)}, u32[]{:S(2)}) collective-permute-start(bf16[3,256]{1,0:T(4,128)(2,1)S(1)} %slice.145), channel_id=1, source_target_pairs={{0,8},{8,16},{16,24},{24,32},{32,40},{40,48},{48,56},{56,64},{64,7... | collective-permute-start | bytes 4616 | tf_op jit(solution)/shard_map/ppermute | solution.py:18
  5.6 3.5 %collective-permute-start.1 = (bf16[3,512]{1,0:T(4,128)(2,1)}, bf16[3,512]{1,0:T(4,128)(2,1)}, u32[]{:S(2)}, u32[]{:S(2)}) collective-permute-start(bf16[3,512]{1,0:T(4,128)(2,1)} %slice.156), channel_id=1, source_target_pairs={{0,8},{8,16},{16,24},{24,32},{32,40},{40,48},{48,56},{56,64},{64,7... | collective-permute-start | bytes 9224 | tf_op jit(solution)/shard_map/ppermute | solution.py:18
  9.8 3.2 %collective-permute-start.8 = (bf16[3,256]{1,0:T(4,128)(2,1)S(1)}, bf16[3,256]{1,0:T(4,128)(2,1)S(1)}, u32[]{:S(2)}, u32[]{:S(2)}) collective-permute-start(bf16[3,256]{1,0:T(4,128)(2,1)S(1)} %slice.168), channel_id=1, source_target_pairs={{0,8},{8,16},{16,24},{24,32},{32,40},{40,48},{48,56},{56,64},{64,7... | collective-permute-start | bytes 4616 | tf_op jit(solution)/shard_map/ppermute | solution.py:18
  55.6 2.6 %collective-permute-start.9 = (bf16[2,1,2,128,128]{4,3,2,1,0:T(8,128)(2,1)}, bf16[2,1,2,128,128]{4,3,2,1,0:T(8,128)(2,1)}, u32[]{:S(2)}, u32[]{:S(2)}) collective-permute-start(bf16[2,1,2,128,128]{4,3,2,1,0:T(8,128)(2,1)} %pad_maximum_fusion.4), channel_id=1, source_target_pairs={{0,8},{8,16},{16,24},{24,32},{32,40},{40,48},{48,56},{56,64},{64,7... | collective-permute-start | bytes 393224 | tf_op jit(solution)/shard_map/ppermute | solution.py:18
  58.2 2.1 %convolution_bitcast_fusion.4 = f32[2,1,2,128,128]{4,3,0,2,1:T(8,128)} fusion(f32[1,2,2,128,256]{4,3,2,1,0:T(8,128)} %copy-done.2, f32[2,128,128]{2,1,0:T(8,128)S(1)} %copy-done.7, f32[2,2,128]{2,1,0:T(2,128)S(1)} %bitcast.550, pred[128,128]{1,0:T(8,128)(4,1)S(1)} %get-tuple-element.312), kind=kOutput, calls=%fused_computation.51 | convolution fusion | flops 100925440 | bytes 675840 | tf_op jit(solution)/shard_map/hrnce,hrnev->hrncv/dot_general | solution.py:81
  64.8 4.3 %while.48 = (s32[]{:T(128)}, f32[1,2,128,128]{3,2,1,0:T(8,128)S(1)}, f32[1,2,128,128]{3,2,1,0:T(8,128)}, f32[2,1,2,128,128]{4,3,2,1,0:T(8,128)S(1)}, f32[2,1,2,128,128]{4,3,2,1,0:T(8,128)S(1)}, /*index=5*/s32[]{:T(128)}) while((s32[]{:T(128)}, f32[1,2,128,128]{3,2,1,0:T(8,128)S(1)}, f32[1,2,128,128]{3,2,1,0:T(8,128)}, ...), condition=%wide.region_3.4_spmd, body=%wide.region_2.3_spmd.sunk | while | flops 100696064 | bytes 1442897 | solution.py:104
  70.1 3.5 %collective-permute-start.2 = (bf16[2,1,2,128,128]{4,3,2,1,0:T(8,128)(2,1)S(1)}, bf16[2,1,2,128,128]{4,3,2,1,0:T(8,128)(2,1)S(1)}, u32[]{:S(2)}, u32[]{:S(2)}) collective-permute-start(bf16[2,1,2,128,128]{4,3,2,1,0:T(8,128)(2,1)S(1)} %pad_maximum_fusion), channel_id=1, source_target_pairs={{0,8},{8,16},{16,24},{24,32},{32,40},{40,48},{48,56},{56,64},{64,7... | collective-permute-start | bytes 393224 | tf_op jit(solution)/shard_map/ppermute | solution.py:18
  73.6 2.3 %fusion.40 = f32[2,1,2,128,128]{4,3,0,2,1:T(8,128)} fusion(f32[1,2,2,128,256]{4,3,2,1,0:T(8,128)} %copy-done.2, f32[2,128,128]{2,1,0:T(8,128)} %fusion.341, f32[2,128,128]{2,1,0:T(8,128)} %get-tuple-element.270, f32[2,2,128]{2,1,0:T(2,128)} %get-tuple-element.284, f32[2,2,128]{2,1,0:T(2,128)} %bitcast.544, pred[128,128]{1,0:T(8,128)(4,1)S(1)} %get-tuple-element.312), kind=kOutput, calls=%fused_computation.53 | convolution fusion | flops 101056512 | bytes 808960 | tf_op jit(solution)/shard_map/hrnce,hrnek->hrnck/dot_general | solution.py:82
  75.9 2.3 %fusion.49 = f32[2,1,2,128,128]{4,3,0,2,1:T(8,128)} fusion(f32[1,2,2,128,256]{4,3,2,1,0:T(8,128)} %copy-done.3, f32[2,128,128]{2,1,0:T(8,128)} %fusion.340, f32[2,128,128]{2,1,0:T(8,128)} %get-tuple-element.269, f32[2,2,128]{2,1,0:T(2,128)} %get-tuple-element.281, f32[2,2,128]{2,1,0:T(2,128)} %bitcast.533, pred[128,128]{1,0:T(8,128)(4,1)S(1)} %get-tuple-element.312), kind=kOutput, calls=%fused_computation.73 | convolution fusion | flops 101056512 | bytes 808960 | tf_op jit(solution)/shard_map/hrnce,hrnek->hrnck/dot_general | solution.py:82
  81.5 4.8 %collective-permute-start.10 = (bf16[2,1,2,128,128]{4,3,2,1,0:T(8,128)(2,1)S(1)}, bf16[2,1,2,128,128]{4,3,2,1,0:T(8,128)(2,1)S(1)}, u32[]{:S(2)}, u32[]{:S(2)}) collective-permute-start(bf16[2,1,2,128,128]{4,3,2,1,0:T(8,128)(2,1)S(1)} %pad_maximum_fusion.5), channel_id=1, source_target_pairs={{0,16},{8,24},{16,32},{24,40},{32,48},{40,56},{48,64},{56,72},{64,... | collective-permute-start | bytes 393224 | tf_op jit(solution)/shard_map/ppermute | solution.py:18
  86.8 3.0 %collective-permute-start.3 = (bf16[2,1,2,128,128]{4,3,2,1,0:T(8,128)(2,1)S(1)}, bf16[2,1,2,128,128]{4,3,2,1,0:T(8,128)(2,1)S(1)}, u32[]{:S(2)}, u32[]{:S(2)}) collective-permute-start(bf16[2,1,2,128,128]{4,3,2,1,0:T(8,128)(2,1)S(1)} %pad_maximum_fusion.1), channel_id=1, source_target_pairs={{0,16},{8,24},{16,32},{24,40},{32,48},{40,56},{48,64},{56,72},{64,... | collective-permute-start | bytes 393224 | tf_op jit(solution)/shard_map/ppermute | solution.py:18
  89.8 2.2 %collective-permute-done.10 = bf16[2,1,2,128,128]{4,3,2,1,0:T(8,128)(2,1)S(1)} collective-permute-done((bf16[2,1,2,128,128]{4,3,2,1,0:T(8,128)(2,1)S(1)}, bf16[2,1,2,128,128]{4,3,2,1,0:T(8,128)(2,1)S(1)}, u32[]{:S(2)}, u32[]{:S(2)}) %collective-permute-start.10) | collective-permute-done | bytes 131104 | tf_op jit(solution)/shard_map/ppermute | solution.py:18
  92.5 1.9 %collective-permute-start.11 = (bf16[2,1,2,128,128]{4,3,2,1,0:T(8,128)(2,1)S(1)}, bf16[2,1,2,128,128]{4,3,2,1,0:T(8,128)(2,1)S(1)}, u32[]{:S(2)}, u32[]{:S(2)}) collective-permute-start(bf16[2,1,2,128,128]{4,3,2,1,0:T(8,128)(2,1)S(1)} %pad_maximum_fusion.6), channel_id=1, source_target_pairs={{0,32},{8,40},{16,48},{24,56},{32,64},{40,72},{48,80},{56,88},{64,... | collective-permute-start | bytes 393224 | tf_op jit(solution)/shard_map/ppermute | solution.py:18
  94.4 4.0 %collective-permute-done.3 = bf16[2,1,2,128,128]{4,3,2,1,0:T(8,128)(2,1)S(1)} collective-permute-done((bf16[2,1,2,128,128]{4,3,2,1,0:T(8,128)(2,1)S(1)}, bf16[2,1,2,128,128]{4,3,2,1,0:T(8,128)(2,1)S(1)}, u32[]{:S(2)}, u32[]{:S(2)}) %collective-permute-start.3) | collective-permute-done | bytes 131104 | tf_op jit(solution)/shard_map/ppermute | solution.py:18
  98.9 1.9 %collective-permute-start.4 = (bf16[2,1,2,128,128]{4,3,2,1,0:T(8,128)(2,1)S(1)}, bf16[2,1,2,128,128]{4,3,2,1,0:T(8,128)(2,1)S(1)}, u32[]{:S(2)}, u32[]{:S(2)}) collective-permute-start(bf16[2,1,2,128,128]{4,3,2,1,0:T(8,128)(2,1)S(1)} %pad_maximum_fusion.2), channel_id=1, source_target_pairs={{0,32},{8,40},{16,48},{24,56},{32,64},{40,72},{48,80},{56,88},{64,... | collective-permute-start | bytes 393224 | tf_op jit(solution)/shard_map/ppermute | solution.py:18
  101.3 2.3 %collective-permute-start.12 = (bf16[2,1,2,128,128]{4,3,2,1,0:T(8,128)(2,1)S(1)}, bf16[2,1,2,128,128]{4,3,2,1,0:T(8,128)(2,1)S(1)}, u32[]{:S(2)}, u32[]{:S(2)}) collective-permute-start(bf16[2,1,2,128,128]{4,3,2,1,0:T(8,128)(2,1)S(1)} %pad_maximum_fusion.7), channel_id=1, source_target_pairs={{0,64},{8,72},{16,80},{24,88},{32,96},{40,104},{48,112},{56,120},{... | collective-permute-start | bytes 393224 | tf_op jit(solution)/shard_map/ppermute | solution.py:18
  103.6 4.3 %collective-permute-done.4 = bf16[2,1,2,128,128]{4,3,2,1,0:T(8,128)(2,1)S(1)} collective-permute-done((bf16[2,1,2,128,128]{4,3,2,1,0:T(8,128)(2,1)S(1)}, bf16[2,1,2,128,128]{4,3,2,1,0:T(8,128)(2,1)S(1)}, u32[]{:S(2)}, u32[]{:S(2)}) %collective-permute-start.4) | collective-permute-done | bytes 131104 | tf_op jit(solution)/shard_map/ppermute | solution.py:18
  110.3 4.3 %collective-permute-done.12 = bf16[2,1,2,128,128]{4,3,2,1,0:T(8,128)(2,1)S(1)} collective-permute-done((bf16[2,1,2,128,128]{4,3,2,1,0:T(8,128)(2,1)S(1)}, bf16[2,1,2,128,128]{4,3,2,1,0:T(8,128)(2,1)S(1)}, u32[]{:S(2)}, u32[]{:S(2)}) %collective-permute-start.12) | collective-permute-done | bytes 131104 | tf_op jit(solution)/shard_map/ppermute | solution.py:18
  119.3 5.6 %collective-permute-done.13 = bf16[1,2,128,128]{3,2,1,0:T(8,128)(2,1)S(1)} collective-permute-done((bf16[1,2,128,128]{3,2,1,0:T(8,128)(2,1)S(1)}, bf16[1,2,128,128]{3,2,1,0:T(8,128)(2,1)S(1)}, u32[]{:S(2)}, u32[]{:S(2)}) %collective-permute-start.13) | collective-permute-done | bytes 65568 | tf_op jit(solution)/shard_map/ppermute | solution.py:18
  125.2 5.9 %collective-permute-start.14 = (bf16[1,2,128,128]{3,2,1,0:T(8,128)(2,1)S(1)}, bf16[1,2,128,128]{3,2,1,0:T(8,128)(2,1)S(1)}, u32[]{:S(2)}, u32[]{:S(2)}) collective-permute-start(bf16[1,2,128,128]{3,2,1,0:T(8,128)(2,1)S(1)} %fusion.68), channel_id=1, source_target_pairs={{0,8},{8,16},{16,24},{24,32},{32,40},{40,48},{48,56},{56,64},{64,7... | collective-permute-start | bytes 196616 | tf_op jit(solution)/shard_map/ppermute | solution.py:18
  135.4 4.4 %while.51 = (s32[]{:T(128)}, f32[1,2,128,128]{3,2,1,0:T(8,128)S(1)}, f32[2,1,2,128,128]{4,3,2,1,0:T(8,128)}, f32[2,1,2,128,128]{4,3,2,1,0:T(8,128)S(1)}, f32[2,1...) while((s32[]{:T(128)}, ...), condition=%wide.region_10.11_spmd, body=%wide.region_9.10_spmd.sunk | while | flops 100728832 | bytes 1312861 | solution.py:136
  135.4 1.9 %fusion.438 = f32[2,1,2,128,128]{4,3,2,1,0:T(8,128)} fusion(f32[2,1,2,128,128]{4,3,2,1,0:T(8,128)} %get-tuple-element.492, s32[]{:T(128)S(6)} %copy.96, f32[1,2,128,128]{3,2,1,0:T(8,128)S(1)} %copy.155, f32[2,1,2,128,128]{4,3,0,2,1:T(8,128)} %get-tuple-element.504, f32[2,1,2,128,128]{4,3,0,2,1:T(8,128)} %get-tuple-element.503), kind=kOutput, calls=%fused_computation.37.clone.1 | convolution fusion | flops 50364416 | bytes 525312 | tf_op jit(solution)/shard_map/while/body/eval_jaxpr/hrck,hrkv->hrcv/dot_general | solution.py:132
  142.6 3.0 %while.49 = (s32[]{:T(128)}, f32[1,2,128,128]{3,2,1,0:T(8,128)S(1)}, f32[2,1,2,128,128]{4,3,2,1,0:T(8,128)S(1)}, f32[2,1,2,128,128]{4,3,2,1,0:T(8,128)S(1)}, f32...) while((s32[]{:T(128)}, ...), condition=%wide.region_5.6_spmd, body=%wide.region_4.5_spmd.sunk | while | flops 100728832 | bytes 1312861 | solution.py:136
  150.0 20.1 %all_to_all.5 = bf16[8,32,2048]{2,1,0:T(8,128)(2,1)S(1)} all-to-all(bf16[8,32,2048]{2,1,0:T(8,128)(2,1)S(1)} %bitcast.530), channel_id=1, replica_groups=mesh['seq'=32,'head'=8] {'head'}, dimensions={0} | all-to-all | bytes 2097152 | tf_op jit(solution)/shard_map/all_to_all | solution.py:202
  (283 shorter events, 85.2 us)
Async XLA Ops:
  0.0 149.2 %copy-start = (bf16[512,2048]{1,0:T(8,128)(2,1)S(1)}, bf16[512,2048]{1,0:T(8,128)(2,1)}, u32[]{:S(2)}) copy-start(bf16[512,2048]{1,0:T(8,128)(2,1)} %param.29) | copy-start | bytes 6291460
  0.8 23.1 %collective-permute-start = (bf16[3,256]{1,0:T(4,128)(2,1)S(1)}, bf16[3,256]{1,0:T(4,128)(2,1)S(1)}, u32[]{:S(2)}, u32[]{:S(2)}) collective-permute-start(bf16[3,256]{1,0:T(4,128)(2,1)S(1)} %slice.145), channel_id=1, source_target_pairs={{0,8},{8,16},{16,24},{24,32},{32,40},{40,48},{48,56},{56,64},{64,7... | collective-permute-start | bytes 4616 | tf_op jit(solution)/shard_map/ppermute | solution.py:18
  5.6 43.6 %collective-permute-start.1 = (bf16[3,512]{1,0:T(4,128)(2,1)}, bf16[3,512]{1,0:T(4,128)(2,1)}, u32[]{:S(2)}, u32[]{:S(2)}) collective-permute-start(bf16[3,512]{1,0:T(4,128)(2,1)} %slice.156), channel_id=1, source_target_pairs={{0,8},{8,16},{16,24},{24,32},{32,40},{40,48},{48,56},{56,64},{64,7... | collective-permute-start | bytes 9224 | tf_op jit(solution)/shard_map/ppermute | solution.py:18
  9.8 16.6 %collective-permute-start.8 = (bf16[3,256]{1,0:T(4,128)(2,1)S(1)}, bf16[3,256]{1,0:T(4,128)(2,1)S(1)}, u32[]{:S(2)}, u32[]{:S(2)}) collective-permute-start(bf16[3,256]{1,0:T(4,128)(2,1)S(1)} %slice.168), channel_id=1, source_target_pairs={{0,8},{8,16},{16,24},{24,32},{32,40},{40,48},{48,56},{56,64},{64,7... | collective-permute-start | bytes 4616 | tf_op jit(solution)/shard_map/ppermute | solution.py:18
  13.0 49.4 %copy-start.5 = (f32[128,128]{1,0:T(8,128)}, f32[128,128]{1,0:T(8,128)S(1)}, u32[]{:S(2)}) copy-start(f32[128,128]{1,0:T(8,128)S(1)} %fusion.315) | copy-start | bytes 196612
  13.0 16.0 %copy-start.33 = (pred[128,128]{1,0:T(8,128)(4,1)}, pred[128,128]{1,0:T(8,128)(4,1)S(1)}, u32[]{:S(2)}) copy-start(pred[128,128]{1,0:T(8,128)(4,1)S(1)} %get-tuple-element.313) | copy-start | bytes 49156
  15.5 13.5 %copy-start.27 = (f32[2,2,128]{2,1,0:T(2,128)}, f32[2,2,128]{2,1,0:T(2,128)S(1)}, u32[]{:S(2)}) copy-start(f32[2,2,128]{2,1,0:T(2,128)S(1)} %mul.561) | copy-start | bytes 6148
  16.1 12.9 %copy-start.22 = (f32[1,2,2,128]{3,2,1,0:T(2,128)}, f32[1,2,2,128]{3,2,1,0:T(2,128)S(1)}, u32[]{:S(2)}) copy-start(f32[1,2,2,128]{3,2,1,0:T(2,128)S(1)} %reduce_window_sum.23) | copy-start | bytes 6148
  55.6 23.8 %collective-permute-start.9 = (bf16[2,1,2,128,128]{4,3,2,1,0:T(8,128)(2,1)}, bf16[2,1,2,128,128]{4,3,2,1,0:T(8,128)(2,1)}, u32[]{:S(2)}, u32[]{:S(2)}) collective-permute-start(bf16[2,1,2,128,128]{4,3,2,1,0:T(8,128)(2,1)} %pad_maximum_fusion.4), channel_id=1, source_target_pairs={{0,8},{8,16},{16,24},{24,32},{32,40},{40,48},{48,56},{56,64},{64,7... | collective-permute-start | bytes 393224 | tf_op jit(solution)/shard_map/ppermute | solution.py:18
  69.1 9.1 %copy-start.4 = (f32[1,2,2,128,256]{4,3,2,1,0:T(8,128)S(1)}, f32[1,2,2,128,256]{4,3,2,1,0:T(8,128)}, u32[]{:S(2)}) copy-start(f32[1,2,2,128,256]{4,3,2,1,0:T(8,128)} %copy-done.3) | copy-start | bytes 1572868
  69.1 9.1 %copy-start.8 = (f32[2,128,128]{2,1,0:T(8,128)S(1)}, f32[2,128,128]{2,1,0:T(8,128)}, u32[]{:S(2)}) copy-start(f32[2,128,128]{2,1,0:T(8,128)} %fusion.340) | copy-start | bytes 393220
  69.1 9.1 %copy-start.21 = (f32[1,2,2,128]{3,2,1,0:T(2,128)S(1)}, f32[1,2,2,128]{3,2,1,0:T(2,128)}, u32[]{:S(2)}) copy-start(f32[1,2,2,128]{3,2,1,0:T(2,128)} %copy-done.19) | copy-start | bytes 6148
  70.1 16.3 %copy-start.1 = (f32[1,2,128,128]{3,2,1,0:T(8,128)S(1)}, f32[1,2,128,128]{3,2,1,0:T(8,128)}, u32[]{:S(2)}) copy-start(f32[1,2,128,128]{3,2,1,0:T(8,128)} %get-tuple-element.136) | copy-start | bytes 393220
  70.1 16.2 %collective-permute-start.2 = (bf16[2,1,2,128,128]{4,3,2,1,0:T(8,128)(2,1)S(1)}, bf16[2,1,2,128,128]{4,3,2,1,0:T(8,128)(2,1)S(1)}, u32[]{:S(2)}, u32[]{:S(2)}) collective-permute-start(bf16[2,1,2,128,128]{4,3,2,1,0:T(8,128)(2,1)S(1)} %pad_maximum_fusion), channel_id=1, source_target_pairs={{0,8},{8,16},{16,24},{24,32},{32,40},{40,48},{48,56},{56,64},{64,7... | collective-permute-start | bytes 393224 | tf_op jit(solution)/shard_map/ppermute | solution.py:18
  81.5 10.5 %collective-permute-start.10 = (bf16[2,1,2,128,128]{4,3,2,1,0:T(8,128)(2,1)S(1)}, bf16[2,1,2,128,128]{4,3,2,1,0:T(8,128)(2,1)S(1)}, u32[]{:S(2)}, u32[]{:S(2)}) collective-permute-start(bf16[2,1,2,128,128]{4,3,2,1,0:T(8,128)(2,1)S(1)} %pad_maximum_fusion.5), channel_id=1, source_target_pairs={{0,16},{8,24},{16,32},{24,40},{32,48},{40,56},{48,64},{56,72},{64,... | collective-permute-start | bytes 393224 | tf_op jit(solution)/shard_map/ppermute | solution.py:18
  86.8 11.5 %collective-permute-start.3 = (bf16[2,1,2,128,128]{4,3,2,1,0:T(8,128)(2,1)S(1)}, bf16[2,1,2,128,128]{4,3,2,1,0:T(8,128)(2,1)S(1)}, u32[]{:S(2)}, u32[]{:S(2)}) collective-permute-start(bf16[2,1,2,128,128]{4,3,2,1,0:T(8,128)(2,1)S(1)} %pad_maximum_fusion.1), channel_id=1, source_target_pairs={{0,16},{8,24},{16,32},{24,40},{32,48},{40,56},{48,64},{56,72},{64,... | collective-permute-start | bytes 393224 | tf_op jit(solution)/shard_map/ppermute | solution.py:18
  92.5 8.3 %collective-permute-start.11 = (bf16[2,1,2,128,128]{4,3,2,1,0:T(8,128)(2,1)S(1)}, bf16[2,1,2,128,128]{4,3,2,1,0:T(8,128)(2,1)S(1)}, u32[]{:S(2)}, u32[]{:S(2)}) collective-permute-start(bf16[2,1,2,128,128]{4,3,2,1,0:T(8,128)(2,1)S(1)} %pad_maximum_fusion.6), channel_id=1, source_target_pairs={{0,32},{8,40},{16,48},{24,56},{32,64},{40,72},{48,80},{56,88},{64,... | collective-permute-start | bytes 393224 | tf_op jit(solution)/shard_map/ppermute | solution.py:18
  98.9 9.0 %collective-permute-start.4 = (bf16[2,1,2,128,128]{4,3,2,1,0:T(8,128)(2,1)S(1)}, bf16[2,1,2,128,128]{4,3,2,1,0:T(8,128)(2,1)S(1)}, u32[]{:S(2)}, u32[]{:S(2)}) collective-permute-start(bf16[2,1,2,128,128]{4,3,2,1,0:T(8,128)(2,1)S(1)} %pad_maximum_fusion.2), channel_id=1, source_target_pairs={{0,32},{8,40},{16,48},{24,56},{32,64},{40,72},{48,80},{56,88},{64,... | collective-permute-start | bytes 393224 | tf_op jit(solution)/shard_map/ppermute | solution.py:18
  101.3 13.3 %collective-permute-start.12 = (bf16[2,1,2,128,128]{4,3,2,1,0:T(8,128)(2,1)S(1)}, bf16[2,1,2,128,128]{4,3,2,1,0:T(8,128)(2,1)S(1)}, u32[]{:S(2)}, u32[]{:S(2)}) collective-permute-start(bf16[2,1,2,128,128]{4,3,2,1,0:T(8,128)(2,1)S(1)} %pad_maximum_fusion.7), channel_id=1, source_target_pairs={{0,64},{8,72},{16,80},{24,88},{32,96},{40,104},{48,112},{56,120},{... | collective-permute-start | bytes 393224 | tf_op jit(solution)/shard_map/ppermute | solution.py:18
  108.3 9.1 %collective-permute-start.5 = (bf16[2,1,2,128,128]{4,3,2,1,0:T(8,128)(2,1)S(1)}, bf16[2,1,2,128,128]{4,3,2,1,0:T(8,128)(2,1)S(1)}, u32[]{:S(2)}, u32[]{:S(2)}) collective-permute-start(bf16[2,1,2,128,128]{4,3,2,1,0:T(8,128)(2,1)S(1)} %pad_maximum_fusion.3), channel_id=1, source_target_pairs={{0,64},{8,72},{16,80},{24,88},{32,96},{40,104},{48,112},{56,120},{... | collective-permute-start | bytes 393224 | tf_op jit(solution)/shard_map/ppermute | solution.py:18
  114.8 10.2 %collective-permute-start.13 = (bf16[1,2,128,128]{3,2,1,0:T(8,128)(2,1)S(1)}, bf16[1,2,128,128]{3,2,1,0:T(8,128)(2,1)S(1)}, u32[]{:S(2)}, u32[]{:S(2)}) collective-permute-start(bf16[1,2,128,128]{3,2,1,0:T(8,128)(2,1)S(1)} %get-tuple-element.302), channel_id=1, source_target_pairs={{0,128},{8,136},{16,144},{24,152},{32,160},{40,168},{48,176},{56,1... | collective-permute-start | bytes 196616 | tf_op jit(solution)/shard_map/ppermute | solution.py:18
  117.6 13.4 %collective-permute-start.6 = (bf16[1,2,128,128]{3,2,1,0:T(8,128)(2,1)S(1)}, bf16[1,2,128,128]{3,2,1,0:T(8,128)(2,1)S(1)}, u32[]{:S(2)}, u32[]{:S(2)}) collective-permute-start(bf16[1,2,128,128]{3,2,1,0:T(8,128)(2,1)S(1)} %get-tuple-element.304), channel_id=1, source_target_pairs={{0,128},{8,136},{16,144},{24,152},{32,160},{40,168},{48,176},{56,1... | collective-permute-start | bytes 196616 | tf_op jit(solution)/shard_map/ppermute | solution.py:18
  125.2 9.5 %collective-permute-start.14 = (bf16[1,2,128,128]{3,2,1,0:T(8,128)(2,1)S(1)}, bf16[1,2,128,128]{3,2,1,0:T(8,128)(2,1)S(1)}, u32[]{:S(2)}, u32[]{:S(2)}) collective-permute-start(bf16[1,2,128,128]{3,2,1,0:T(8,128)(2,1)S(1)} %fusion.68), channel_id=1, source_target_pairs={{0,8},{8,16},{16,24},{24,32},{32,40},{40,48},{48,56},{56,64},{64,7... | collective-permute-start | bytes 196616 | tf_op jit(solution)/shard_map/ppermute | solution.py:18
  131.9 9.8 %collective-permute-start.7 = (bf16[1,2,128,128]{3,2,1,0:T(8,128)(2,1)}, bf16[1,2,128,128]{3,2,1,0:T(8,128)(2,1)}, u32[]{:S(2)}, u32[]{:S(2)}) collective-permute-start(bf16[1,2,128,128]{3,2,1,0:T(8,128)(2,1)} %fusion.69), channel_id=1, source_target_pairs={{0,8},{8,16},{16,24},{24,32},{32,40},{40,48},{48,56},{56,64},{64,7... | collective-permute-start | bytes 196616 | tf_op jit(solution)/shard_map/ppermute | solution.py:18
  (36 other events, 134.7 us)

commit v6 on v5

--- a/solution.py
+++ b/solution.py
@@ -53,8 +53,7 @@
     return jnp.einsum("hrke,hrev->hrkv", matrix, state_now, precision=highest)
 
 
-def recurrence(query_blocks, key_blocks, value_blocks, strength_blocks, decay_blocks):
-    key_heads, ratio_heads = value_blocks.shape[:2]
+def chunk_maps(query_blocks, key_blocks, value_blocks, strength_blocks, decay_blocks):
     cumulative = jnp.cumsum(decay_blocks, axis=-1)
     positions = jnp.arange(SPAN)
     inclusive = positions[:, None] >= positions[None, :]
@@ -88,6 +87,11 @@
         "hrnck,hrnce->hrnke", scaled_keys, key_part, precision=highest
     )
     inject = jnp.einsum("hrnck,hrncv->hrnkv", scaled_keys, value_part, precision=highest)
+    return transit, inject, coupling, local_out
+
+
+def relay_group(transit, inject, coupling, local_out):
+    key_heads, ratio_heads = transit.shape[:2]
     transit_seq = jnp.moveaxis(transit, 2, 0)
     inject_seq = jnp.moveaxis(inject, 2, 0)
     identity = jnp.broadcast_to(jnp.eye(DK, dtype=jnp.float32), (key_heads, ratio_heads, DK, DK))
@@ -178,15 +182,9 @@
     value_blocks = values.reshape(spans, SPAN, key_heads, ratio_heads, DV).transpose(2, 3, 0, 1, 4)
     strength_blocks = strength.reshape(key_heads, ratio_heads, spans, SPAN)
     decay_blocks = log_decay.reshape(key_heads, ratio_heads, spans, SPAN)
+    maps = chunk_maps(query_blocks, key_blocks, value_blocks, strength_blocks, decay_blocks)
     parts = [
-        recurrence(
-            query_blocks[group : group + 1],
-            key_blocks[group : group + 1],
-            value_blocks[group : group + 1],
-            strength_blocks[group : group + 1],
-            decay_blocks[group : group + 1],
-        )
-        for group in range(key_heads)
+        relay_group(*[piece[group : group + 1] for piece in maps]) for group in range(key_heads)
     ]
     outputs = jnp.concatenate(parts, axis=1)
     core_out = jnp.moveaxis(outputs, 0, 2)
@@ -199,13 +197,14 @@
         jnp.bfloat16
     )
     head_size = lax.axis_size("head")
-    pieces = lax.all_to_all(
-        partial_sum.reshape(head_size, local_rows // head_size, partial_sum.shape[1]),
-        "head",
-        0,
-        0,
-    )
-    return jnp.sum(pieces.astype(jnp.float32), axis=0).astype(jnp.bfloat16)
+    head_index = lax.axis_index("head")
+    pieces = partial_sum.reshape(head_size, local_rows // head_size, partial_sum.shape[1])
+    summed = pieces[head_index].astype(jnp.float32)
+    for hop in range(1, head_size):
+        outgoing = pieces[(head_index + hop) % head_size]
+        pairs = [(i, (i + hop) % head_size) for i in range(head_size)]
+        summed = summed + lax.ppermute(outgoing, "head", pairs).astype(jnp.float32)
+    return summed.astype(jnp.bfloat16)
 
 
 def solution(mesh):

time: 172 us -> 167 us (0.971); the launches traced: 171 us -> 164 us
  blocking collectives: 20.1 us -> 0 us
  starting transfers between devices: 42.6 us -> 53 us
  matrix products: 49 us -> 38.7 us
  local copies, waits for them, and re-layouts: 18.2 us -> 24.5 us
  waiting for transfers between devices: 24.1 us -> 29.5 us
    all_to_all x1 -> x0, blocking collectives: 20.1 us -> none  [shards(): lax.all_to_all(partial_sum.reshape(head_size, local_rows // head_size, pa...]
    ppermute x0 -> x7, starting transfers between devices: none -> 10.2 us  [shards(): summed = summed + lax.ppermute(outgoing, 'head', pairs).astype(jnp.float32)]
    dot_general x14 -> x7, matrix products: 14.6 us -> 9.27 us  [the longest x1 2.65 us: chunk_maps(): jnp.einsum('hrnce,hrnev->hrncv', attention, value_part, precision=highest)]
    ppermute x0 -> x7, waiting for transfers between devices: none -> 5.33 us  [shards(): summed = summed + lax.ppermute(outgoing, 'head', pairs).astype(jnp.float32)]
    transpose x0 -> x4, local copies, waits for them, and re-layouts: none -> 4.23 us  [the longest x1 1.89 us: relay_group(): jnp.moveaxis(local_out, 2, 0)]
    dot_general x14 -> x7, matrix products: 7.71 us -> 4.7 us  [unit_lower_inverse(): jnp.einsum('...ij,...jk->...ik', jnp.einsum('...ij,...jk->...ik', inverse...]
    dot_general x14 -> x7, matrix products: 9.14 us -> 6.23 us  [unit_lower_inverse(): jnp.einsum('...ij,...jk->...ik', inverse, coupling, precision=highest)]
    convert_element_type x3 -> x4, other arithmetic: 0.87 us -> 2.87 us  [the longest x1 2 us: shards(): return summed.astype(jnp.bfloat16)]
  transfers between devices with their start and end apart: 15 -> 22, of which waited for: 8 -> 12; matrix products, arithmetic and copies ran while one was open for 39% -> 32% of each run, Pallas kernels for 0% -> 0%
where the time goes in v6:
time: 167 us; the launch traced here: 164 us
  starting transfers between devices  53 us (32%)
  matrix products  38.7 us (23%)
  waiting for transfers between devices  29.5 us (18%)
  local copies, waits for them, and re-layouts  24.5 us (15%)
  other arithmetic  16.4 us (10%)
    ppermute x15, starting transfers between devices, shifted(): return lax.ppermute(array, axis, pairs)  42.8 us
    ppermute x15, waiting for transfers between devices, shifted(): return lax.ppermute(array, axis, pairs)  24.2 us
    dot_general x30, matrix products, apply_map(): return jnp.einsum('hrke,hrev->hrkv', matrix, state_now, precision=highest)  10.5 us
    ppermute x7, starting transfers between devices, shards(): summed = summed + lax.ppermute(outgoing, 'head', pairs).astype(jnp.float32)  10.2 us
    dot_general x7, matrix products, unit_lower_inverse(): jnp.einsum('...ij,...jk->...ik', inverse, coupling, precision=highest)  6.23 us
    dot_general x4, matrix products, replay(): jnp.einsum('hrck,hrkv->hrcv', coupling_now, state_now, precision=highest)  6.2 us
    ppermute x7, waiting for transfers between devices, shards(): summed = summed + lax.ppermute(outgoing, 'head', pairs).astype(jnp.float32)  5.33 us
    dot_general x7, matrix products, unit_lower_inverse(): jnp.einsum('...ij,...jk->...ik', jnp.einsum('...ij,...jk->...ik', inverse...  4.7 us
  transfers between devices with their start and end apart: 22, of which 12 were waited for; matrix products, arithmetic and copies ran while one was open for 32% of the time, Pallas kernels for 0%

profile of v6, /device:TPU:128, one launch (start us, length us, event | category | flops | bytes accessed | tf_op | source)
XLA Modules:
  0.0 163.6 jit_solution(15264570396045793585)
XLA Ops:
  0.8 3.5 %collective-permute-start = (bf16[3,256]{1,0:T(4,128)(2,1)S(1)}, bf16[3,256]{1,0:T(4,128)(2,1)S(1)}, u32[]{:S(2)}, u32[]{:S(2)}) collective-permute-start(bf16[3,256]{1,0:T(4,128)(2,1)S(1)} %slice.116), channel_id=1, source_target_pairs={{0,8},{8,16},{16,24},{24,32},{32,40},{40,48},{48,56},{56,64},{64,7... | collective-permute-start | bytes 4616 | tf_op jit(solution)/shard_map/ppermute | solution.py:18
  5.6 3.5 %collective-permute-start.1 = (bf16[3,512]{1,0:T(4,128)(2,1)}, bf16[3,512]{1,0:T(4,128)(2,1)}, u32[]{:S(2)}, u32[]{:S(2)}) collective-permute-start(bf16[3,512]{1,0:T(4,128)(2,1)} %slice.125), channel_id=1, source_target_pairs={{0,8},{8,16},{16,24},{24,32},{32,40},{40,48},{48,56},{56,64},{64,7... | collective-permute-start | bytes 9224 | tf_op jit(solution)/shard_map/ppermute | solution.py:18
  10.4 3.2 %collective-permute-start.8 = (bf16[3,256]{1,0:T(4,128)(2,1)}, bf16[3,256]{1,0:T(4,128)(2,1)}, u32[]{:S(2)}, u32[]{:S(2)}) collective-permute-start(bf16[3,256]{1,0:T(4,128)(2,1)} %slice.138), channel_id=1, source_target_pairs={{0,8},{8,16},{16,24},{24,32},{32,40},{40,48},{48,56},{56,64},{64,7... | collective-permute-start | bytes 4616 | tf_op jit(solution)/shard_map/ppermute | solution.py:18
  42.0 2.2 %reshape.1091 = f32[2,128,2,2,128]{4,3,2,1,0:T(2,128)} reshape(f32[256,512]{1,0:T(8,128)} %divide_multiply_fusion) | data formatting | bytes 1048576 | tf_op jit(solution)/shard_map/reshape | solution.py:182
  52.5 2.7 %collective-permute-start.2 = (bf16[2,1,2,128,128]{4,3,2,1,0:T(8,128)(2,1)}, bf16[2,1,2,128,128]{4,3,2,1,0:T(8,128)(2,1)}, u32[]{:S(2)}, u32[]{:S(2)}) collective-permute-start(bf16[2,1,2,128,128]{4,3,2,1,0:T(8,128)(2,1)} %pad_maximum_fusion), channel_id=1, source_target_pairs={{0,8},{8,16},{16,24},{24,32},{32,40},{40,48},{48,56},{56,64},{64,7... | collective-permute-start | bytes 393224 | tf_op jit(solution)/shard_map/ppermute | solution.py:18
  55.3 2.6 %fusion.99 = f32[2,2,2,128,128]{4,3,2,1,0:T(8,128)} fusion(f32[2,2,2,128,256]{4,3,2,1,0:T(8,128)} %copy-done.1, f32[2,2,128,128]{3,2,1,0:T(8,128)S(1)} %fusion.233, f32[2,2,2,128]{3,2,1,0:T(2,128)S(1)} %reduce_window_sum.11, pred[128,128]{1,0:T(8,128)(4,1)S(1)} %copy-done.9), kind=kOutput, calls=%fused_computation.148 | convolution fusion | flops 201850880 | bytes 1335296 | tf_op jit(solution)/shard_map/hrnce,hrnev->hrncv/dot_general | solution.py:80
  61.5 4.3 %while.50 = (s32[]{:T(128)}, f32[1,2,128,128]{3,2,1,0:T(8,128)S(1)}, f32[1,2,128,128]{3,2,1,0:T(8,128)}, f32[2,1,2,128,128]{4,3,2,1,0:T(8,128)S(1)}, f32[2,1,2,128,128]{4,3,2,1,0:T(8,128)S(1)}, /*index=5*/s32[]{:T(128)}) while((s32[]{:T(128)}, f32[1,2,128,128]{3,2,1,0:T(8,128)S(1)}, f32[1,2,128,128]{3,2,1,0:T(8,128)}, ...), condition=%wide.region_7.8_spmd, body=%wide.region_6.7_spmd.sunk | while | flops 100696064 | bytes 1442889 | solution.py:108
  66.8 3.5 %collective-permute-start.9 = (bf16[2,1,2,128,128]{4,3,2,1,0:T(8,128)(2,1)S(1)}, bf16[2,1,2,128,128]{4,3,2,1,0:T(8,128)(2,1)S(1)}, u32[]{:S(2)}, u32[]{:S(2)}) collective-permute-start(bf16[2,1,2,128,128]{4,3,2,1,0:T(8,128)(2,1)S(1)} %pad_maximum_fusion.4), channel_id=1, source_target_pairs={{0,8},{8,16},{16,24},{24,32},{32,40},{40,48},{48,56},{56,64},{64,7... | collective-permute-start | bytes 393224 | tf_op jit(solution)/shard_map/ppermute | solution.py:18
  74.3 4.8 %collective-permute-start.3 = (bf16[2,1,2,128,128]{4,3,2,1,0:T(8,128)(2,1)S(1)}, bf16[2,1,2,128,128]{4,3,2,1,0:T(8,128)(2,1)S(1)}, u32[]{:S(2)}, u32[]{:S(2)}) collective-permute-start(bf16[2,1,2,128,128]{4,3,2,1,0:T(8,128)(2,1)S(1)} %pad_maximum_fusion.1), channel_id=1, source_target_pairs={{0,16},{8,24},{16,32},{24,40},{32,48},{40,56},{48,64},{56,72},{64,... | collective-permute-start | bytes 393224 | tf_op jit(solution)/shard_map/ppermute | solution.py:18
  79.6 3.0 %collective-permute-start.10 = (bf16[2,1,2,128,128]{4,3,2,1,0:T(8,128)(2,1)S(1)}, bf16[2,1,2,128,128]{4,3,2,1,0:T(8,128)(2,1)S(1)}, u32[]{:S(2)}, u32[]{:S(2)}) collective-permute-start(bf16[2,1,2,128,128]{4,3,2,1,0:T(8,128)(2,1)S(1)} %pad_maximum_fusion.5), channel_id=1, source_target_pairs={{0,16},{8,24},{16,32},{24,40},{32,48},{40,56},{48,64},{56,72},{64,... | collective-permute-start | bytes 393224 | tf_op jit(solution)/shard_map/ppermute | solution.py:18
  82.6 2.1 %collective-permute-done.3 = bf16[2,1,2,128,128]{4,3,2,1,0:T(8,128)(2,1)S(1)} collective-permute-done((bf16[2,1,2,128,128]{4,3,2,1,0:T(8,128)(2,1)S(1)}, bf16[2,1,2,128,128]{4,3,2,1,0:T(8,128)(2,1)S(1)}, u32[]{:S(2)}, u32[]{:S(2)}) %collective-permute-start.3) | collective-permute-done | bytes 131104 | tf_op jit(solution)/shard_map/ppermute | solution.py:18
  87.2 4.0 %collective-permute-done.10 = bf16[2,1,2,128,128]{4,3,2,1,0:T(8,128)(2,1)S(1)} collective-permute-done((bf16[2,1,2,128,128]{4,3,2,1,0:T(8,128)(2,1)S(1)}, bf16[2,1,2,128,128]{4,3,2,1,0:T(8,128)(2,1)S(1)}, u32[]{:S(2)}, u32[]{:S(2)}) %collective-permute-start.10) | collective-permute-done | bytes 131104 | tf_op jit(solution)/shard_map/ppermute | solution.py:18
  94.1 2.3 %collective-permute-start.5 = (bf16[2,1,2,128,128]{4,3,2,1,0:T(8,128)(2,1)S(1)}, bf16[2,1,2,128,128]{4,3,2,1,0:T(8,128)(2,1)S(1)}, u32[]{:S(2)}, u32[]{:S(2)}) collective-permute-start(bf16[2,1,2,128,128]{4,3,2,1,0:T(8,128)(2,1)S(1)} %pad_maximum_fusion.3), channel_id=1, source_target_pairs={{0,64},{8,72},{16,80},{24,88},{32,96},{40,104},{48,112},{56,120},{... | collective-permute-start | bytes 393224 | tf_op jit(solution)/shard_map/ppermute | solution.py:18
  96.4 4.3 %collective-permute-done.11 = bf16[2,1,2,128,128]{4,3,2,1,0:T(8,128)(2,1)S(1)} collective-permute-done((bf16[2,1,2,128,128]{4,3,2,1,0:T(8,128)(2,1)S(1)}, bf16[2,1,2,128,128]{4,3,2,1,0:T(8,128)(2,1)S(1)}, u32[]{:S(2)}, u32[]{:S(2)}) %collective-permute-start.11) | collective-permute-done | bytes 131104 | tf_op jit(solution)/shard_map/ppermute | solution.py:18
  103.0 4.3 %collective-permute-done.5 = bf16[2,1,2,128,128]{4,3,2,1,0:T(8,128)(2,1)S(1)} collective-permute-done((bf16[2,1,2,128,128]{4,3,2,1,0:T(8,128)(2,1)S(1)}, bf16[2,1,2,128,128]{4,3,2,1,0:T(8,128)(2,1)S(1)}, u32[]{:S(2)}, u32[]{:S(2)}) %collective-permute-start.5) | collective-permute-done | bytes 131104 | tf_op jit(solution)/shard_map/ppermute | solution.py:18
  112.2 5.5 %collective-permute-done.6 = bf16[1,2,128,128]{3,2,1,0:T(8,128)(2,1)S(1)} collective-permute-done((bf16[1,2,128,128]{3,2,1,0:T(8,128)(2,1)S(1)}, bf16[1,2,128,128]{3,2,1,0:T(8,128)(2,1)S(1)}, u32[]{:S(2)}, u32[]{:S(2)}) %collective-permute-start.6) | collective-permute-done | bytes 65568 | tf_op jit(solution)/shard_map/ppermute | solution.py:18
  118.0 5.9 %collective-permute-start.7 = (bf16[1,2,128,128]{3,2,1,0:T(8,128)(2,1)S(1)}, bf16[1,2,128,128]{3,2,1,0:T(8,128)(2,1)S(1)}, u32[]{:S(2)}, u32[]{:S(2)}) collective-permute-start(bf16[1,2,128,128]{3,2,1,0:T(8,128)(2,1)S(1)} %fusion.58), channel_id=1, source_target_pairs={{0,8},{8,16},{16,24},{24,32},{32,40},{40,48},{48,56},{56,64},{64,7... | collective-permute-start | bytes 196616 | tf_op jit(solution)/shard_map/ppermute | solution.py:18
  124.7 2.1 %collective-permute-start.14 = (bf16[1,2,128,128]{3,2,1,0:T(8,128)(2,1)}, bf16[1,2,128,128]{3,2,1,0:T(8,128)(2,1)}, u32[]{:S(2)}, u32[]{:S(2)}) collective-permute-start(bf16[1,2,128,128]{3,2,1,0:T(8,128)(2,1)} %fusion.57), channel_id=1, source_target_pairs={{0,8},{8,16},{16,24},{24,32},{32,40},{40,48},{48,56},{56,64},{64,7... | collective-permute-start | bytes 196616 | tf_op jit(solution)/shard_map/ppermute | solution.py:18
  128.2 4.4 %while.49 = (s32[]{:T(128)}, f32[1,2,128,128]{3,2,1,0:T(8,128)S(1)}, f32[2,1,2,128,128]{4,3,2,1,0:T(8,128)}, f32[2,1,2,128,128]{4,3,2,1,0:T(8,128)S(1)}, f32[2,1...) while((s32[]{:T(128)}, ...), condition=%wide.region_5.6_spmd, body=%wide.region_4.5_spmd.sunk | while | flops 100728832 | bytes 1312853 | solution.py:140
  135.4 3.0 %while.51 = (s32[]{:T(128)}, f32[1,2,128,128]{3,2,1,0:T(8,128)S(1)}, f32[2,1,2,128,128]{4,3,2,1,0:T(8,128)S(1)}, f32[2,1,2,128,128]{4,3,2,1,0:T(8,128)S(1)}, f32...) while((s32[]{:T(128)}, ...), condition=%wide.region_9.10_spmd, body=%wide.region_8.9_spmd.sunk | while | flops 100728832 | bytes 1312853 | solution.py:140
  146.9 2.1 %collective-permute-start.17 = (bf16[32,2048]{1,0:T(8,128)(2,1)}, bf16[32,2048]{1,0:T(8,128)(2,1)}, u32[]{:S(2)}, u32[]{:S(2)}) collective-permute-start(bf16[32,2048]{1,0:T(8,128)(2,1)} %get-tuple-element.270), channel_id=1, source_target_pairs={{0,3},{1,4},{2,5},{3,6},{4,7},{5,0},{6,1},{7,2},{8,11},{9,12},{10,... | collective-permute-start | bytes 393224 | tf_op jit(solution)/shard_map/ppermute | solution.py:206
  149.0 2.0 %collective-permute-start.18 = (bf16[32,2048]{1,0:T(8,128)(2,1)}, bf16[32,2048]{1,0:T(8,128)(2,1)}, u32[]{:S(2)}, u32[]{:S(2)}) collective-permute-start(bf16[32,2048]{1,0:T(8,128)(2,1)} %get-tuple-element.269), channel_id=1, source_target_pairs={{0,4},{1,5},{2,6},{3,7},{4,0},{5,1},{6,2},{7,3},{8,12},{9,13},{10,... | collective-permute-start | bytes 393224 | tf_op jit(solution)/shard_map/ppermute | solution.py:206
  156.3 2.3 %collective-permute-done.17 = bf16[32,2048]{1,0:T(8,128)(2,1)} collective-permute-done((bf16[32,2048]{1,0:T(8,128)(2,1)}, bf16[32,2048]{1,0:T(8,128)(2,1)}, u32[]{:S(2)}, u32[]{:S(2)}) %collective-permute-start.17) | collective-permute-done | bytes 131104 | tf_op jit(solution)/shard_map/ppermute | solution.py:206
  161.6 2.0 %fusion.120 = bf16[32,2048]{1,0:T(8,128)(2,1)} fusion(bf16[32,2048]{1,0:T(8,128)(2,1)} %collective-permute-done.21, bf16[32,2048]{1,0:T(8,128)(2,1)} %collective-permute-done.20, bf16[32,2048]{1,0:T(8,128)(2,1)} %collective-permute-done.19, bf16[32,2048]{1,0:T(8,128)(2,1)} %collective-permute-done.18, bf16[32,2048]{1,0:T(8,128)(2,1)} %collective-permute-done.17, ...), kind=kLoop, calls=%fused_computation.184 | loop fusion | flops 1048576 | bytes 1179652 | tf_op jit(solution)/shard_map/convert_element_type | solution.py:207
  (217 shorter events, 95.4 us)
Async XLA Ops:
  0.0 142.8 %copy-start = (bf16[512,2048]{1,0:T(8,128)(2,1)S(1)}, bf16[512,2048]{1,0:T(8,128)(2,1)}, u32[]{:S(2)}) copy-start(bf16[512,2048]{1,0:T(8,128)(2,1)} %param.29) | copy-start | bytes 6291460
  0.8 22.1 %collective-permute-start = (bf16[3,256]{1,0:T(4,128)(2,1)S(1)}, bf16[3,256]{1,0:T(4,128)(2,1)S(1)}, u32[]{:S(2)}, u32[]{:S(2)}) collective-permute-start(bf16[3,256]{1,0:T(4,128)(2,1)S(1)} %slice.116), channel_id=1, source_target_pairs={{0,8},{8,16},{16,24},{24,32},{32,40},{40,48},{48,56},{56,64},{64,7... | collective-permute-start | bytes 4616 | tf_op jit(solution)/shard_map/ppermute | solution.py:18
  5.6 33.6 %collective-permute-start.1 = (bf16[3,512]{1,0:T(4,128)(2,1)}, bf16[3,512]{1,0:T(4,128)(2,1)}, u32[]{:S(2)}, u32[]{:S(2)}) collective-permute-start(bf16[3,512]{1,0:T(4,128)(2,1)} %slice.125), channel_id=1, source_target_pairs={{0,8},{8,16},{16,24},{24,32},{32,40},{40,48},{48,56},{56,64},{64,7... | collective-permute-start | bytes 9224 | tf_op jit(solution)/shard_map/ppermute | solution.py:18
  10.4 26.3 %collective-permute-start.8 = (bf16[3,256]{1,0:T(4,128)(2,1)}, bf16[3,256]{1,0:T(4,128)(2,1)}, u32[]{:S(2)}, u32[]{:S(2)}) collective-permute-start(bf16[3,256]{1,0:T(4,128)(2,1)} %slice.138), channel_id=1, source_target_pairs={{0,8},{8,16},{16,24},{24,32},{32,40},{40,48},{48,56},{56,64},{64,7... | collective-permute-start | bytes 4616 | tf_op jit(solution)/shard_map/ppermute | solution.py:18
  13.6 36.9 %copy-start.4 = (f32[128,128]{1,0:T(8,128)}, f32[128,128]{1,0:T(8,128)S(1)}, u32[]{:S(2)}) copy-start(f32[128,128]{1,0:T(8,128)S(1)} %fusion.220) | copy-start | bytes 196612
  52.5 19.6 %collective-permute-start.2 = (bf16[2,1,2,128,128]{4,3,2,1,0:T(8,128)(2,1)}, bf16[2,1,2,128,128]{4,3,2,1,0:T(8,128)(2,1)}, u32[]{:S(2)}, u32[]{:S(2)}) collective-permute-start(bf16[2,1,2,128,128]{4,3,2,1,0:T(8,128)(2,1)} %pad_maximum_fusion), channel_id=1, source_target_pairs={{0,8},{8,16},{16,24},{24,32},{32,40},{40,48},{48,56},{56,64},{64,7... | collective-permute-start | bytes 393224 | tf_op jit(solution)/shard_map/ppermute | solution.py:18
  66.8 12.4 %collective-permute-start.9 = (bf16[2,1,2,128,128]{4,3,2,1,0:T(8,128)(2,1)S(1)}, bf16[2,1,2,128,128]{4,3,2,1,0:T(8,128)(2,1)S(1)}, u32[]{:S(2)}, u32[]{:S(2)}) collective-permute-start(bf16[2,1,2,128,128]{4,3,2,1,0:T(8,128)(2,1)S(1)} %pad_maximum_fusion.4), channel_id=1, source_target_pairs={{0,8},{8,16},{16,24},{24,32},{32,40},{40,48},{48,56},{56,64},{64,7... | collective-permute-start | bytes 393224 | tf_op jit(solution)/shard_map/ppermute | solution.py:18
  74.3 10.5 %collective-permute-start.3 = (bf16[2,1,2,128,128]{4,3,2,1,0:T(8,128)(2,1)S(1)}, bf16[2,1,2,128,128]{4,3,2,1,0:T(8,128)(2,1)S(1)}, u32[]{:S(2)}, u32[]{:S(2)}) collective-permute-start(bf16[2,1,2,128,128]{4,3,2,1,0:T(8,128)(2,1)S(1)} %pad_maximum_fusion.1), channel_id=1, source_target_pairs={{0,16},{8,24},{16,32},{24,40},{32,48},{40,56},{48,64},{56,72},{64,... | collective-permute-start | bytes 393224 | tf_op jit(solution)/shard_map/ppermute | solution.py:18
  79.6 11.6 %collective-permute-start.10 = (bf16[2,1,2,128,128]{4,3,2,1,0:T(8,128)(2,1)S(1)}, bf16[2,1,2,128,128]{4,3,2,1,0:T(8,128)(2,1)S(1)}, u32[]{:S(2)}, u32[]{:S(2)}) collective-permute-start(bf16[2,1,2,128,128]{4,3,2,1,0:T(8,128)(2,1)S(1)} %pad_maximum_fusion.5), channel_id=1, source_target_pairs={{0,16},{8,24},{16,32},{24,40},{32,48},{40,56},{48,64},{56,72},{64,... | collective-permute-start | bytes 393224 | tf_op jit(solution)/shard_map/ppermute | solution.py:18
  85.3 8.3 %collective-permute-start.4 = (bf16[2,1,2,128,128]{4,3,2,1,0:T(8,128)(2,1)S(1)}, bf16[2,1,2,128,128]{4,3,2,1,0:T(8,128)(2,1)S(1)}, u32[]{:S(2)}, u32[]{:S(2)}) collective-permute-start(bf16[2,1,2,128,128]{4,3,2,1,0:T(8,128)(2,1)S(1)} %pad_maximum_fusion.2), channel_id=1, source_target_pairs={{0,32},{8,40},{16,48},{24,56},{32,64},{40,72},{48,80},{56,88},{64,... | collective-permute-start | bytes 393224 | tf_op jit(solution)/shard_map/ppermute | solution.py:18
  91.7 9.0 %collective-permute-start.11 = (bf16[2,1,2,128,128]{4,3,2,1,0:T(8,128)(2,1)S(1)}, bf16[2,1,2,128,128]{4,3,2,1,0:T(8,128)(2,1)S(1)}, u32[]{:S(2)}, u32[]{:S(2)}) collective-permute-start(bf16[2,1,2,128,128]{4,3,2,1,0:T(8,128)(2,1)S(1)} %pad_maximum_fusion.6), channel_id=1, source_target_pairs={{0,32},{8,40},{16,48},{24,56},{32,64},{40,72},{48,80},{56,88},{64,... | collective-permute-start | bytes 393224 | tf_op jit(solution)/shard_map/ppermute | solution.py:18
  94.1 13.3 %collective-permute-start.5 = (bf16[2,1,2,128,128]{4,3,2,1,0:T(8,128)(2,1)S(1)}, bf16[2,1,2,128,128]{4,3,2,1,0:T(8,128)(2,1)S(1)}, u32[]{:S(2)}, u32[]{:S(2)}) collective-permute-start(bf16[2,1,2,128,128]{4,3,2,1,0:T(8,128)(2,1)S(1)} %pad_maximum_fusion.3), channel_id=1, source_target_pairs={{0,64},{8,72},{16,80},{24,88},{32,96},{40,104},{48,112},{56,120},{... | collective-permute-start | bytes 393224 | tf_op jit(solution)/shard_map/ppermute | solution.py:18
  101.1 9.2 %collective-permute-start.12 = (bf16[2,1,2,128,128]{4,3,2,1,0:T(8,128)(2,1)S(1)}, bf16[2,1,2,128,128]{4,3,2,1,0:T(8,128)(2,1)S(1)}, u32[]{:S(2)}, u32[]{:S(2)}) collective-permute-start(bf16[2,1,2,128,128]{4,3,2,1,0:T(8,128)(2,1)S(1)} %pad_maximum_fusion.7), channel_id=1, source_target_pairs={{0,64},{8,72},{16,80},{24,88},{32,96},{40,104},{48,112},{56,120},{... | collective-permute-start | bytes 393224 | tf_op jit(solution)/shard_map/ppermute | solution.py:18
  107.6 10.2 %collective-permute-start.6 = (bf16[1,2,128,128]{3,2,1,0:T(8,128)(2,1)S(1)}, bf16[1,2,128,128]{3,2,1,0:T(8,128)(2,1)S(1)}, u32[]{:S(2)}, u32[]{:S(2)}) collective-permute-start(bf16[1,2,128,128]{3,2,1,0:T(8,128)(2,1)S(1)} %get-tuple-element.304), channel_id=1, source_target_pairs={{0,128},{8,136},{16,144},{24,152},{32,160},{40,168},{48,176},{56,1... | collective-permute-start | bytes 196616 | tf_op jit(solution)/shard_map/ppermute | solution.py:18
  110.5 13.4 %collective-permute-start.13 = (bf16[1,2,128,128]{3,2,1,0:T(8,128)(2,1)S(1)}, bf16[1,2,128,128]{3,2,1,0:T(8,128)(2,1)S(1)}, u32[]{:S(2)}, u32[]{:S(2)}) collective-permute-start(bf16[1,2,128,128]{3,2,1,0:T(8,128)(2,1)S(1)} %get-tuple-element.302), channel_id=1, source_target_pairs={{0,128},{8,136},{16,144},{24,152},{32,160},{40,168},{48,176},{56,1... | collective-permute-start | bytes 196616 | tf_op jit(solution)/shard_map/ppermute | solution.py:18
  118.0 9.5 %collective-permute-start.7 = (bf16[1,2,128,128]{3,2,1,0:T(8,128)(2,1)S(1)}, bf16[1,2,128,128]{3,2,1,0:T(8,128)(2,1)S(1)}, u32[]{:S(2)}, u32[]{:S(2)}) collective-permute-start(bf16[1,2,128,128]{3,2,1,0:T(8,128)(2,1)S(1)} %fusion.58), channel_id=1, source_target_pairs={{0,8},{8,16},{16,24},{24,32},{32,40},{40,48},{48,56},{56,64},{64,7... | collective-permute-start | bytes 196616 | tf_op jit(solution)/shard_map/ppermute | solution.py:18
  124.7 9.8 %collective-permute-start.14 = (bf16[1,2,128,128]{3,2,1,0:T(8,128)(2,1)}, bf16[1,2,128,128]{3,2,1,0:T(8,128)(2,1)}, u32[]{:S(2)}, u32[]{:S(2)}) collective-permute-start(bf16[1,2,128,128]{3,2,1,0:T(8,128)(2,1)} %fusion.57), channel_id=1, source_target_pairs={{0,8},{8,16},{16,24},{24,32},{32,40},{40,48},{48,56},{56,64},{64,7... | collective-permute-start | bytes 196616 | tf_op jit(solution)/shard_map/ppermute | solution.py:18
  145.4 7.2 %collective-permute-start.15 = (bf16[32,2048]{1,0:T(8,128)(2,1)S(1)}, bf16[32,2048]{1,0:T(8,128)(2,1)S(1)}, u32[]{:S(2)}, u32[]{:S(2)}) collective-permute-start(bf16[32,2048]{1,0:T(8,128)(2,1)S(1)} %get-tuple-element.265), channel_id=1, source_target_pairs={{0,1},{1,2},{2,3},{3,4},{4,5},{5,6},{6,7},{7,0},{8,9},{9,10},{10,1... | collective-permute-start | bytes 393224 | tf_op jit(solution)/shard_map/ppermute | solution.py:206
  145.4 8.6 %collective-permute-start.16 = (bf16[32,2048]{1,0:T(8,128)(2,1)S(1)}, bf16[32,2048]{1,0:T(8,128)(2,1)S(1)}, u32[]{:S(2)}, u32[]{:S(2)}) collective-permute-start(bf16[32,2048]{1,0:T(8,128)(2,1)S(1)} %get-tuple-element.271), channel_id=1, source_target_pairs={{0,2},{1,3},{2,4},{3,5},{4,6},{5,7},{6,0},{7,1},{8,10},{9,11},{10,... | collective-permute-start | bytes 393224 | tf_op jit(solution)/shard_map/ppermute | solution.py:206
  146.9 11.6 %collective-permute-start.17 = (bf16[32,2048]{1,0:T(8,128)(2,1)}, bf16[32,2048]{1,0:T(8,128)(2,1)}, u32[]{:S(2)}, u32[]{:S(2)}) collective-permute-start(bf16[32,2048]{1,0:T(8,128)(2,1)} %get-tuple-element.270), channel_id=1, source_target_pairs={{0,3},{1,4},{2,5},{3,6},{4,7},{5,0},{6,1},{7,2},{8,11},{9,12},{10,... | collective-permute-start | bytes 393224 | tf_op jit(solution)/shard_map/ppermute | solution.py:206
  149.0 10.7 %collective-permute-start.18 = (bf16[32,2048]{1,0:T(8,128)(2,1)}, bf16[32,2048]{1,0:T(8,128)(2,1)}, u32[]{:S(2)}, u32[]{:S(2)}) collective-permute-start(bf16[32,2048]{1,0:T(8,128)(2,1)} %get-tuple-element.269), channel_id=1, source_target_pairs={{0,4},{1,5},{2,6},{3,7},{4,0},{5,1},{6,2},{7,3},{8,12},{9,13},{10,... | collective-permute-start | bytes 393224 | tf_op jit(solution)/shard_map/ppermute | solution.py:206
  151.0 8.7 %collective-permute-start.19 = (bf16[32,2048]{1,0:T(8,128)(2,1)}, bf16[32,2048]{1,0:T(8,128)(2,1)}, u32[]{:S(2)}, u32[]{:S(2)}) collective-permute-start(bf16[32,2048]{1,0:T(8,128)(2,1)} %get-tuple-element.268), channel_id=1, source_target_pairs={{0,5},{1,6},{2,7},{3,0},{4,1},{5,2},{6,3},{7,4},{8,13},{9,14},{10,... | collective-permute-start | bytes 393224 | tf_op jit(solution)/shard_map/ppermute | solution.py:206
  152.6 8.7 %collective-permute-start.20 = (bf16[32,2048]{1,0:T(8,128)(2,1)S(1)}, bf16[32,2048]{1,0:T(8,128)(2,1)}, u32[]{:S(2)}, u32[]{:S(2)}) collective-permute-start(bf16[32,2048]{1,0:T(8,128)(2,1)S(1)} %get-tuple-element.267), channel_id=1, source_target_pairs={{0,6},{1,7},{2,0},{3,1},{4,2},{5,3},{6,4},{7,5},{8,14},{9,15},{10,... | collective-permute-start | bytes 393224 | tf_op jit(solution)/shard_map/ppermute | solution.py:206
  154.7 6.9 %collective-permute-start.21 = (bf16[32,2048]{1,0:T(8,128)(2,1)S(1)}, bf16[32,2048]{1,0:T(8,128)(2,1)}, u32[]{:S(2)}, u32[]{:S(2)}) collective-permute-start(bf16[32,2048]{1,0:T(8,128)(2,1)S(1)} %get-tuple-element.266), channel_id=1, source_target_pairs={{0,7},{1,0},{2,1},{3,2},{4,3},{5,4},{6,5},{7,6},{8,15},{9,8},{10,9... | collective-permute-start | bytes 393224 | tf_op jit(solution)/shard_map/ppermute | solution.py:206
  (18 other events, 95.7 us)

commit v7 on v6

--- a/solution.py
+++ b/solution.py
@@ -106,7 +106,7 @@
         )
 
     (total_map, local_end), ignored = lax.scan(
-        sweep_spans, (identity, zero_state), (transit_seq, inject_seq)
+        sweep_spans, (identity, zero_state), (transit_seq, inject_seq), unroll=True
     )
 
     seq_size = lax.axis_size("seq")
@@ -141,6 +141,7 @@
         replay,
         incoming,
         (transit_seq, inject_seq, jnp.moveaxis(coupling, 2, 0), jnp.moveaxis(local_out, 2, 0)),
+        unroll=True,
     )
     return outputs
 
@@ -193,16 +194,20 @@
     scale_rows = lax.rsqrt(jnp.mean(core_out * core_out, axis=-1, keepdims=True) + epsilon)
     normed = core_out * scale_rows * norm_gain.astype(jnp.float32) * jax.nn.silu(gate_values)
     hidden = normed.reshape(local_rows, value_heads * DV).astype(jnp.bfloat16)
-    partial_sum = jnp.dot(hidden, out_weight, preferred_element_type=jnp.float32).astype(
-        jnp.bfloat16
-    )
+    partial_sum = jnp.dot(hidden, out_weight, preferred_element_type=jnp.float32)
     head_size = lax.axis_size("head")
     head_index = lax.axis_index("head")
-    pieces = partial_sum.reshape(head_size, local_rows // head_size, partial_sum.shape[1])
-    summed = pieces[head_index].astype(jnp.float32)
-    for hop in range(1, head_size):
-        outgoing = pieces[(head_index + hop) % head_size]
-        pairs = [(i, (i + hop) % head_size) for i in range(head_size)]
+    chips = head_size // 2
+    pieces = partial_sum.reshape(chips, 2, local_rows // head_size, partial_sum.shape[1])
+    parity = head_index % 2
+    chip = head_index // 2
+    sibling_pairs = [(i, i ^ 1) for i in range(head_size)]
+    from_sibling = lax.ppermute(pieces[:, 1 - parity].astype(jnp.bfloat16), "head", sibling_pairs)
+    chip_sum = (pieces[:, parity] + from_sibling.astype(jnp.float32)).astype(jnp.bfloat16)
+    summed = chip_sum[chip].astype(jnp.float32)
+    for hop in range(1, chips):
+        outgoing = chip_sum[(chip + hop) % chips]
+        pairs = [(i, (i + 2 * hop) % head_size) for i in range(head_size)]
         summed = summed + lax.ppermute(outgoing, "head", pairs).astype(jnp.float32)
     return summed.astype(jnp.bfloat16)
 

time: 167 us -> 135 us (0.81); the launches traced: 164 us -> 134 us
  matrix products: 38.7 us -> 25.7 us
  local copies, waits for them, and re-layouts: 24.5 us -> 13.7 us
  waiting for transfers between devices: 29.5 us -> 36.5 us
  starting transfers between devices: 53 us -> 47 us
  other arithmetic: 16.4 us -> 10.4 us
    ppermute x15, waiting for transfers between devices: 24.2 us -> 29.8 us  [shifted(): return lax.ppermute(array, axis, pairs)]
    dot_general x4, matrix products: 6.2 us -> 1.33 us  [replay(): jnp.einsum('hrck,hrkv->hrcv', coupling_now, state_now, precision=highest)]
    ppermute x7 -> x3, starting transfers between devices: 10.2 us -> 5.74 us  [shards(): summed = summed + lax.ppermute(outgoing, 'head', pairs).astype(jnp.float32)]
    dot_general x30 -> x28, matrix products: 10.5 us -> 6.13 us  [apply_map(): return jnp.einsum('hrke,hrev->hrkv', matrix, state_now, precision=highest)]
    while x16 -> x0, local copies, waits for them, and re-layouts: 1.99 us -> none
    transpose x1, local copies, waits for them, and re-layouts: 1.89 us -> 0.04 us  [relay_group(): jnp.moveaxis(local_out, 2, 0)]
    ppermute x0 -> x1, waiting for transfers between devices: none -> 1.81 us  [shards(): lax.ppermute(pieces[:, 1 - parity].astype(jnp.bfloat16), 'head', sibling_...]
    ppermute x7 -> x3, waiting for transfers between devices: 5.33 us -> 4.89 us  [shards(): summed = summed + lax.ppermute(outgoing, 'head', pairs).astype(jnp.float32)]
  transfers between devices with their start and end apart: 22 -> 19, of which waited for: 12 -> 13; matrix products, arithmetic and copies ran while one was open for 32% -> 24% of each run, Pallas kernels for 0% -> 0%
where the time goes in v7:
time: 135 us; the launch traced here: 134 us
  starting transfers between devices  47 us (35%)
  waiting for transfers between devices  36.5 us (27%)
  matrix products  25.7 us (19%)
  local copies, waits for them, and re-layouts  13.7 us (10%)
  other arithmetic  10.4 us (8%)
    ppermute x15, starting transfers between devices, shifted(): return lax.ppermute(array, axis, pairs)  41.1 us
    ppermute x15, waiting for transfers between devices, shifted(): return lax.ppermute(array, axis, pairs)  29.8 us
    dot_general x7, matrix products, unit_lower_inverse(): jnp.einsum('...ij,...jk->...ik', inverse, coupling, precision=highest)  6.22 us
    dot_general x28, matrix products, apply_map(): return jnp.einsum('hrke,hrev->hrkv', matrix, state_now, precision=highest)  6.13 us
    ppermute x3, starting transfers between devices, shards(): summed = summed + lax.ppermute(outgoing, 'head', pairs).astype(jnp.float32)  5.74 us
    ppermute x3, waiting for transfers between devices, shards(): summed = summed + lax.ppermute(outgoing, 'head', pairs).astype(jnp.float32)  4.89 us
    dot_general x7, matrix products, unit_lower_inverse(): jnp.einsum('...ij,...jk->...ik', jnp.einsum('...ij,...jk->...ik', inverse...  4.69 us
    slice x3, local copies, waits for them, and re-layouts, conv_silu(): summed = summed + conv_taps[offset] * padded[offset:offset + length]  3.1 us
  transfers between devices with their start and end apart: 19, of which 13 were waited for; matrix products, arithmetic and copies ran while one was open for 24% of the time, Pallas kernels for 0%

profile of v7, /device:TPU:128, one launch (start us, length us, event | category | flops | bytes accessed | tf_op | source)
XLA Modules:
  0.0 134.4 jit_solution(12803342481403309376)
XLA Ops:
  0.8 3.5 %collective-permute-start.1 = (bf16[3,256]{1,0:T(4,128)(2,1)S(1)}, bf16[3,256]{1,0:T(4,128)(2,1)S(1)}, u32[]{:S(2)}, u32[]{:S(2)}) collective-permute-start(bf16[3,256]{1,0:T(4,128)(2,1)S(1)} %slice.176), channel_id=1, source_target_pairs={{0,8},{8,16},{16,24},{24,32},{32,40},{40,48},{48,56},{56,64},{64,7... | collective-permute-start | bytes 4616 | tf_op jit(solution)/shard_map/ppermute | solution.py:18
  5.6 3.5 %collective-permute-start.2 = (bf16[3,512]{1,0:T(4,128)(2,1)}, bf16[3,512]{1,0:T(4,128)(2,1)S(1)}, u32[]{:S(2)}, u32[]{:S(2)}) collective-permute-start(bf16[3,512]{1,0:T(4,128)(2,1)} %slice.185), channel_id=1, source_target_pairs={{0,8},{8,16},{16,24},{24,32},{32,40},{40,48},{48,56},{56,64},{64,7... | collective-permute-start | bytes 9224 | tf_op jit(solution)/shard_map/ppermute | solution.py:18
  9.8 3.2 %collective-permute-start = (bf16[3,256]{1,0:T(4,128)(2,1)S(1)}, bf16[3,256]{1,0:T(4,128)(2,1)S(1)}, u32[]{:S(2)}, u32[]{:S(2)}) collective-permute-start(bf16[3,256]{1,0:T(4,128)(2,1)S(1)} %slice.167), channel_id=1, source_target_pairs={{0,8},{8,16},{16,24},{24,32},{32,40},{40,48},{48,56},{56,64},{64,7... | collective-permute-start | bytes 4616 | tf_op jit(solution)/shard_map/ppermute | solution.py:18
  37.6 2.2 %reshape.1164 = f32[2,128,2,2,128]{4,3,2,1,0:T(2,128)} reshape(f32[256,512]{1,0:T(8,128)} %divide_multiply_fusion) | data formatting | bytes 1048576 | tf_op jit(solution)/shard_map/reshape | solution.py:183
  45.8 2.6 %collective-permute-start.3 = (bf16[2,1,2,128,128]{4,3,2,1,0:T(8,128)(2,1)S(1)}, bf16[2,1,2,128,128]{4,3,2,1,0:T(8,128)(2,1)S(1)}, u32[]{:S(2)}, u32[]{:S(2)}) collective-permute-start(bf16[2,1,2,128,128]{4,3,2,1,0:T(8,128)(2,1)S(1)} %pad_maximum_fusion), channel_id=1, source_target_pairs={{0,8},{8,16},{16,24},{24,32},{32,40},{40,48},{48,56},{56,64},{64,7... | collective-permute-start | bytes 393224 | tf_op jit(solution)/shard_map/ppermute | solution.py:18
  51.7 3.5 %collective-permute-start.9 = (bf16[2,1,2,128,128]{4,3,2,1,0:T(8,128)(2,1)S(1)}, bf16[2,1,2,128,128]{4,3,2,1,0:T(8,128)(2,1)S(1)}, u32[]{:S(2)}, u32[]{:S(2)}) collective-permute-start(bf16[2,1,2,128,128]{4,3,2,1,0:T(8,128)(2,1)S(1)} %pad_maximum_fusion.4), channel_id=1, source_target_pairs={{0,8},{8,16},{16,24},{24,32},{32,40},{40,48},{48,56},{56,64},{64,7... | collective-permute-start | bytes 393224 | tf_op jit(solution)/shard_map/ppermute | solution.py:18
  56.5 4.0 %collective-permute-start.4 = (bf16[2,1,2,128,128]{4,3,2,1,0:T(8,128)(2,1)S(1)}, bf16[2,1,2,128,128]{4,3,2,1,0:T(8,128)(2,1)S(1)}, u32[]{:S(2)}, u32[]{:S(2)}) collective-permute-start(bf16[2,1,2,128,128]{4,3,2,1,0:T(8,128)(2,1)S(1)} %pad_maximum_fusion.1), channel_id=1, source_target_pairs={{0,16},{8,24},{16,32},{24,40},{32,48},{40,56},{48,64},{56,72},{64,... | collective-permute-start | bytes 393224 | tf_op jit(solution)/shard_map/ppermute | solution.py:18
  62.3 1.9 %collective-permute-start.10 = (bf16[2,1,2,128,128]{4,3,2,1,0:T(8,128)(2,1)S(1)}, bf16[2,1,2,128,128]{4,3,2,1,0:T(8,128)(2,1)S(1)}, u32[]{:S(2)}, u32[]{:S(2)}) collective-permute-start(bf16[2,1,2,128,128]{4,3,2,1,0:T(8,128)(2,1)S(1)} %pad_maximum_fusion.5), channel_id=1, source_target_pairs={{0,16},{8,24},{16,32},{24,40},{32,48},{40,56},{48,64},{56,72},{64,... | collective-permute-start | bytes 393224 | tf_op jit(solution)/shard_map/ppermute | solution.py:18
  64.3 2.7 %collective-permute-done.4 = bf16[2,1,2,128,128]{4,3,2,1,0:T(8,128)(2,1)S(1)} collective-permute-done((bf16[2,1,2,128,128]{4,3,2,1,0:T(8,128)(2,1)S(1)}, bf16[2,1,2,128,128]{4,3,2,1,0:T(8,128)(2,1)S(1)}, u32[]{:S(2)}, u32[]{:S(2)}) %collective-permute-start.4) | collective-permute-done | bytes 131104 | tf_op jit(solution)/shard_map/ppermute | solution.py:18
  67.4 1.9 %collective-permute-start.5 = (bf16[2,1,2,128,128]{4,3,2,1,0:T(8,128)(2,1)S(1)}, bf16[2,1,2,128,128]{4,3,2,1,0:T(8,128)(2,1)S(1)}, u32[]{:S(2)}, u32[]{:S(2)}) collective-permute-start(bf16[2,1,2,128,128]{4,3,2,1,0:T(8,128)(2,1)S(1)} %pad_maximum_fusion.2), channel_id=1, source_target_pairs={{0,32},{8,40},{16,48},{24,56},{32,64},{40,72},{48,80},{56,88},{64,... | collective-permute-start | bytes 393224 | tf_op jit(solution)/shard_map/ppermute | solution.py:18
  69.4 3.9 %collective-permute-done.10 = bf16[2,1,2,128,128]{4,3,2,1,0:T(8,128)(2,1)S(1)} collective-permute-done((bf16[2,1,2,128,128]{4,3,2,1,0:T(8,128)(2,1)S(1)}, bf16[2,1,2,128,128]{4,3,2,1,0:T(8,128)(2,1)S(1)}, u32[]{:S(2)}, u32[]{:S(2)}) %collective-permute-start.10) | collective-permute-done | bytes 131104 | tf_op jit(solution)/shard_map/ppermute | solution.py:18
  73.7 1.9 %collective-permute-start.11 = (bf16[2,1,2,128,128]{4,3,2,1,0:T(8,128)(2,1)S(1)}, bf16[2,1,2,128,128]{4,3,2,1,0:T(8,128)(2,1)S(1)}, u32[]{:S(2)}, u32[]{:S(2)}) collective-permute-start(bf16[2,1,2,128,128]{4,3,2,1,0:T(8,128)(2,1)S(1)} %pad_maximum_fusion.6), channel_id=1, source_target_pairs={{0,32},{8,40},{16,48},{24,56},{32,64},{40,72},{48,80},{56,88},{64,... | collective-permute-start | bytes 393224 | tf_op jit(solution)/shard_map/ppermute | solution.py:18
  76.1 2.1 %collective-permute-start.6 = (bf16[2,1,2,128,128]{4,3,2,1,0:T(8,128)(2,1)S(1)}, bf16[2,1,2,128,128]{4,3,2,1,0:T(8,128)(2,1)S(1)}, u32[]{:S(2)}, u32[]{:S(2)}) collective-permute-start(bf16[2,1,2,128,128]{4,3,2,1,0:T(8,128)(2,1)S(1)} %pad_maximum_fusion.3), channel_id=1, source_target_pairs={{0,64},{8,72},{16,80},{24,88},{32,96},{40,104},{48,112},{56,120},{... | collective-permute-start | bytes 393224 | tf_op jit(solution)/shard_map/ppermute | solution.py:18
  78.2 4.5 %collective-permute-done.11 = bf16[2,1,2,128,128]{4,3,2,1,0:T(8,128)(2,1)S(1)} collective-permute-done((bf16[2,1,2,128,128]{4,3,2,1,0:T(8,128)(2,1)S(1)}, bf16[2,1,2,128,128]{4,3,2,1,0:T(8,128)(2,1)S(1)}, u32[]{:S(2)}, u32[]{:S(2)}) %collective-permute-start.11) | collective-permute-done | bytes 131104 | tf_op jit(solution)/shard_map/ppermute | solution.py:18
  83.3 1.9 %collective-permute-start.12 = (bf16[2,1,2,128,128]{4,3,2,1,0:T(8,128)(2,1)S(1)}, bf16[2,1,2,128,128]{4,3,2,1,0:T(8,128)(2,1)S(1)}, u32[]{:S(2)}, u32[]{:S(2)}) collective-permute-start(bf16[2,1,2,128,128]{4,3,2,1,0:T(8,128)(2,1)S(1)} %pad_maximum_fusion.7), channel_id=1, source_target_pairs={{0,64},{8,72},{16,80},{24,88},{32,96},{40,104},{48,112},{56,120},{... | collective-permute-start | bytes 393224 | tf_op jit(solution)/shard_map/ppermute | solution.py:18
  85.2 3.0 %collective-permute-done.6 = bf16[2,1,2,128,128]{4,3,2,1,0:T(8,128)(2,1)S(1)} collective-permute-done((bf16[2,1,2,128,128]{4,3,2,1,0:T(8,128)(2,1)S(1)}, bf16[2,1,2,128,128]{4,3,2,1,0:T(8,128)(2,1)S(1)}, u32[]{:S(2)}, u32[]{:S(2)}) %collective-permute-start.6) | collective-permute-done | bytes 131104 | tf_op jit(solution)/shard_map/ppermute | solution.py:18
  89.7 3.8 %collective-permute-done.12 = bf16[2,1,2,128,128]{4,3,2,1,0:T(8,128)(2,1)S(1)} collective-permute-done((bf16[2,1,2,128,128]{4,3,2,1,0:T(8,128)(2,1)S(1)}, bf16[2,1,2,128,128]{4,3,2,1,0:T(8,128)(2,1)S(1)}, u32[]{:S(2)}, u32[]{:S(2)}) %collective-permute-start.12) | collective-permute-done | bytes 131104 | tf_op jit(solution)/shard_map/ppermute | solution.py:18
  95.7 2.8 %collective-permute-done.7 = bf16[1,2,128,128]{3,2,1,0:T(8,128)(2,1)S(1)} collective-permute-done((bf16[1,2,128,128]{3,2,1,0:T(8,128)(2,1)S(1)}, bf16[1,2,128,128]{3,2,1,0:T(8,128)(2,1)S(1)}, u32[]{:S(2)}, u32[]{:S(2)}) %collective-permute-start.7) | collective-permute-done | bytes 65568 | tf_op jit(solution)/shard_map/ppermute | solution.py:18
  98.7 6.4 %collective-permute-start.8 = (bf16[1,2,128,128]{3,2,1,0:T(8,128)(2,1)S(1)}, bf16[1,2,128,128]{3,2,1,0:T(8,128)(2,1)S(1)}, u32[]{:S(2)}, u32[]{:S(2)}) collective-permute-start(bf16[1,2,128,128]{3,2,1,0:T(8,128)(2,1)S(1)} %fusion.16), channel_id=1, source_target_pairs={{0,8},{8,16},{16,24},{24,32},{32,40},{40,48},{48,56},{56,64},{64,7... | collective-permute-start | bytes 196616 | tf_op jit(solution)/shard_map/ppermute | solution.py:18
  105.4 1.9 %collective-permute-start.14 = (bf16[1,2,128,128]{3,2,1,0:T(8,128)(2,1)S(1)}, bf16[1,2,128,128]{3,2,1,0:T(8,128)(2,1)S(1)}, u32[]{:S(2)}, u32[]{:S(2)}) collective-permute-start(bf16[1,2,128,128]{3,2,1,0:T(8,128)(2,1)S(1)} %fusion.15), channel_id=1, source_target_pairs={{0,8},{8,16},{16,24},{24,32},{32,40},{40,48},{48,56},{56,64},{64,7... | collective-permute-start | bytes 196616 | tf_op jit(solution)/shard_map/ppermute | solution.py:18
  108.8 6.1 %collective-permute-done.14 = bf16[1,2,128,128]{3,2,1,0:T(8,128)(2,1)S(1)} collective-permute-done((bf16[1,2,128,128]{3,2,1,0:T(8,128)(2,1)S(1)}, bf16[1,2,128,128]{3,2,1,0:T(8,128)(2,1)S(1)}, u32[]{:S(2)}, u32[]{:S(2)}) %collective-permute-start.14) | collective-permute-done | bytes 65568 | tf_op jit(solution)/shard_map/ppermute | solution.py:18
  119.9 1.8 %collective-permute-done.15 = bf16[4,32,2048]{2,1,0:T(8,128)(2,1)S(1)} collective-permute-done((bf16[4,32,2048]{2,1,0:T(8,128)(2,1)S(1)}, bf16[4,32,2048]{2,1,0:T(8,128)(2,1)S(1)}, u32[]{:S(2)}, u32[]{:S(2)}) %collective-permute-start.15) | collective-permute-done | bytes 524320 | tf_op jit(solution)/shard_map/ppermute | solution.py:205
  124.7 2.7 %collective-permute-start.17 = (bf16[32,2048]{1,0:T(8,128)(2,1)S(1)}, bf16[32,2048]{1,0:T(8,128)(2,1)S(1)}, u32[]{:S(2)}, u32[]{:S(2)}) collective-permute-start(bf16[32,2048]{1,0:T(8,128)(2,1)S(1)} %get-tuple-element.11), channel_id=1, source_target_pairs={{0,4},{1,5},{2,6},{3,7},{4,0},{5,1},{6,2},{7,3},{8,12},{9,13},{10,... | collective-permute-start | bytes 393224 | tf_op jit(solution)/shard_map/ppermute | solution.py:211
  129.9 3.8 %collective-permute-done.17 = bf16[32,2048]{1,0:T(8,128)(2,1)S(1)} collective-permute-done((bf16[32,2048]{1,0:T(8,128)(2,1)S(1)}, bf16[32,2048]{1,0:T(8,128)(2,1)S(1)}, u32[]{:S(2)}, u32[]{:S(2)}) %collective-permute-start.17) | collective-permute-done | bytes 131104 | tf_op jit(solution)/shard_map/ppermute | solution.py:211
  (158 shorter events, 57.6 us)
Async XLA Ops:
  0.0 117.6 %copy-start = (bf16[512,2048]{1,0:T(8,128)(2,1)S(1)}, bf16[512,2048]{1,0:T(8,128)(2,1)}, u32[]{:S(2)}) copy-start(bf16[512,2048]{1,0:T(8,128)(2,1)} %param.21) | copy-start | bytes 6291460
  0.8 19.1 %collective-permute-start.1 = (bf16[3,256]{1,0:T(4,128)(2,1)S(1)}, bf16[3,256]{1,0:T(4,128)(2,1)S(1)}, u32[]{:S(2)}, u32[]{:S(2)}) collective-permute-start(bf16[3,256]{1,0:T(4,128)(2,1)S(1)} %slice.176), channel_id=1, source_target_pairs={{0,8},{8,16},{16,24},{24,32},{32,40},{40,48},{48,56},{56,64},{64,7... | collective-permute-start | bytes 4616 | tf_op jit(solution)/shard_map/ppermute | solution.py:18
  5.6 29.8 %collective-permute-start.2 = (bf16[3,512]{1,0:T(4,128)(2,1)}, bf16[3,512]{1,0:T(4,128)(2,1)S(1)}, u32[]{:S(2)}, u32[]{:S(2)}) collective-permute-start(bf16[3,512]{1,0:T(4,128)(2,1)} %slice.185), channel_id=1, source_target_pairs={{0,8},{8,16},{16,24},{24,32},{32,40},{40,48},{48,56},{56,64},{64,7... | collective-permute-start | bytes 9224 | tf_op jit(solution)/shard_map/ppermute | solution.py:18
  9.8 23.9 %collective-permute-start = (bf16[3,256]{1,0:T(4,128)(2,1)S(1)}, bf16[3,256]{1,0:T(4,128)(2,1)S(1)}, u32[]{:S(2)}, u32[]{:S(2)}) collective-permute-start(bf16[3,256]{1,0:T(4,128)(2,1)S(1)} %slice.167), channel_id=1, source_target_pairs={{0,8},{8,16},{16,24},{24,32},{32,40},{40,48},{48,56},{56,64},{64,7... | collective-permute-start | bytes 4616 | tf_op jit(solution)/shard_map/ppermute | solution.py:18
  31.9 1.8 %copy-start.4 = (bf16[256,256]{1,0:T(8,128)(2,1)S(1)}, bf16[256,256]{1,0:T(8,128)(2,1)}, u32[]{:S(2)}) copy-start(bf16[256,256]{1,0:T(8,128)(2,1)} %param.11) | copy-start | bytes 393220
  31.9 1.8 %copy-start.5 = (f32[1,256]{1,0:T(1,128)S(1)}, f32[1,256]{1,0:T(1,128)}, u32[]{:S(2)}) copy-start(f32[1,256]{1,0:T(1,128)} %get-tuple-element.32) | copy-start | bytes 3076
  45.2 4.4 %copy-start.2 = (f32[2,128,2,128]{3,1,0,2:T(8,128)S(1)}, f32[2,128,2,128]{3,1,0,2:T(8,128)}, u32[]{:S(2)}) copy-start(f32[2,128,2,128]{3,1,0,2:T(8,128)} %copy.91) | copy-start | bytes 786436
  45.8 10.2 %collective-permute-start.3 = (bf16[2,1,2,128,128]{4,3,2,1,0:T(8,128)(2,1)S(1)}, bf16[2,1,2,128,128]{4,3,2,1,0:T(8,128)(2,1)S(1)}, u32[]{:S(2)}, u32[]{:S(2)}) collective-permute-start(bf16[2,1,2,128,128]{4,3,2,1,0:T(8,128)(2,1)S(1)} %pad_maximum_fusion), channel_id=1, source_target_pairs={{0,8},{8,16},{16,24},{24,32},{32,40},{40,48},{48,56},{56,64},{64,7... | collective-permute-start | bytes 393224 | tf_op jit(solution)/shard_map/ppermute | solution.py:18
  51.7 10.2 %collective-permute-start.9 = (bf16[2,1,2,128,128]{4,3,2,1,0:T(8,128)(2,1)S(1)}, bf16[2,1,2,128,128]{4,3,2,1,0:T(8,128)(2,1)S(1)}, u32[]{:S(2)}, u32[]{:S(2)}) collective-permute-start(bf16[2,1,2,128,128]{4,3,2,1,0:T(8,128)(2,1)S(1)} %pad_maximum_fusion.4), channel_id=1, source_target_pairs={{0,8},{8,16},{16,24},{24,32},{32,40},{40,48},{48,56},{56,64},{64,7... | collective-permute-start | bytes 393224 | tf_op jit(solution)/shard_map/ppermute | solution.py:18
  56.5 10.5 %collective-permute-start.4 = (bf16[2,1,2,128,128]{4,3,2,1,0:T(8,128)(2,1)S(1)}, bf16[2,1,2,128,128]{4,3,2,1,0:T(8,128)(2,1)S(1)}, u32[]{:S(2)}, u32[]{:S(2)}) collective-permute-start(bf16[2,1,2,128,128]{4,3,2,1,0:T(8,128)(2,1)S(1)} %pad_maximum_fusion.1), channel_id=1, source_target_pairs={{0,16},{8,24},{16,32},{24,40},{32,48},{40,56},{48,64},{56,72},{64,... | collective-permute-start | bytes 393224 | tf_op jit(solution)/shard_map/ppermute | solution.py:18
  62.3 10.9 %collective-permute-start.10 = (bf16[2,1,2,128,128]{4,3,2,1,0:T(8,128)(2,1)S(1)}, bf16[2,1,2,128,128]{4,3,2,1,0:T(8,128)(2,1)S(1)}, u32[]{:S(2)}, u32[]{:S(2)}) collective-permute-start(bf16[2,1,2,128,128]{4,3,2,1,0:T(8,128)(2,1)S(1)} %pad_maximum_fusion.5), channel_id=1, source_target_pairs={{0,16},{8,24},{16,32},{24,40},{32,48},{40,56},{48,64},{56,72},{64,... | collective-permute-start | bytes 393224 | tf_op jit(solution)/shard_map/ppermute | solution.py:18
  67.4 8.2 %collective-permute-start.5 = (bf16[2,1,2,128,128]{4,3,2,1,0:T(8,128)(2,1)S(1)}, bf16[2,1,2,128,128]{4,3,2,1,0:T(8,128)(2,1)S(1)}, u32[]{:S(2)}, u32[]{:S(2)}) collective-permute-start(bf16[2,1,2,128,128]{4,3,2,1,0:T(8,128)(2,1)S(1)} %pad_maximum_fusion.2), channel_id=1, source_target_pairs={{0,32},{8,40},{16,48},{24,56},{32,64},{40,72},{48,80},{56,88},{64,... | collective-permute-start | bytes 393224 | tf_op jit(solution)/shard_map/ppermute | solution.py:18
  73.7 9.1 %collective-permute-start.11 = (bf16[2,1,2,128,128]{4,3,2,1,0:T(8,128)(2,1)S(1)}, bf16[2,1,2,128,128]{4,3,2,1,0:T(8,128)(2,1)S(1)}, u32[]{:S(2)}, u32[]{:S(2)}) collective-permute-start(bf16[2,1,2,128,128]{4,3,2,1,0:T(8,128)(2,1)S(1)} %pad_maximum_fusion.6), channel_id=1, source_target_pairs={{0,32},{8,40},{16,48},{24,56},{32,64},{40,72},{48,80},{56,88},{64,... | collective-permute-start | bytes 393224 | tf_op jit(solution)/shard_map/ppermute | solution.py:18
  76.1 12.1 %collective-permute-start.6 = (bf16[2,1,2,128,128]{4,3,2,1,0:T(8,128)(2,1)S(1)}, bf16[2,1,2,128,128]{4,3,2,1,0:T(8,128)(2,1)S(1)}, u32[]{:S(2)}, u32[]{:S(2)}) collective-permute-start(bf16[2,1,2,128,128]{4,3,2,1,0:T(8,128)(2,1)S(1)} %pad_maximum_fusion.3), channel_id=1, source_target_pairs={{0,64},{8,72},{16,80},{24,88},{32,96},{40,104},{48,112},{56,120},{... | collective-permute-start | bytes 393224 | tf_op jit(solution)/shard_map/ppermute | solution.py:18
  83.3 10.3 %collective-permute-start.12 = (bf16[2,1,2,128,128]{4,3,2,1,0:T(8,128)(2,1)S(1)}, bf16[2,1,2,128,128]{4,3,2,1,0:T(8,128)(2,1)S(1)}, u32[]{:S(2)}, u32[]{:S(2)}) collective-permute-start(bf16[2,1,2,128,128]{4,3,2,1,0:T(8,128)(2,1)S(1)} %pad_maximum_fusion.7), channel_id=1, source_target_pairs={{0,64},{8,72},{16,80},{24,88},{32,96},{40,104},{48,112},{56,120},{... | collective-permute-start | bytes 393224 | tf_op jit(solution)/shard_map/ppermute | solution.py:18
  88.4 10.1 %collective-permute-start.7 = (bf16[1,2,128,128]{3,2,1,0:T(8,128)(2,1)S(1)}, bf16[1,2,128,128]{3,2,1,0:T(8,128)(2,1)S(1)}, u32[]{:S(2)}, u32[]{:S(2)}) collective-permute-start(bf16[1,2,128,128]{3,2,1,0:T(8,128)(2,1)S(1)} %convert_bitcast_fusion.9), channel_id=1, source_target_pairs={{0,128},{8,136},{16,144},{24,152},{32,160},{40,168},{48,176},{56,1... | collective-permute-start | bytes 196616 | tf_op jit(solution)/shard_map/ppermute | solution.py:18
  93.8 11.4 %collective-permute-start.13 = (bf16[1,2,128,128]{3,2,1,0:T(8,128)(2,1)S(1)}, bf16[1,2,128,128]{3,2,1,0:T(8,128)(2,1)S(1)}, u32[]{:S(2)}, u32[]{:S(2)}) collective-permute-start(bf16[1,2,128,128]{3,2,1,0:T(8,128)(2,1)S(1)} %convert_bitcast_fusion), channel_id=1, source_target_pairs={{0,128},{8,136},{16,144},{24,152},{32,160},{40,168},{48,176},{56,1... | collective-permute-start | bytes 196616 | tf_op jit(solution)/shard_map/ppermute | solution.py:18
  98.7 9.5 %collective-permute-start.8 = (bf16[1,2,128,128]{3,2,1,0:T(8,128)(2,1)S(1)}, bf16[1,2,128,128]{3,2,1,0:T(8,128)(2,1)S(1)}, u32[]{:S(2)}, u32[]{:S(2)}) collective-permute-start(bf16[1,2,128,128]{3,2,1,0:T(8,128)(2,1)S(1)} %fusion.16), channel_id=1, source_target_pairs={{0,8},{8,16},{16,24},{24,32},{32,40},{40,48},{48,56},{56,64},{64,7... | collective-permute-start | bytes 196616 | tf_op jit(solution)/shard_map/ppermute | solution.py:18
  105.4 9.5 %collective-permute-start.14 = (bf16[1,2,128,128]{3,2,1,0:T(8,128)(2,1)S(1)}, bf16[1,2,128,128]{3,2,1,0:T(8,128)(2,1)S(1)}, u32[]{:S(2)}, u32[]{:S(2)}) collective-permute-start(bf16[1,2,128,128]{3,2,1,0:T(8,128)(2,1)S(1)} %fusion.15), channel_id=1, source_target_pairs={{0,8},{8,16},{16,24},{24,32},{32,40},{40,48},{48,56},{56,64},{64,7... | collective-permute-start | bytes 196616 | tf_op jit(solution)/shard_map/ppermute | solution.py:18
  118.3 1.3 copy-start.1
  119.7 2.0 %collective-permute-start.15 = (bf16[4,32,2048]{2,1,0:T(8,128)(2,1)S(1)}, bf16[4,32,2048]{2,1,0:T(8,128)(2,1)S(1)}, u32[]{:S(2)}, u32[]{:S(2)}) collective-permute-start(bf16[4,32,2048]{2,1,0:T(8,128)(2,1)S(1)} %fusion.26), channel_id=1, source_target_pairs={{0,1},{1,0},{2,3},{3,2},{4,5},{5,4},{6,7},{7,6},{8,9},{9,8},{10,11... | collective-permute-start | bytes 1572872 | tf_op jit(solution)/shard_map/ppermute | solution.py:205
  123.1 6.8 %collective-permute-start.16 = (bf16[32,2048]{1,0:T(8,128)(2,1)S(1)}, bf16[32,2048]{1,0:T(8,128)(2,1)S(1)}, u32[]{:S(2)}, u32[]{:S(2)}) collective-permute-start(bf16[32,2048]{1,0:T(8,128)(2,1)S(1)} %get-tuple-element.9), channel_id=1, source_target_pairs={{0,2},{1,3},{2,4},{3,5},{4,6},{5,7},{6,0},{7,1},{8,10},{9,11},{10,... | collective-permute-start | bytes 393224 | tf_op jit(solution)/shard_map/ppermute | solution.py:211
  124.7 9.0 %collective-permute-start.17 = (bf16[32,2048]{1,0:T(8,128)(2,1)S(1)}, bf16[32,2048]{1,0:T(8,128)(2,1)S(1)}, u32[]{:S(2)}, u32[]{:S(2)}) collective-permute-start(bf16[32,2048]{1,0:T(8,128)(2,1)S(1)} %get-tuple-element.11), channel_id=1, source_target_pairs={{0,4},{1,5},{2,6},{3,7},{4,0},{5,1},{6,2},{7,3},{8,12},{9,13},{10,... | collective-permute-start | bytes 393224 | tf_op jit(solution)/shard_map/ppermute | solution.py:211
  127.4 6.3 %collective-permute-start.18 = (bf16[32,2048]{1,0:T(8,128)(2,1)S(1)}, bf16[32,2048]{1,0:T(8,128)(2,1)S(1)}, u32[]{:S(2)}, u32[]{:S(2)}) collective-permute-start(bf16[32,2048]{1,0:T(8,128)(2,1)S(1)} %get-tuple-element.10), channel_id=1, source_target_pairs={{0,6},{1,7},{2,0},{3,1},{4,2},{5,3},{6,4},{7,5},{8,14},{9,15},{10,... | collective-permute-start | bytes 393224 | tf_op jit(solution)/shard_map/ppermute | solution.py:211
  (1 other events, 1.3 us)

commit v8 on v7

--- a/solution.py
+++ b/solution.py
@@ -161,15 +161,23 @@
 ):
     local_rows = query_proj.shape[0]
     rim_width = conv_query.shape[0] - 1
-    before_query, before_key, before_value = shifted(
-        (
-            query_proj[local_rows - rim_width :],
-            key_proj[local_rows - rim_width :],
-            value_proj[local_rows - rim_width :],
+    query_width = query_proj.shape[1]
+    key_width = key_proj.shape[1]
+    before_all = shifted(
+        jnp.concatenate(
+            [
+                query_proj[local_rows - rim_width :],
+                key_proj[local_rows - rim_width :],
+                value_proj[local_rows - rim_width :],
+            ],
+            axis=1,
         ),
         "seq",
         1,
     )
+    before_query = before_all[:, :query_width]
+    before_key = before_all[:, query_width : query_width + key_width]
+    before_value = before_all[:, query_width + key_width :]
     key_heads = key_proj.shape[1] // DK
     value_heads = value_proj.shape[1] // DV
     ratio_heads = value_heads // key_heads

time: 135 us -> 128 us (0.948); the launches traced: 134 us -> 126 us
  starting transfers between devices: 47 us -> 35.5 us
  waiting for transfers between devices: 36.5 us -> 42.5 us
  local copies, waits for them, and re-layouts: 13.7 us -> 11.5 us
  other arithmetic: 10.4 us -> 8.75 us
    ppermute x15 -> x13, starting transfers between devices: 41.1 us -> 30.9 us  [shifted(): return lax.ppermute(array, axis, pairs)]
    ppermute x3, waiting for transfers between devices: 4.89 us -> 7.89 us  [shards(): summed = summed + lax.ppermute(outgoing, 'head', pairs).astype(jnp.float32)]
    ppermute x15 -> x13, waiting for transfers between devices: 29.8 us -> 32.8 us  [shifted(): return lax.ppermute(array, axis, pairs)]
  transfers between devices with their start and end apart: 19 -> 17, of which waited for: 13 -> 15; matrix products, arithmetic and copies ran while one was open for 24% -> 11% of each run, Pallas kernels for 0% -> 0%
where the time goes in v8:
time: 128 us; the launch traced here: 126 us
  waiting for transfers between devices  42.5 us (33%)
  starting transfers between devices  35.5 us (28%)
  matrix products  26.4 us (21%)
  local copies, waits for them, and re-layouts  11.5 us (9%)
  other arithmetic  8.75 us (7%)
    ppermute x13, waiting for transfers between devices, shifted(): return lax.ppermute(array, axis, pairs)  32.8 us
    ppermute x13, starting transfers between devices, shifted(): return lax.ppermute(array, axis, pairs)  30.9 us
    ppermute x3, waiting for transfers between devices, shards(): summed = summed + lax.ppermute(outgoing, 'head', pairs).astype(jnp.float32)  7.89 us
    dot_general x7, matrix products, unit_lower_inverse(): jnp.einsum('...ij,...jk->...ik', inverse, coupling, precision=highest)  6.45 us
    dot_general x28, matrix products, apply_map(): return jnp.einsum('hrke,hrev->hrkv', matrix, state_now, precision=highest)  6.13 us
    dot_general x7, matrix products, unit_lower_inverse(): jnp.einsum('...ij,...jk->...ik', jnp.einsum('...ij,...jk->...ik', inverse...  4.52 us
    ppermute x3, starting transfers between devices, shards(): summed = summed + lax.ppermute(outgoing, 'head', pairs).astype(jnp.float32)  4.52 us
  transfers between devices with their start and end apart: 17, of which 15 were waited for; matrix products, arithmetic and copies ran while one was open for 11% of the time, Pallas kernels for 0%

profile of v8, /device:TPU:128, one launch (start us, length us, event | category | flops | bytes accessed | tf_op | source)
XLA Modules:
  0.0 125.8 jit_solution(18392037213154501685)
XLA Ops:
  2.2 3.5 %collective-permute-start = (bf16[3,1024]{1,0:T(4,128)(2,1)S(1)}, bf16[3,1024]{1,0:T(4,128)(2,1)S(1)}, u32[]{:S(2)}, u32[]{:S(2)}) collective-permute-start(bf16[3,1024]{1,0:T(4,128)(2,1)S(1)} %pad_maximum_fusion.8), channel_id=1, source_target_pairs={{0,8},{8,16},{16,24},{24,32},{32,40},{40,48},{48,56},{56,64},{64,7... | collective-permute-start | bytes 18440 | tf_op jit(solution)/shard_map/ppermute | solution.py:18
  36.1 3.6 %collective-permute-start.7 = (bf16[2,1,2,128,128]{4,3,2,1,0:T(8,128)(2,1)S(1)}, bf16[2,1,2,128,128]{4,3,2,1,0:T(8,128)(2,1)S(1)}, u32[]{:S(2)}, u32[]{:S(2)}) collective-permute-start(bf16[2,1,2,128,128]{4,3,2,1,0:T(8,128)(2,1)S(1)} %pad_maximum_fusion.4), channel_id=1, source_target_pairs={{0,8},{8,16},{16,24},{24,32},{32,40},{40,48},{48,56},{56,64},{64,7... | collective-permute-start | bytes 393224 | tf_op jit(solution)/shard_map/ppermute | solution.py:18
  42.1 3.2 %collective-permute-start.1 = (bf16[2,1,2,128,128]{4,3,2,1,0:T(8,128)(2,1)S(1)}, bf16[2,1,2,128,128]{4,3,2,1,0:T(8,128)(2,1)S(1)}, u32[]{:S(2)}, u32[]{:S(2)}) collective-permute-start(bf16[2,1,2,128,128]{4,3,2,1,0:T(8,128)(2,1)S(1)} %pad_maximum_fusion), channel_id=1, source_target_pairs={{0,8},{8,16},{16,24},{24,32},{32,40},{40,48},{48,56},{56,64},{64,7... | collective-permute-start | bytes 393224 | tf_op jit(solution)/shard_map/ppermute | solution.py:18
  46.8 4.0 %collective-permute-start.8 = (bf16[2,1,2,128,128]{4,3,2,1,0:T(8,128)(2,1)S(1)}, bf16[2,1,2,128,128]{4,3,2,1,0:T(8,128)(2,1)S(1)}, u32[]{:S(2)}, u32[]{:S(2)}) collective-permute-start(bf16[2,1,2,128,128]{4,3,2,1,0:T(8,128)(2,1)S(1)} %pad_maximum_fusion.5), channel_id=1, source_target_pairs={{0,16},{8,24},{16,32},{24,40},{32,48},{40,56},{48,64},{56,72},{64,... | collective-permute-start | bytes 393224 | tf_op jit(solution)/shard_map/ppermute | solution.py:18
  52.8 2.2 %collective-permute-start.2 = (bf16[2,1,2,128,128]{4,3,2,1,0:T(8,128)(2,1)S(1)}, bf16[2,1,2,128,128]{4,3,2,1,0:T(8,128)(2,1)S(1)}, u32[]{:S(2)}, u32[]{:S(2)}) collective-permute-start(bf16[2,1,2,128,128]{4,3,2,1,0:T(8,128)(2,1)S(1)} %pad_maximum_fusion.1), channel_id=1, source_target_pairs={{0,16},{8,24},{16,32},{24,40},{32,48},{40,56},{48,64},{56,72},{64,... | collective-permute-start | bytes 393224 | tf_op jit(solution)/shard_map/ppermute | solution.py:18
  55.0 2.4 %collective-permute-done.8 = bf16[2,1,2,128,128]{4,3,2,1,0:T(8,128)(2,1)S(1)} collective-permute-done((bf16[2,1,2,128,128]{4,3,2,1,0:T(8,128)(2,1)S(1)}, bf16[2,1,2,128,128]{4,3,2,1,0:T(8,128)(2,1)S(1)}, u32[]{:S(2)}, u32[]{:S(2)}) %collective-permute-start.8) | collective-permute-done | bytes 131104 | tf_op jit(solution)/shard_map/ppermute | solution.py:18
  57.8 1.9 %collective-permute-start.9 = (bf16[2,1,2,128,128]{4,3,2,1,0:T(8,128)(2,1)S(1)}, bf16[2,1,2,128,128]{4,3,2,1,0:T(8,128)(2,1)S(1)}, u32[]{:S(2)}, u32[]{:S(2)}) collective-permute-start(bf16[2,1,2,128,128]{4,3,2,1,0:T(8,128)(2,1)S(1)} %pad_maximum_fusion.6), channel_id=1, source_target_pairs={{0,32},{8,40},{16,48},{24,56},{32,64},{40,72},{48,80},{56,88},{64,... | collective-permute-start | bytes 393224 | tf_op jit(solution)/shard_map/ppermute | solution.py:18
  59.7 4.5 %collective-permute-done.2 = bf16[2,1,2,128,128]{4,3,2,1,0:T(8,128)(2,1)S(1)} collective-permute-done((bf16[2,1,2,128,128]{4,3,2,1,0:T(8,128)(2,1)S(1)}, bf16[2,1,2,128,128]{4,3,2,1,0:T(8,128)(2,1)S(1)}, u32[]{:S(2)}, u32[]{:S(2)}) %collective-permute-start.2) | collective-permute-done | bytes 131104 | tf_op jit(solution)/shard_map/ppermute | solution.py:18
  64.7 1.9 %collective-permute-start.3 = (bf16[2,1,2,128,128]{4,3,2,1,0:T(8,128)(2,1)S(1)}, bf16[2,1,2,128,128]{4,3,2,1,0:T(8,128)(2,1)S(1)}, u32[]{:S(2)}, u32[]{:S(2)}) collective-permute-start(bf16[2,1,2,128,128]{4,3,2,1,0:T(8,128)(2,1)S(1)} %pad_maximum_fusion.2), channel_id=1, source_target_pairs={{0,32},{8,40},{16,48},{24,56},{32,64},{40,72},{48,80},{56,88},{64,... | collective-permute-start | bytes 393224 | tf_op jit(solution)/shard_map/ppermute | solution.py:18
  67.1 2.0 %collective-permute-start.10 = (bf16[2,1,2,128,128]{4,3,2,1,0:T(8,128)(2,1)S(1)}, bf16[2,1,2,128,128]{4,3,2,1,0:T(8,128)(2,1)S(1)}, u32[]{:S(2)}, u32[]{:S(2)}) collective-permute-start(bf16[2,1,2,128,128]{4,3,2,1,0:T(8,128)(2,1)S(1)} %pad_maximum_fusion.7), channel_id=1, source_target_pairs={{0,64},{8,72},{16,80},{24,88},{32,96},{40,104},{48,112},{56,120},{... | collective-permute-start | bytes 393224 | tf_op jit(solution)/shard_map/ppermute | solution.py:18
  69.1 4.4 %collective-permute-done.3 = bf16[2,1,2,128,128]{4,3,2,1,0:T(8,128)(2,1)S(1)} collective-permute-done((bf16[2,1,2,128,128]{4,3,2,1,0:T(8,128)(2,1)S(1)}, bf16[2,1,2,128,128]{4,3,2,1,0:T(8,128)(2,1)S(1)}, u32[]{:S(2)}, u32[]{:S(2)}) %collective-permute-start.3) | collective-permute-done | bytes 131104 | tf_op jit(solution)/shard_map/ppermute | solution.py:18
  74.0 1.9 %collective-permute-start.4 = (bf16[2,1,2,128,128]{4,3,2,1,0:T(8,128)(2,1)S(1)}, bf16[2,1,2,128,128]{4,3,2,1,0:T(8,128)(2,1)S(1)}, u32[]{:S(2)}, u32[]{:S(2)}) collective-permute-start(bf16[2,1,2,128,128]{4,3,2,1,0:T(8,128)(2,1)S(1)} %pad_maximum_fusion.3), channel_id=1, source_target_pairs={{0,64},{8,72},{16,80},{24,88},{32,96},{40,104},{48,112},{56,120},{... | collective-permute-start | bytes 393224 | tf_op jit(solution)/shard_map/ppermute | solution.py:18
  75.9 4.8 %collective-permute-done.10 = bf16[2,1,2,128,128]{4,3,2,1,0:T(8,128)(2,1)S(1)} collective-permute-done((bf16[2,1,2,128,128]{4,3,2,1,0:T(8,128)(2,1)S(1)}, bf16[2,1,2,128,128]{4,3,2,1,0:T(8,128)(2,1)S(1)}, u32[]{:S(2)}, u32[]{:S(2)}) %collective-permute-start.10) | collective-permute-done | bytes 131104 | tf_op jit(solution)/shard_map/ppermute | solution.py:18
  82.3 2.2 %collective-permute-done.4 = bf16[2,1,2,128,128]{4,3,2,1,0:T(8,128)(2,1)S(1)} collective-permute-done((bf16[2,1,2,128,128]{4,3,2,1,0:T(8,128)(2,1)S(1)}, bf16[2,1,2,128,128]{4,3,2,1,0:T(8,128)(2,1)S(1)}, u32[]{:S(2)}, u32[]{:S(2)}) %collective-permute-start.4) | collective-permute-done | bytes 131104 | tf_op jit(solution)/shard_map/ppermute | solution.py:18
  86.6 4.4 %collective-permute-done.11 = bf16[1,2,128,128]{3,2,1,0:T(8,128)(2,1)S(1)} collective-permute-done((bf16[1,2,128,128]{3,2,1,0:T(8,128)(2,1)S(1)}, bf16[1,2,128,128]{3,2,1,0:T(8,128)(2,1)S(1)}, u32[]{:S(2)}, u32[]{:S(2)}) %collective-permute-start.11) | collective-permute-done | bytes 65568 | tf_op jit(solution)/shard_map/ppermute | solution.py:18
  91.2 1.9 %collective-permute-start.12 = (bf16[1,2,128,128]{3,2,1,0:T(8,128)(2,1)S(1)}, bf16[1,2,128,128]{3,2,1,0:T(8,128)(2,1)S(1)}, u32[]{:S(2)}, u32[]{:S(2)}) collective-permute-start(bf16[1,2,128,128]{3,2,1,0:T(8,128)(2,1)S(1)} %fusion.15), channel_id=1, source_target_pairs={{0,8},{8,16},{16,24},{24,32},{32,40},{40,48},{48,56},{56,64},{64,7... | collective-permute-start | bytes 196616 | tf_op jit(solution)/shard_map/ppermute | solution.py:18
  95.0 1.9 %collective-permute-start.6 = (bf16[1,2,128,128]{3,2,1,0:T(8,128)(2,1)S(1)}, bf16[1,2,128,128]{3,2,1,0:T(8,128)(2,1)S(1)}, u32[]{:S(2)}, u32[]{:S(2)}) collective-permute-start(bf16[1,2,128,128]{3,2,1,0:T(8,128)(2,1)S(1)} %fusion.16), channel_id=1, source_target_pairs={{0,8},{8,16},{16,24},{24,32},{32,40},{40,48},{48,56},{56,64},{64,7... | collective-permute-start | bytes 196616 | tf_op jit(solution)/shard_map/ppermute | solution.py:18
  96.9 3.8 %collective-permute-done.12 = bf16[1,2,128,128]{3,2,1,0:T(8,128)(2,1)S(1)} collective-permute-done((bf16[1,2,128,128]{3,2,1,0:T(8,128)(2,1)S(1)}, bf16[1,2,128,128]{3,2,1,0:T(8,128)(2,1)S(1)}, u32[]{:S(2)}, u32[]{:S(2)}) %collective-permute-start.12) | collective-permute-done | bytes 65568 | tf_op jit(solution)/shard_map/ppermute | solution.py:18
  101.3 3.1 %collective-permute-done.6 = bf16[1,2,128,128]{3,2,1,0:T(8,128)(2,1)S(1)} collective-permute-done((bf16[1,2,128,128]{3,2,1,0:T(8,128)(2,1)S(1)}, bf16[1,2,128,128]{3,2,1,0:T(8,128)(2,1)S(1)}, u32[]{:S(2)}, u32[]{:S(2)}) %collective-permute-start.6) | collective-permute-done | bytes 65568 | tf_op jit(solution)/shard_map/ppermute | solution.py:18
  109.5 1.8 %collective-permute-done.13 = bf16[4,32,2048]{2,1,0:T(8,128)(2,1)S(1)} collective-permute-done((bf16[4,32,2048]{2,1,0:T(8,128)(2,1)S(1)}, bf16[4,32,2048]{2,1,0:T(8,128)(2,1)S(1)}, u32[]{:S(2)}, u32[]{:S(2)}) %collective-permute-start.13) | collective-permute-done | bytes 524320 | tf_op jit(solution)/shard_map/ppermute | solution.py:213
  112.7 2.8 %collective-permute-start.16 = (bf16[32,2048]{1,0:T(8,128)(2,1)S(1)}, bf16[32,2048]{1,0:T(8,128)(2,1)S(1)}, u32[]{:S(2)}, u32[]{:S(2)}) collective-permute-start(bf16[32,2048]{1,0:T(8,128)(2,1)S(1)} %get-tuple-element.10), channel_id=1, source_target_pairs={{0,6},{1,7},{2,0},{3,1},{4,2},{5,3},{6,4},{7,5},{8,14},{9,15},{10,... | collective-permute-start | bytes 393224 | tf_op jit(solution)/shard_map/ppermute | solution.py:219
  117.2 4.2 %collective-permute-done.16 = bf16[32,2048]{1,0:T(8,128)(2,1)S(1)} collective-permute-done((bf16[32,2048]{1,0:T(8,128)(2,1)S(1)}, bf16[32,2048]{1,0:T(8,128)(2,1)S(1)}, u32[]{:S(2)}, u32[]{:S(2)}) %collective-permute-start.16) | collective-permute-done | bytes 131104 | tf_op jit(solution)/shard_map/ppermute | solution.py:219
  121.4 2.0 %collective-permute-done.15 = bf16[32,2048]{1,0:T(8,128)(2,1)S(1)} collective-permute-done((bf16[32,2048]{1,0:T(8,128)(2,1)S(1)}, bf16[32,2048]{1,0:T(8,128)(2,1)S(1)}, u32[]{:S(2)}, u32[]{:S(2)}) %collective-permute-start.15) | collective-permute-done | bytes 131104 | tf_op jit(solution)/shard_map/ppermute | solution.py:219
  123.4 1.7 %collective-permute-done.14 = bf16[32,2048]{1,0:T(8,128)(2,1)S(1)} collective-permute-done((bf16[32,2048]{1,0:T(8,128)(2,1)S(1)}, bf16[32,2048]{1,0:T(8,128)(2,1)S(1)}, u32[]{:S(2)}, u32[]{:S(2)}) %collective-permute-start.14) | collective-permute-done | bytes 131104 | tf_op jit(solution)/shard_map/ppermute | solution.py:219
  (157 shorter events, 54.4 us)
Async XLA Ops:
  0.0 107.2 %copy-start = (bf16[512,2048]{1,0:T(8,128)(2,1)S(1)}, bf16[512,2048]{1,0:T(8,128)(2,1)}, u32[]{:S(2)}) copy-start(bf16[512,2048]{1,0:T(8,128)(2,1)} %param.21) | copy-start | bytes 6291460
  2.2 9.8 %collective-permute-start = (bf16[3,1024]{1,0:T(4,128)(2,1)S(1)}, bf16[3,1024]{1,0:T(4,128)(2,1)S(1)}, u32[]{:S(2)}, u32[]{:S(2)}) collective-permute-start(bf16[3,1024]{1,0:T(4,128)(2,1)S(1)} %pad_maximum_fusion.8), channel_id=1, source_target_pairs={{0,8},{8,16},{16,24},{24,32},{32,40},{40,48},{48,56},{56,64},{64,7... | collective-permute-start | bytes 18440 | tf_op jit(solution)/shard_map/ppermute | solution.py:18
  26.7 1.8 %copy-start.4 = (bf16[256,512]{1,0:T(8,128)(2,1)S(1)}, bf16[256,512]{1,0:T(8,128)(2,1)}, u32[]{:S(2)}) copy-start(bf16[256,512]{1,0:T(8,128)(2,1)} %param.13) | copy-start | bytes 786436
  33.7 6.0 %copy-start.2 = (f32[2,2,128,128]{3,2,1,0:T(8,128)S(1)}, f32[2,2,128,128]{3,2,1,0:T(8,128)}, u32[]{:S(2)}) copy-start(f32[2,2,128,128]{3,2,1,0:T(8,128)} %fusion.156) | copy-start | bytes 786436
  36.0 9.2 %copy-start.3 = (f32[2,128,2,128]{3,1,0,2:T(8,128)S(1)}, f32[2,128,2,128]{3,1,0,2:T(8,128)}, u32[]{:S(2)}) copy-start(f32[2,128,2,128]{3,1,0,2:T(8,128)} %copy.91) | copy-start | bytes 786436
  36.1 10.3 %collective-permute-start.7 = (bf16[2,1,2,128,128]{4,3,2,1,0:T(8,128)(2,1)S(1)}, bf16[2,1,2,128,128]{4,3,2,1,0:T(8,128)(2,1)S(1)}, u32[]{:S(2)}, u32[]{:S(2)}) collective-permute-start(bf16[2,1,2,128,128]{4,3,2,1,0:T(8,128)(2,1)S(1)} %pad_maximum_fusion.4), channel_id=1, source_target_pairs={{0,8},{8,16},{16,24},{24,32},{32,40},{40,48},{48,56},{56,64},{64,7... | collective-permute-start | bytes 393224 | tf_op jit(solution)/shard_map/ppermute | solution.py:18
  42.1 10.2 %collective-permute-start.1 = (bf16[2,1,2,128,128]{4,3,2,1,0:T(8,128)(2,1)S(1)}, bf16[2,1,2,128,128]{4,3,2,1,0:T(8,128)(2,1)S(1)}, u32[]{:S(2)}, u32[]{:S(2)}) collective-permute-start(bf16[2,1,2,128,128]{4,3,2,1,0:T(8,128)(2,1)S(1)} %pad_maximum_fusion), channel_id=1, source_target_pairs={{0,8},{8,16},{16,24},{24,32},{32,40},{40,48},{48,56},{56,64},{64,7... | collective-permute-start | bytes 393224 | tf_op jit(solution)/shard_map/ppermute | solution.py:18
  46.8 10.5 %collective-permute-start.8 = (bf16[2,1,2,128,128]{4,3,2,1,0:T(8,128)(2,1)S(1)}, bf16[2,1,2,128,128]{4,3,2,1,0:T(8,128)(2,1)S(1)}, u32[]{:S(2)}, u32[]{:S(2)}) collective-permute-start(bf16[2,1,2,128,128]{4,3,2,1,0:T(8,128)(2,1)S(1)} %pad_maximum_fusion.5), channel_id=1, source_target_pairs={{0,16},{8,24},{16,32},{24,40},{32,48},{40,56},{48,64},{56,72},{64,... | collective-permute-start | bytes 393224 | tf_op jit(solution)/shard_map/ppermute | solution.py:18
  52.8 11.5 %collective-permute-start.2 = (bf16[2,1,2,128,128]{4,3,2,1,0:T(8,128)(2,1)S(1)}, bf16[2,1,2,128,128]{4,3,2,1,0:T(8,128)(2,1)S(1)}, u32[]{:S(2)}, u32[]{:S(2)}) collective-permute-start(bf16[2,1,2,128,128]{4,3,2,1,0:T(8,128)(2,1)S(1)} %pad_maximum_fusion.1), channel_id=1, source_target_pairs={{0,16},{8,24},{16,32},{24,40},{32,48},{40,56},{48,64},{56,72},{64,... | collective-permute-start | bytes 393224 | tf_op jit(solution)/shard_map/ppermute | solution.py:18
  57.8 8.8 %collective-permute-start.9 = (bf16[2,1,2,128,128]{4,3,2,1,0:T(8,128)(2,1)S(1)}, bf16[2,1,2,128,128]{4,3,2,1,0:T(8,128)(2,1)S(1)}, u32[]{:S(2)}, u32[]{:S(2)}) collective-permute-start(bf16[2,1,2,128,128]{4,3,2,1,0:T(8,128)(2,1)S(1)} %pad_maximum_fusion.6), channel_id=1, source_target_pairs={{0,32},{8,40},{16,48},{24,56},{32,64},{40,72},{48,80},{56,88},{64,... | collective-permute-start | bytes 393224 | tf_op jit(solution)/shard_map/ppermute | solution.py:18
  64.7 8.8 %collective-permute-start.3 = (bf16[2,1,2,128,128]{4,3,2,1,0:T(8,128)(2,1)S(1)}, bf16[2,1,2,128,128]{4,3,2,1,0:T(8,128)(2,1)S(1)}, u32[]{:S(2)}, u32[]{:S(2)}) collective-permute-start(bf16[2,1,2,128,128]{4,3,2,1,0:T(8,128)(2,1)S(1)} %pad_maximum_fusion.2), channel_id=1, source_target_pairs={{0,32},{8,40},{16,48},{24,56},{32,64},{40,72},{48,80},{56,88},{64,... | collective-permute-start | bytes 393224 | tf_op jit(solution)/shard_map/ppermute | solution.py:18
  67.1 13.6 %collective-permute-start.10 = (bf16[2,1,2,128,128]{4,3,2,1,0:T(8,128)(2,1)S(1)}, bf16[2,1,2,128,128]{4,3,2,1,0:T(8,128)(2,1)S(1)}, u32[]{:S(2)}, u32[]{:S(2)}) collective-permute-start(bf16[2,1,2,128,128]{4,3,2,1,0:T(8,128)(2,1)S(1)} %pad_maximum_fusion.7), channel_id=1, source_target_pairs={{0,64},{8,72},{16,80},{24,88},{32,96},{40,104},{48,112},{56,120},{... | collective-permute-start | bytes 393224 | tf_op jit(solution)/shard_map/ppermute | solution.py:18
  74.0 10.5 %collective-permute-start.4 = (bf16[2,1,2,128,128]{4,3,2,1,0:T(8,128)(2,1)S(1)}, bf16[2,1,2,128,128]{4,3,2,1,0:T(8,128)(2,1)S(1)}, u32[]{:S(2)}, u32[]{:S(2)}) collective-permute-start(bf16[2,1,2,128,128]{4,3,2,1,0:T(8,128)(2,1)S(1)} %pad_maximum_fusion.3), channel_id=1, source_target_pairs={{0,64},{8,72},{16,80},{24,88},{32,96},{40,104},{48,112},{56,120},{... | collective-permute-start | bytes 393224 | tf_op jit(solution)/shard_map/ppermute | solution.py:18
  81.0 10.1 %collective-permute-start.11 = (bf16[1,2,128,128]{3,2,1,0:T(8,128)(2,1)S(1)}, bf16[1,2,128,128]{3,2,1,0:T(8,128)(2,1)S(1)}, u32[]{:S(2)}, u32[]{:S(2)}) collective-permute-start(bf16[1,2,128,128]{3,2,1,0:T(8,128)(2,1)S(1)} %convert_bitcast_fusion), channel_id=1, source_target_pairs={{0,128},{8,136},{16,144},{24,152},{32,160},{40,168},{48,176},{56,1... | collective-permute-start | bytes 196616 | tf_op jit(solution)/shard_map/ppermute | solution.py:18
  84.7 10.1 %collective-permute-start.5 = (bf16[1,2,128,128]{3,2,1,0:T(8,128)(2,1)S(1)}, bf16[1,2,128,128]{3,2,1,0:T(8,128)(2,1)S(1)}, u32[]{:S(2)}, u32[]{:S(2)}) collective-permute-start(bf16[1,2,128,128]{3,2,1,0:T(8,128)(2,1)S(1)} %convert_bitcast_fusion.9), channel_id=1, source_target_pairs={{0,128},{8,136},{16,144},{24,152},{32,160},{40,168},{48,176},{56,1... | collective-permute-start | bytes 196616 | tf_op jit(solution)/shard_map/ppermute | solution.py:18
  91.2 9.5 %collective-permute-start.12 = (bf16[1,2,128,128]{3,2,1,0:T(8,128)(2,1)S(1)}, bf16[1,2,128,128]{3,2,1,0:T(8,128)(2,1)S(1)}, u32[]{:S(2)}, u32[]{:S(2)}) collective-permute-start(bf16[1,2,128,128]{3,2,1,0:T(8,128)(2,1)S(1)} %fusion.15), channel_id=1, source_target_pairs={{0,8},{8,16},{16,24},{24,32},{32,40},{40,48},{48,56},{56,64},{64,7... | collective-permute-start | bytes 196616 | tf_op jit(solution)/shard_map/ppermute | solution.py:18
  95.0 9.5 %collective-permute-start.6 = (bf16[1,2,128,128]{3,2,1,0:T(8,128)(2,1)S(1)}, bf16[1,2,128,128]{3,2,1,0:T(8,128)(2,1)S(1)}, u32[]{:S(2)}, u32[]{:S(2)}) collective-permute-start(bf16[1,2,128,128]{3,2,1,0:T(8,128)(2,1)S(1)} %fusion.16), channel_id=1, source_target_pairs={{0,8},{8,16},{16,24},{24,32},{32,40},{40,48},{48,56},{56,64},{64,7... | collective-permute-start | bytes 196616 | tf_op jit(solution)/shard_map/ppermute | solution.py:18
  105.6 1.4 %copy-start.5 = (bf16[256,512]{1,0:T(8,128)(2,1)S(1)}, bf16[256,512]{1,0:T(8,128)(2,1)}, u32[]{:S(2)}) copy-start(bf16[256,512]{1,0:T(8,128)(2,1)} %param.14) | copy-start | bytes 786436
  107.9 1.3 %copy-start.1 = (f32[4,2,32,2048]{3,2,1,0:T(8,128)}, f32[4,2,32,2048]{3,2,1,0:T(8,128)S(1)}, u32[]{:S(2)}) copy-start(f32[4,2,32,2048]{3,2,1,0:T(8,128)S(1)} %fusion) | copy-start | bytes 6291460
  109.3 2.0 %collective-permute-start.13 = (bf16[4,32,2048]{2,1,0:T(8,128)(2,1)S(1)}, bf16[4,32,2048]{2,1,0:T(8,128)(2,1)S(1)}, u32[]{:S(2)}, u32[]{:S(2)}) collective-permute-start(bf16[4,32,2048]{2,1,0:T(8,128)(2,1)S(1)} %fusion.26), channel_id=1, source_target_pairs={{0,1},{1,0},{2,3},{3,2},{4,5},{5,4},{6,7},{7,6},{8,9},{9,8},{10,11... | collective-permute-start | bytes 1572872 | tf_op jit(solution)/shard_map/ppermute | solution.py:213
  112.7 8.7 %collective-permute-start.16 = (bf16[32,2048]{1,0:T(8,128)(2,1)S(1)}, bf16[32,2048]{1,0:T(8,128)(2,1)S(1)}, u32[]{:S(2)}, u32[]{:S(2)}) collective-permute-start(bf16[32,2048]{1,0:T(8,128)(2,1)S(1)} %get-tuple-element.10), channel_id=1, source_target_pairs={{0,6},{1,7},{2,0},{3,1},{4,2},{5,3},{6,4},{7,5},{8,14},{9,15},{10,... | collective-permute-start | bytes 393224 | tf_op jit(solution)/shard_map/ppermute | solution.py:219
  115.5 7.9 %collective-permute-start.15 = (bf16[32,2048]{1,0:T(8,128)(2,1)S(1)}, bf16[32,2048]{1,0:T(8,128)(2,1)S(1)}, u32[]{:S(2)}, u32[]{:S(2)}) collective-permute-start(bf16[32,2048]{1,0:T(8,128)(2,1)S(1)} %get-tuple-element.11), channel_id=1, source_target_pairs={{0,4},{1,5},{2,6},{3,7},{4,0},{5,1},{6,2},{7,3},{8,12},{9,13},{10,... | collective-permute-start | bytes 393224 | tf_op jit(solution)/shard_map/ppermute | solution.py:219
  116.3 8.8 %collective-permute-start.14 = (bf16[32,2048]{1,0:T(8,128)(2,1)S(1)}, bf16[32,2048]{1,0:T(8,128)(2,1)S(1)}, u32[]{:S(2)}, u32[]{:S(2)}) collective-permute-start(bf16[32,2048]{1,0:T(8,128)(2,1)S(1)} %get-tuple-element.9), channel_id=1, source_target_pairs={{0,2},{1,3},{2,4},{3,5},{4,6},{5,7},{6,0},{7,1},{8,10},{9,11},{10,... | collective-permute-start | bytes 393224 | tf_op jit(solution)/shard_map/ppermute | solution.py:219

commit v9 on v8

--- a/solution.py
+++ b/solution.py
@@ -192,10 +192,7 @@
     strength_blocks = strength.reshape(key_heads, ratio_heads, spans, SPAN)
     decay_blocks = log_decay.reshape(key_heads, ratio_heads, spans, SPAN)
     maps = chunk_maps(query_blocks, key_blocks, value_blocks, strength_blocks, decay_blocks)
-    parts = [
-        relay_group(*[piece[group : group + 1] for piece in maps]) for group in range(key_heads)
-    ]
-    outputs = jnp.concatenate(parts, axis=1)
+    outputs = relay_group(*maps)
     core_out = jnp.moveaxis(outputs, 0, 2)
     core_out = core_out.transpose(2, 3, 0, 1, 4).reshape(local_rows, value_heads, DV)
     gate_values = gate_proj.astype(jnp.float32).reshape(local_rows, value_heads, DV)

time: 128 us -> 143 us (1.12); the launches traced: 126 us -> 142 us
  waiting for transfers between devices: 42.5 us -> 58.1 us
  starting transfers between devices: 35.5 us -> 21.5 us
  local copies, waits for them, and re-layouts: 11.5 us -> 17.3 us
  other arithmetic: 8.75 us -> 13.8 us
  matrix products: 26.4 us -> 30.6 us
    ppermute x13 -> x7, waiting for transfers between devices: 32.8 us -> 50.8 us  [shifted(): return lax.ppermute(array, axis, pairs)]
    ppermute x13 -> x7, starting transfers between devices: 30.9 us -> 16.3 us  [shifted(): return lax.ppermute(array, axis, pairs)]
    dot_general x28 -> x14, matrix products: 6.13 us -> 10.5 us  [apply_map(): return jnp.einsum('hrke,hrev->hrkv', matrix, state_now, precision=highest)]
    unnamed x12 -> x62, local copies, waits for them, and re-layouts: 1.35 us -> 4.98 us
    ppermute x3, waiting for transfers between devices: 7.89 us -> 5.46 us  [shards(): summed = summed + lax.ppermute(outgoing, 'head', pairs).astype(jnp.float32)]
    another operation x24 -> x12, other arithmetic: 0.31 us -> 2.4 us  [relay_group(): jnp.stack([prefix_map, prefix_end]).astype(jnp.bfloat16)]
    reshape x2, local copies, waits for them, and re-layouts: 0.86 us -> 2.81 us  [shards(): queries.reshape(spans, SPAN, key_heads, DK).transpose(2, 0, 1, 3)[:, None]]
  transfers between devices with their start and end apart: 17 -> 11, of which waited for: 15 -> 10; matrix products, arithmetic and copies ran while one was open for 11% -> 11% of each run, Pallas kernels for 0% -> 0%
where the time goes in v9:
time: 143 us; the launch traced here: 142 us
  waiting for transfers between devices  58.1 us (41%)
  matrix products  30.6 us (21%)
  starting transfers between devices  21.5 us (15%)
  local copies, waits for them, and re-layouts  17.3 us (12%)
  other arithmetic  13.8 us (10%)
    ppermute x7, waiting for transfers between devices, shifted(): return lax.ppermute(array, axis, pairs)  50.8 us
    ppermute x7, starting transfers between devices, shifted(): return lax.ppermute(array, axis, pairs)  16.3 us
    dot_general x14, matrix products, apply_map(): return jnp.einsum('hrke,hrev->hrkv', matrix, state_now, precision=highest)  10.5 us
    dot_general x7, matrix products, unit_lower_inverse(): jnp.einsum('...ij,...jk->...ik', inverse, coupling, precision=highest)  6.22 us
    ppermute x3, waiting for transfers between devices, shards(): summed = summed + lax.ppermute(outgoing, 'head', pairs).astype(jnp.float32)  5.46 us
    ppermute x3, starting transfers between devices, shards(): summed = summed + lax.ppermute(outgoing, 'head', pairs).astype(jnp.float32)  5.16 us
    unnamed x62, local copies, waits for them, and re-layouts  4.98 us
    dot_general x7, matrix products, unit_lower_inverse(): jnp.einsum('...ij,...jk->...ik', jnp.einsum('...ij,...jk->...ik', inverse...  4.7 us
  transfers between devices with their start and end apart: 11, of which 10 were waited for; matrix products, arithmetic and copies ran while one was open for 11% of the time, Pallas kernels for 0%

profile of v9, /device:TPU:128, one launch (start us, length us, event | category | flops | bytes accessed | tf_op | source)
XLA Modules:
  0.0 142.3 jit_solution(9720959153121468163)
XLA Ops:
  2.2 3.5 %collective-permute-start = (bf16[3,1024]{1,0:T(4,128)(2,1)S(1)}, bf16[3,1024]{1,0:T(4,128)(2,1)S(1)}, u32[]{:S(2)}, u32[]{:S(2)}) collective-permute-start(bf16[3,1024]{1,0:T(4,128)(2,1)S(1)} %pad_maximum_fusion.4), channel_id=1, source_target_pairs={{0,8},{8,16},{16,24},{24,32},{32,40},{40,48},{48,56},{56,64},{64,7... | collective-permute-start | bytes 18440 | tf_op jit(solution)/shard_map/ppermute | solution.py:18
  7.2 1.4 %fusion.149 = (f32[1,256]{1,0:T(1,128)}, f32[1,256]{1,0:T(1,128)}, f32[1,256]{1,0:T(1,128)}, f32[1,256]{1,0:T(1,128)}) fusion(bf16[4,256]{1,0:T(4,128)(2,1)} %param.18), kind=kLoop, calls=%fused_computation.278 | loop fusion | bytes 8192 | tf_op jit(solution)/shard_map/slice | solution.py:27
  38.2 3.5 %collective-permute-start.1 = (bf16[2,2,2,128,128]{4,3,2,1,0:T(8,128)(2,1)}, bf16[2,2,2,128,128]{4,3,2,1,0:T(8,128)(2,1)}, u32[]{:S(2)}, u32[]{:S(2)}) collective-permute-start(bf16[2,2,2,128,128]{4,3,2,1,0:T(8,128)(2,1)} %pad_maximum_fusion), channel_id=1, source_target_pairs={{0,8},{8,16},{16,24},{24,32},{32,40},{40,48},{48,56},{56,64},{64,7... | collective-permute-start | bytes 786440 | tf_op jit(solution)/shard_map/ppermute | solution.py:18
  41.7 9.8 %collective-permute-done.1 = bf16[2,2,2,128,128]{4,3,2,1,0:T(8,128)(2,1)} collective-permute-done((bf16[2,2,2,128,128]{4,3,2,1,0:T(8,128)(2,1)}, bf16[2,2,2,128,128]{4,3,2,1,0:T(8,128)(2,1)}, u32[]{:S(2)}, u32[]{:S(2)}) %collective-permute-start.1) | collective-permute-done | bytes 262176 | tf_op jit(solution)/shard_map/ppermute | solution.py:18
  56.4 1.9 %collective-permute-start.2 = (bf16[2,2,2,128,128]{4,3,2,1,0:T(8,128)(2,1)}, bf16[2,2,2,128,128]{4,3,2,1,0:T(8,128)(2,1)}, u32[]{:S(2)}, u32[]{:S(2)}) collective-permute-start(bf16[2,2,2,128,128]{4,3,2,1,0:T(8,128)(2,1)} %pad_maximum_fusion.1), channel_id=1, source_target_pairs={{0,16},{8,24},{16,32},{24,40},{32,48},{40,56},{48,64},{56,72},{64,... | collective-permute-start | bytes 786440 | tf_op jit(solution)/shard_map/ppermute | solution.py:18
  58.4 10.7 %collective-permute-done.2 = bf16[2,2,2,128,128]{4,3,2,1,0:T(8,128)(2,1)} collective-permute-done((bf16[2,2,2,128,128]{4,3,2,1,0:T(8,128)(2,1)}, bf16[2,2,2,128,128]{4,3,2,1,0:T(8,128)(2,1)}, u32[]{:S(2)}, u32[]{:S(2)}) %collective-permute-start.2) | collective-permute-done | bytes 262176 | tf_op jit(solution)/shard_map/ppermute | solution.py:18
  69.1 1.4 convolution_select_fusion.2
  71.2 1.4 convolution_add_fusion.6
  74.0 1.9 %collective-permute-start.3 = (bf16[2,2,2,128,128]{4,3,2,1,0:T(8,128)(2,1)}, bf16[2,2,2,128,128]{4,3,2,1,0:T(8,128)(2,1)}, u32[]{:S(2)}, u32[]{:S(2)}) collective-permute-start(bf16[2,2,2,128,128]{4,3,2,1,0:T(8,128)(2,1)} %pad_maximum_fusion.2), channel_id=1, source_target_pairs={{0,32},{8,40},{16,48},{24,56},{32,64},{40,72},{48,80},{56,88},{64,... | collective-permute-start | bytes 786440 | tf_op jit(solution)/shard_map/ppermute | solution.py:18
  76.8 1.8 %reshape.590 = f32[2,128,2,128]{3,2,1,0:T(2,128)} reshape(f32[256,256]{1,0:T(8,128)} %divide_multiply_fusion.2) | data formatting | bytes 524288 | tf_op jit(solution)/shard_map/reshape | solution.py:189
  79.6 1.6 %fusion.59 = f32[2,2,128,128]{3,2,1,0:T(8,128)S(1)} fusion(f32[2,2,128,128]{3,2,1,0:T(8,128)S(1)} %fusion.61, f32[2,128,2,128]{3,2,1,0:T(2,128)} %reshape.590), kind=kOutput, calls=%fused_computation.121 | convolution fusion | flops 100663296 | bytes 786432 | tf_op jit(solution)/shard_map/hxnck,hxnek->hxnce/dot_general | solution.py:64
  81.3 2.6 %collective-permute-done.3 = bf16[2,2,2,128,128]{4,3,2,1,0:T(8,128)(2,1)} collective-permute-done((bf16[2,2,2,128,128]{4,3,2,1,0:T(8,128)(2,1)}, bf16[2,2,2,128,128]{4,3,2,1,0:T(8,128)(2,1)}, u32[]{:S(2)}, u32[]{:S(2)}) %collective-permute-start.3) | collective-permute-done | bytes 262176 | tf_op jit(solution)/shard_map/ppermute | solution.py:18
  86.5 2.1 %collective-permute-start.4 = (bf16[2,2,2,128,128]{4,3,2,1,0:T(8,128)(2,1)S(1)}, bf16[2,2,2,128,128]{4,3,2,1,0:T(8,128)(2,1)S(1)}, u32[]{:S(2)}, u32[]{:S(2)}) collective-permute-start(bf16[2,2,2,128,128]{4,3,2,1,0:T(8,128)(2,1)S(1)} %pad_maximum_fusion.3), channel_id=1, source_target_pairs={{0,64},{8,72},{16,80},{24,88},{32,96},{40,104},{48,112},{56,120},{... | collective-permute-start | bytes 786440 | tf_op jit(solution)/shard_map/ppermute | solution.py:18
  89.4 11.7 %collective-permute-done.4 = bf16[2,2,2,128,128]{4,3,2,1,0:T(8,128)(2,1)S(1)} collective-permute-done((bf16[2,2,2,128,128]{4,3,2,1,0:T(8,128)(2,1)S(1)}, bf16[2,2,2,128,128]{4,3,2,1,0:T(8,128)(2,1)S(1)}, u32[]{:S(2)}, u32[]{:S(2)}) %collective-permute-start.4) | collective-permute-done | bytes 262176 | tf_op jit(solution)/shard_map/ppermute | solution.py:18
  102.9 9.2 %collective-permute-done.5 = bf16[2,2,128,128]{3,2,1,0:T(8,128)(2,1)S(1)} collective-permute-done((bf16[2,2,128,128]{3,2,1,0:T(8,128)(2,1)S(1)}, bf16[2,2,128,128]{3,2,1,0:T(8,128)(2,1)S(1)}, u32[]{:S(2)}, u32[]{:S(2)}) %collective-permute-start.5) | collective-permute-done | bytes 131104 | tf_op jit(solution)/shard_map/ppermute | solution.py:18
  112.4 2.1 %collective-permute-start.6 = (bf16[2,2,128,128]{3,2,1,0:T(8,128)(2,1)S(1)}, bf16[2,2,128,128]{3,2,1,0:T(8,128)(2,1)S(1)}, u32[]{:S(2)}, u32[]{:S(2)}) collective-permute-start(bf16[2,2,128,128]{3,2,1,0:T(8,128)(2,1)S(1)} %fusion.13), channel_id=1, source_target_pairs={{0,8},{8,16},{16,24},{24,32},{32,40},{40,48},{48,56},{56,64},{64,7... | collective-permute-start | bytes 393224 | tf_op jit(solution)/shard_map/ppermute | solution.py:18
  115.8 6.8 %collective-permute-done.6 = bf16[2,2,128,128]{3,2,1,0:T(8,128)(2,1)S(1)} collective-permute-done((bf16[2,2,128,128]{3,2,1,0:T(8,128)(2,1)S(1)}, bf16[2,2,128,128]{3,2,1,0:T(8,128)(2,1)S(1)}, u32[]{:S(2)}, u32[]{:S(2)}) %collective-permute-start.6) | collective-permute-done | bytes 131104 | tf_op jit(solution)/shard_map/ppermute | solution.py:18
  127.8 1.8 %collective-permute-done.7 = bf16[4,32,2048]{2,1,0:T(8,128)(2,1)S(1)} collective-permute-done((bf16[4,32,2048]{2,1,0:T(8,128)(2,1)S(1)}, bf16[4,32,2048]{2,1,0:T(8,128)(2,1)S(1)}, u32[]{:S(2)}, u32[]{:S(2)}) %collective-permute-start.7) | collective-permute-done | bytes 524320 | tf_op jit(solution)/shard_map/ppermute | solution.py:210
  131.0 1.6 %collective-permute-start.8 = (bf16[32,2048]{1,0:T(8,128)(2,1)S(1)}, bf16[32,2048]{1,0:T(8,128)(2,1)S(1)}, u32[]{:S(2)}, u32[]{:S(2)}) collective-permute-start(bf16[32,2048]{1,0:T(8,128)(2,1)S(1)} %get-tuple-element.11), channel_id=1, source_target_pairs={{0,2},{1,3},{2,4},{3,5},{4,6},{5,7},{6,0},{7,1},{8,10},{9,11},{10,... | collective-permute-start | bytes 393224 | tf_op jit(solution)/shard_map/ppermute | solution.py:216
  132.5 1.7 %collective-permute-start.10 = (bf16[32,2048]{1,0:T(8,128)(2,1)S(1)}, bf16[32,2048]{1,0:T(8,128)(2,1)S(1)}, u32[]{:S(2)}, u32[]{:S(2)}) collective-permute-start(bf16[32,2048]{1,0:T(8,128)(2,1)S(1)} %get-tuple-element.12), channel_id=1, source_target_pairs={{0,6},{1,7},{2,0},{3,1},{4,2},{5,3},{6,4},{7,5},{8,14},{9,15},{10,... | collective-permute-start | bytes 393224 | tf_op jit(solution)/shard_map/ppermute | solution.py:216
  134.3 1.8 %collective-permute-start.9 = (bf16[32,2048]{1,0:T(8,128)(2,1)S(1)}, bf16[32,2048]{1,0:T(8,128)(2,1)S(1)}, u32[]{:S(2)}, u32[]{:S(2)}) collective-permute-start(bf16[32,2048]{1,0:T(8,128)(2,1)S(1)} %get-tuple-element.13), channel_id=1, source_target_pairs={{0,4},{1,5},{2,6},{3,7},{4,0},{5,1},{6,2},{7,3},{8,12},{9,13},{10,... | collective-permute-start | bytes 393224 | tf_op jit(solution)/shard_map/ppermute | solution.py:216
  136.1 1.7 %collective-permute-done.8 = bf16[32,2048]{1,0:T(8,128)(2,1)S(1)} collective-permute-done((bf16[32,2048]{1,0:T(8,128)(2,1)S(1)}, bf16[32,2048]{1,0:T(8,128)(2,1)S(1)}, u32[]{:S(2)}, u32[]{:S(2)}) %collective-permute-start.8) | collective-permute-done | bytes 131104 | tf_op jit(solution)/shard_map/ppermute | solution.py:216
  137.8 2.1 %collective-permute-done.10 = bf16[32,2048]{1,0:T(8,128)(2,1)S(1)} collective-permute-done((bf16[32,2048]{1,0:T(8,128)(2,1)S(1)}, bf16[32,2048]{1,0:T(8,128)(2,1)S(1)}, u32[]{:S(2)}, u32[]{:S(2)}) %collective-permute-start.10) | collective-permute-done | bytes 131104 | tf_op jit(solution)/shard_map/ppermute | solution.py:216
  139.9 1.7 %collective-permute-done.9 = bf16[32,2048]{1,0:T(8,128)(2,1)S(1)} collective-permute-done((bf16[32,2048]{1,0:T(8,128)(2,1)S(1)}, bf16[32,2048]{1,0:T(8,128)(2,1)S(1)}, u32[]{:S(2)}, u32[]{:S(2)}) %collective-permute-start.9) | collective-permute-done | bytes 131104 | tf_op jit(solution)/shard_map/ppermute | solution.py:216
  (163 shorter events, 55.4 us)
Async XLA Ops:
  0.0 125.4 %copy-start = (bf16[512,2048]{1,0:T(8,128)(2,1)S(1)}, bf16[512,2048]{1,0:T(8,128)(2,1)}, u32[]{:S(2)}) copy-start(bf16[512,2048]{1,0:T(8,128)(2,1)} %param.21) | copy-start | bytes 6291460
  2.2 11.3 %collective-permute-start = (bf16[3,1024]{1,0:T(4,128)(2,1)S(1)}, bf16[3,1024]{1,0:T(4,128)(2,1)S(1)}, u32[]{:S(2)}, u32[]{:S(2)}) collective-permute-start(bf16[3,1024]{1,0:T(4,128)(2,1)S(1)} %pad_maximum_fusion.4), channel_id=1, source_target_pairs={{0,8},{8,16},{16,24},{24,32},{32,40},{40,48},{48,56},{56,64},{64,7... | collective-permute-start | bytes 18440 | tf_op jit(solution)/shard_map/ppermute | solution.py:18
  17.8 2.5 %copy-start.26 = (pred[128,128]{1,0:T(8,128)(4,1)S(1)}, pred[128,128]{1,0:T(8,128)(4,1)}, u32[]{:S(2)}) copy-start(pred[128,128]{1,0:T(8,128)(4,1)} %get-tuple-element.50) | copy-start | bytes 49156
  33.9 3.0 %copy-start.11 = (f32[2,2,2,128,128]{4,3,2,1,0:T(8,128)}, f32[2,2,2,128,128]{4,3,2,1,0:T(8,128)S(1)}, u32[]{:S(2)}) copy-start(f32[2,2,2,128,128]{4,3,2,1,0:T(8,128)S(1)} %convolution_bitcast_fusion.1) | copy-start | bytes 1572868
  35.0 3.1 %copy-start.2 = (f32[2,2,2,128,128]{4,3,2,1,0:T(8,128)}, f32[2,2,2,128,128]{4,3,2,1,0:T(8,128)S(1)}, u32[]{:S(2)}) copy-start(f32[2,2,2,128,128]{4,3,2,1,0:T(8,128)S(1)} %fusion.2) | copy-start | bytes 1572868
  35.4 6.2 %copy-start.30 = (bf16[128]{0:T(256)(128)(2,1)S(1)}, bf16[128]{0:T(256)(128)(2,1)}, u32[]{:S(2)}) copy-start(bf16[128]{0:T(256)(128)(2,1)} %param.20) | copy-start | bytes 772
  37.4 4.3 %copy-start.16 = (f32[2,2,128,128]{3,2,1,0:T(8,128)}, f32[2,2,128,128]{3,2,1,0:T(8,128)S(1)}, u32[]{:S(2)}) copy-start(f32[2,2,128,128]{3,2,1,0:T(8,128)S(1)} %convolution_add_fusion.8) | copy-start | bytes 786436
  37.4 21.0 %copy-start.29 = (bf16[4,256]{1,0:T(4,128)(2,1)S(1)}, bf16[4,256]{1,0:T(4,128)(2,1)}, u32[]{:S(2)}) copy-start(bf16[4,256]{1,0:T(4,128)(2,1)} %param.17) | copy-start | bytes 6148
  38.2 13.3 %collective-permute-start.1 = (bf16[2,2,2,128,128]{4,3,2,1,0:T(8,128)(2,1)}, bf16[2,2,2,128,128]{4,3,2,1,0:T(8,128)(2,1)}, u32[]{:S(2)}, u32[]{:S(2)}) collective-permute-start(bf16[2,2,2,128,128]{4,3,2,1,0:T(8,128)(2,1)} %pad_maximum_fusion), channel_id=1, source_target_pairs={{0,8},{8,16},{16,24},{24,32},{32,40},{40,48},{48,56},{56,64},{64,7... | collective-permute-start | bytes 786440 | tf_op jit(solution)/shard_map/ppermute | solution.py:18
  56.4 12.7 %collective-permute-start.2 = (bf16[2,2,2,128,128]{4,3,2,1,0:T(8,128)(2,1)}, bf16[2,2,2,128,128]{4,3,2,1,0:T(8,128)(2,1)}, u32[]{:S(2)}, u32[]{:S(2)}) collective-permute-start(bf16[2,2,2,128,128]{4,3,2,1,0:T(8,128)(2,1)} %pad_maximum_fusion.1), channel_id=1, source_target_pairs={{0,16},{8,24},{16,32},{24,40},{32,48},{40,56},{48,64},{56,72},{64,... | collective-permute-start | bytes 786440 | tf_op jit(solution)/shard_map/ppermute | solution.py:18
  58.4 17.6 %copy-start.1 = (f32[259,256]{1,0:T(8,128)S(1)}, f32[259,256]{1,0:T(8,128)}, u32[]{:S(2)}) copy-start(f32[259,256]{1,0:T(8,128)} %get-tuple-element.42) | copy-start | bytes 795652
  74.0 9.8 %collective-permute-start.3 = (bf16[2,2,2,128,128]{4,3,2,1,0:T(8,128)(2,1)}, bf16[2,2,2,128,128]{4,3,2,1,0:T(8,128)(2,1)}, u32[]{:S(2)}, u32[]{:S(2)}) collective-permute-start(bf16[2,2,2,128,128]{4,3,2,1,0:T(8,128)(2,1)} %pad_maximum_fusion.2), channel_id=1, source_target_pairs={{0,32},{8,40},{16,48},{24,56},{32,64},{40,72},{48,80},{56,88},{64,... | collective-permute-start | bytes 786440 | tf_op jit(solution)/shard_map/ppermute | solution.py:18
  78.6 6.6 %copy-start.10 = (f32[2,2,128,128]{3,2,1,0:T(8,128)S(1)}, f32[2,2,128,128]{3,2,1,0:T(8,128)}, u32[]{:S(2)}) copy-start(f32[2,2,128,128]{3,2,1,0:T(8,128)} %copy-done.9) | copy-start | bytes 786436
  78.6 6.6 %copy-start.15 = (f32[2,2,128,128]{3,2,1,0:T(8,128)S(1)}, f32[2,2,128,128]{3,2,1,0:T(8,128)}, u32[]{:S(2)}) copy-start(f32[2,2,128,128]{3,2,1,0:T(8,128)} %copy-done.14) | copy-start | bytes 786436
  86.5 28.1 %copy-start.6 = (f32[2,2,2,128,128]{4,3,2,1,0:T(8,128)S(1)}, f32[2,2,2,128,128]{4,3,2,1,0:T(8,128)}, u32[]{:S(2)}) copy-start(f32[2,2,2,128,128]{4,3,2,1,0:T(8,128)} %copy-done.5) | copy-start | bytes 1572868
  86.5 14.6 %collective-permute-start.4 = (bf16[2,2,2,128,128]{4,3,2,1,0:T(8,128)(2,1)S(1)}, bf16[2,2,2,128,128]{4,3,2,1,0:T(8,128)(2,1)S(1)}, u32[]{:S(2)}, u32[]{:S(2)}) collective-permute-start(bf16[2,2,2,128,128]{4,3,2,1,0:T(8,128)(2,1)S(1)} %pad_maximum_fusion.3), channel_id=1, source_target_pairs={{0,64},{8,72},{16,80},{24,88},{32,96},{40,104},{48,112},{56,120},{... | collective-permute-start | bytes 786440 | tf_op jit(solution)/shard_map/ppermute | solution.py:18
  89.4 33.2 %copy-start.3 = (f32[2,2,2,128,128]{4,3,2,1,0:T(8,128)S(1)}, f32[2,2,2,128,128]{4,3,2,1,0:T(8,128)}, u32[]{:S(2)}) copy-start(f32[2,2,2,128,128]{4,3,2,1,0:T(8,128)} %copy-done.2) | copy-start | bytes 1572868
  89.4 33.2 %copy-start.12 = (f32[2,2,2,128,128]{4,3,2,1,0:T(8,128)S(1)}, f32[2,2,2,128,128]{4,3,2,1,0:T(8,128)}, u32[]{:S(2)}) copy-start(f32[2,2,2,128,128]{4,3,2,1,0:T(8,128)} %copy-done.11) | copy-start | bytes 1572868
  101.4 10.8 %collective-permute-start.5 = (bf16[2,2,128,128]{3,2,1,0:T(8,128)(2,1)S(1)}, bf16[2,2,128,128]{3,2,1,0:T(8,128)(2,1)S(1)}, u32[]{:S(2)}, u32[]{:S(2)}) collective-permute-start(bf16[2,2,128,128]{3,2,1,0:T(8,128)(2,1)S(1)} %get-tuple-element.40), channel_id=1, source_target_pairs={{0,128},{8,136},{16,144},{24,152},{32,160},{40,168},{48,176},{56,1... | collective-permute-start | bytes 393224 | tf_op jit(solution)/shard_map/ppermute | solution.py:18
  112.4 10.2 %collective-permute-start.6 = (bf16[2,2,128,128]{3,2,1,0:T(8,128)(2,1)S(1)}, bf16[2,2,128,128]{3,2,1,0:T(8,128)(2,1)S(1)}, u32[]{:S(2)}, u32[]{:S(2)}) collective-permute-start(bf16[2,2,128,128]{3,2,1,0:T(8,128)(2,1)S(1)} %fusion.13), channel_id=1, source_target_pairs={{0,8},{8,16},{16,24},{24,32},{32,40},{40,48},{48,56},{56,64},{64,7... | collective-permute-start | bytes 393224 | tf_op jit(solution)/shard_map/ppermute | solution.py:18
  127.6 2.0 %collective-permute-start.7 = (bf16[4,32,2048]{2,1,0:T(8,128)(2,1)S(1)}, bf16[4,32,2048]{2,1,0:T(8,128)(2,1)S(1)}, u32[]{:S(2)}, u32[]{:S(2)}) collective-permute-start(bf16[4,32,2048]{2,1,0:T(8,128)(2,1)S(1)} %fusion.23), channel_id=1, source_target_pairs={{0,1},{1,0},{2,3},{3,2},{4,5},{5,4},{6,7},{7,6},{8,9},{9,8},{10,11... | collective-permute-start | bytes 1572872 | tf_op jit(solution)/shard_map/ppermute | solution.py:210
  131.0 6.8 %collective-permute-start.8 = (bf16[32,2048]{1,0:T(8,128)(2,1)S(1)}, bf16[32,2048]{1,0:T(8,128)(2,1)S(1)}, u32[]{:S(2)}, u32[]{:S(2)}) collective-permute-start(bf16[32,2048]{1,0:T(8,128)(2,1)S(1)} %get-tuple-element.11), channel_id=1, source_target_pairs={{0,2},{1,3},{2,4},{3,5},{4,6},{5,7},{6,0},{7,1},{8,10},{9,11},{10,... | collective-permute-start | bytes 393224 | tf_op jit(solution)/shard_map/ppermute | solution.py:216
  132.5 7.4 %collective-permute-start.10 = (bf16[32,2048]{1,0:T(8,128)(2,1)S(1)}, bf16[32,2048]{1,0:T(8,128)(2,1)S(1)}, u32[]{:S(2)}, u32[]{:S(2)}) collective-permute-start(bf16[32,2048]{1,0:T(8,128)(2,1)S(1)} %get-tuple-element.12), channel_id=1, source_target_pairs={{0,6},{1,7},{2,0},{3,1},{4,2},{5,3},{6,4},{7,5},{8,14},{9,15},{10,... | collective-permute-start | bytes 393224 | tf_op jit(solution)/shard_map/ppermute | solution.py:216
  134.3 7.3 %collective-permute-start.9 = (bf16[32,2048]{1,0:T(8,128)(2,1)S(1)}, bf16[32,2048]{1,0:T(8,128)(2,1)S(1)}, u32[]{:S(2)}, u32[]{:S(2)}) collective-permute-start(bf16[32,2048]{1,0:T(8,128)(2,1)S(1)} %get-tuple-element.13), channel_id=1, source_target_pairs={{0,4},{1,5},{2,6},{3,7},{4,0},{5,1},{6,2},{7,3},{8,12},{9,13},{10,... | collective-permute-start | bytes 393224 | tf_op jit(solution)/shard_map/ppermute | solution.py:216
  (18 other events, 26.3 us)

commit v10 on v8

--- a/solution.py
+++ b/solution.py
@@ -113,22 +113,20 @@
     seq_index = lax.axis_index("seq")
     prefix_map, prefix_end = total_map, local_end
     distance = 1
-    while distance < seq_size:
-        if 2 * distance < seq_size:
-            earlier_map, earlier_end = shifted(
-                jnp.stack([prefix_map, prefix_end]).astype(jnp.bfloat16), "seq", distance
-            ).astype(jnp.float32)
-            prefix_end = apply_map(prefix_map, earlier_end) + prefix_end
-            prefix_map = jnp.where(
-                seq_index >= distance, apply_map(prefix_map, earlier_map), prefix_map
-            )
-        else:
-            earlier_end = shifted(prefix_end.astype(jnp.bfloat16), "seq", distance).astype(
-                jnp.float32
-            )
-            prefix_end = apply_map(prefix_map, earlier_end) + prefix_end
+    while 2 * distance < seq_size:
+        earlier_map, earlier_end = shifted(
+            jnp.stack([prefix_map, prefix_end]).astype(jnp.bfloat16), "seq", distance
+        ).astype(jnp.float32)
+        prefix_end = apply_map(prefix_map, earlier_end) + prefix_end
+        prefix_map = jnp.where(
+            seq_index >= distance, apply_map(prefix_map, earlier_map), prefix_map
+        )
         distance *= 2
-    incoming = shifted(prefix_end.astype(jnp.bfloat16), "seq", 1).astype(jnp.float32)
+    last_map, last_end = shifted(
+        jnp.stack([prefix_map, prefix_end]).astype(jnp.bfloat16), "seq", 1
+    ).astype(jnp.float32)
+    far_end = shifted(prefix_end.astype(jnp.bfloat16), "seq", distance + 1).astype(jnp.float32)
+    incoming = apply_map(last_map, far_end) + last_end
 
     def replay(state_now, span_in):
         transit_now, inject_now, coupling_now, local_now = span_in

time: 128 us -> 123 us (0.961)
  the two profiles are of different devices: /device:TPU:128 before, /device:TPU:17 now
where the time goes in v10:
time: 123 us
  starting transfers between devices  62.6 us (51%)
  matrix products  27.7 us (23%)
  local copies, waits for them, and re-layouts  12.1 us (10%)
  waiting for transfers between devices  10.2 us (8%)
  other arithmetic  8.76 us (7%)
  between operations  1.24 us (1%)
    ppermute x13, starting transfers between devices, shifted(): return lax.ppermute(array, axis, pairs)  49.7 us
    ppermute x1, starting transfers between devices, shards(): lax.ppermute(pieces[:, 1 - parity].astype(jnp.bfloat16), 'head', sibling_...  9.29 us
    ppermute x3, waiting for transfers between devices, shards(): summed = summed + lax.ppermute(outgoing, 'head', pairs).astype(jnp.float32)  8.6 us
    dot_general x7, matrix products, unit_lower_inverse(): jnp.einsum('...ij,...jk->...ik', inverse, coupling, precision=highest)  7.43 us
    dot_general x28, matrix products, apply_map(): return jnp.einsum('hrke,hrev->hrkv', matrix, state_now, precision=highest)  6.18 us
    dot_general x7, matrix products, unit_lower_inverse(): jnp.einsum('...ij,...jk->...ik', jnp.einsum('...ij,...jk->...ik', inverse...  4.51 us
    ppermute x3, starting transfers between devices, shards(): summed = summed + lax.ppermute(outgoing, 'head', pairs).astype(jnp.float32)  3.68 us
    slice x3, local copies, waits for them, and re-layouts, conv_silu(): summed = summed + conv_taps[offset] * padded[offset:offset + length]  3.1 us
  transfers between devices with their start and end apart: 17, of which 5 were waited for; matrix products, arithmetic and copies ran while one was open for 12% of the time, Pallas kernels for 0%

profile of v10, /device:TPU:17, one launch (start us, length us, event | category | flops | bytes accessed | tf_op | source)
XLA Modules:
  0.0 122.6 jit_solution(12732250088846186022)
XLA Ops:
  2.2 2.9 %collective-permute-start = (bf16[3,1024]{1,0:T(4,128)(2,1)S(1)}, bf16[3,1024]{1,0:T(4,128)(2,1)S(1)}, u32[]{:S(2)}, u32[]{:S(2)}) collective-permute-start(bf16[3,1024]{1,0:T(4,128)(2,1)S(1)} %pad_maximum_fusion.10), channel_id=1, source_target_pairs={{0,8},{8,16},{16,24},{24,32},{32,40},{40,48},{48,56},{56,64},{64,7... | collective-permute-start | bytes 18440 | tf_op jit(solution)/shard_map/ppermute | solution.py:18
  8.8 1.4 %fusion.158 = (f32[1,512]{1,0:T(1,128)S(1)}, f32[1,512]{1,0:T(1,128)}, f32[1,512]{1,0:T(1,128)}, f32[1,512]{1,0:T(1,128)}) fusion(bf16[4,512]{1,0:T(4,128)(2,1)} %param.19), kind=kLoop, calls=%fused_computation.340 | loop fusion | bytes 16384 | tf_op jit(solution)/shard_map/slice | solution.py:27
  15.3 1.4 %fusion.154 = f32[2,2,128,128]{3,2,1,0:T(8,128)} fusion(f32[2,2,128,128]{3,2,1,0:T(8,128)S(1)} %fusion.66, f32[2,128,2,128]{3,2,1,0:T(2,128)S(1)} %reshape.1248), kind=kOutput, calls=%fused_computation.336 | convolution fusion | flops 100663296 | bytes 786432 | tf_op jit(solution)/shard_map/hxnck,hxnek->hxnce/dot_general | solution.py:64
  26.8 2.1 %fusion.37 = f32[2,2,2,128,128]{4,3,2,1,0:T(8,128)S(1)} fusion(f32[2,2,2,128,128]{4,3,2,1,0:T(8,128)S(1)} %fusion.3, f32[2,2,128,128]{3,2,1,0:T(8,128)} %copy-done.5, f32[2,2,2,128]{3,2,1,0:T(2,128)S(1)} %mul.296, f32[128,128]{1,0:T(8,128)S(1)} %fusion.141, f32[2,2,2,128]{3,2,1,0:T(2,128)S(1)} %reduce_window_sum.11, ...), kind=kOutput, calls=%fused_computation.87 | convolution fusion | flops 202375168 | bytes 1433600 | tf_op jit(solution)/shard_map/...ij,...jk->...ik/dot_general | solution.py:43
  31.1 1.2 %bitcast_multiply_fusion.1 = f32[2,2,2,128,128]{4,3,2,1,0:T(8,128)S(1)} fusion(f32[2,128,2,2,128]{4,3,2,1,0:T(2,128)} %reshape.1250, f32[2,2,2,128]{3,2,1,0:T(2,128)S(1)} %mul.296), kind=kLoop, calls=%fused_computation.82 | loop fusion | flops 131072 | bytes 1052672 | tf_op jit(solution)/shard_map/mul | solution.py:69
  37.2 3.3 %collective-permute-start.7 = (bf16[2,1,2,128,128]{4,3,2,1,0:T(8,128)(2,1)S(1)}, bf16[2,1,2,128,128]{4,3,2,1,0:T(8,128)(2,1)S(1)}, u32[]{:S(2)}, u32[]{:S(2)}) collective-permute-start(bf16[2,1,2,128,128]{4,3,2,1,0:T(8,128)(2,1)S(1)} %pad_maximum_fusion.5), channel_id=1, source_target_pairs={{0,8},{8,16},{16,24},{24,32},{32,40},{40,48},{48,56},{56,64},{64,7... | collective-permute-start | bytes 393224 | tf_op jit(solution)/shard_map/ppermute | solution.py:18
  42.9 3.2 %collective-permute-start.1 = (bf16[2,1,2,128,128]{4,3,2,1,0:T(8,128)(2,1)S(1)}, bf16[2,1,2,128,128]{4,3,2,1,0:T(8,128)(2,1)S(1)}, u32[]{:S(2)}, u32[]{:S(2)}) collective-permute-start(bf16[2,1,2,128,128]{4,3,2,1,0:T(8,128)(2,1)S(1)} %pad_maximum_fusion), channel_id=1, source_target_pairs={{0,8},{8,16},{16,24},{24,32},{32,40},{40,48},{48,56},{56,64},{64,7... | collective-permute-start | bytes 393224 | tf_op jit(solution)/shard_map/ppermute | solution.py:18
  47.5 3.3 %collective-permute-start.8 = (bf16[2,1,2,128,128]{4,3,2,1,0:T(8,128)(2,1)S(1)}, bf16[2,1,2,128,128]{4,3,2,1,0:T(8,128)(2,1)S(1)}, u32[]{:S(2)}, u32[]{:S(2)}) collective-permute-start(bf16[2,1,2,128,128]{4,3,2,1,0:T(8,128)(2,1)S(1)} %pad_maximum_fusion.6), channel_id=1, source_target_pairs={{0,16},{8,24},{16,32},{24,40},{32,48},{40,56},{48,64},{56,72},{64,... | collective-permute-start | bytes 393224 | tf_op jit(solution)/shard_map/ppermute | solution.py:18
  51.3 4.8 %collective-permute-start.2 = (bf16[2,1,2,128,128]{4,3,2,1,0:T(8,128)(2,1)S(1)}, bf16[2,1,2,128,128]{4,3,2,1,0:T(8,128)(2,1)S(1)}, u32[]{:S(2)}, u32[]{:S(2)}) collective-permute-start(bf16[2,1,2,128,128]{4,3,2,1,0:T(8,128)(2,1)S(1)} %pad_maximum_fusion.1), channel_id=1, source_target_pairs={{0,16},{8,24},{16,32},{24,40},{32,48},{40,56},{48,64},{56,72},{64,... | collective-permute-start | bytes 393224 | tf_op jit(solution)/shard_map/ppermute | solution.py:18
  56.6 3.5 %collective-permute-start.9 = (bf16[2,1,2,128,128]{4,3,2,1,0:T(8,128)(2,1)S(1)}, bf16[2,1,2,128,128]{4,3,2,1,0:T(8,128)(2,1)S(1)}, u32[]{:S(2)}, u32[]{:S(2)}) collective-permute-start(bf16[2,1,2,128,128]{4,3,2,1,0:T(8,128)(2,1)S(1)} %pad_maximum_fusion.7), channel_id=1, source_target_pairs={{0,32},{8,40},{16,48},{24,56},{32,64},{40,72},{48,80},{56,88},{64,... | collective-permute-start | bytes 393224 | tf_op jit(solution)/shard_map/ppermute | solution.py:18
  60.7 4.8 %collective-permute-start.3 = (bf16[2,1,2,128,128]{4,3,2,1,0:T(8,128)(2,1)S(1)}, bf16[2,1,2,128,128]{4,3,2,1,0:T(8,128)(2,1)S(1)}, u32[]{:S(2)}, u32[]{:S(2)}) collective-permute-start(bf16[2,1,2,128,128]{4,3,2,1,0:T(8,128)(2,1)S(1)} %pad_maximum_fusion.2), channel_id=1, source_target_pairs={{0,32},{8,40},{16,48},{24,56},{32,64},{40,72},{48,80},{56,88},{64,... | collective-permute-start | bytes 393224 | tf_op jit(solution)/shard_map/ppermute | solution.py:18
  65.9 3.2 %collective-permute-start.10 = (bf16[2,1,2,128,128]{4,3,2,1,0:T(8,128)(2,1)S(1)}, bf16[2,1,2,128,128]{4,3,2,1,0:T(8,128)(2,1)S(1)}, u32[]{:S(2)}, u32[]{:S(2)}) collective-permute-start(bf16[2,1,2,128,128]{4,3,2,1,0:T(8,128)(2,1)S(1)} %pad_maximum_fusion.8), channel_id=1, source_target_pairs={{0,64},{8,72},{16,80},{24,88},{32,96},{40,104},{48,112},{56,120},{... | collective-permute-start | bytes 393224 | tf_op jit(solution)/shard_map/ppermute | solution.py:18
  69.7 5.1 %collective-permute-start.4 = (bf16[2,1,2,128,128]{4,3,2,1,0:T(8,128)(2,1)S(1)}, bf16[2,1,2,128,128]{4,3,2,1,0:T(8,128)(2,1)S(1)}, u32[]{:S(2)}, u32[]{:S(2)}) collective-permute-start(bf16[2,1,2,128,128]{4,3,2,1,0:T(8,128)(2,1)S(1)} %pad_maximum_fusion.3), channel_id=1, source_target_pairs={{0,64},{8,72},{16,80},{24,88},{32,96},{40,104},{48,112},{56,120},{... | collective-permute-start | bytes 393224 | tf_op jit(solution)/shard_map/ppermute | solution.py:18
  75.3 2.7 %collective-permute-start.11 = (bf16[2,1,2,128,128]{4,3,2,1,0:T(8,128)(2,1)S(1)}, bf16[2,1,2,128,128]{4,3,2,1,0:T(8,128)(2,1)S(1)}, u32[]{:S(2)}, u32[]{:S(2)}) collective-permute-start(bf16[2,1,2,128,128]{4,3,2,1,0:T(8,128)(2,1)S(1)} %pad_maximum_fusion.9), channel_id=1, source_target_pairs={{0,8},{8,16},{16,24},{24,32},{32,40},{40,48},{48,56},{56,64},{64,7... | collective-permute-start | bytes 393224 | tf_op jit(solution)/shard_map/ppermute | solution.py:18
  77.9 8.2 %collective-permute-start.12 = (bf16[1,2,128,128]{3,2,1,0:T(8,128)(2,1)S(1)}, bf16[1,2,128,128]{3,2,1,0:T(8,128)(2,1)S(1)}, u32[]{:S(2)}, u32[]{:S(2)}) collective-permute-start(bf16[1,2,128,128]{3,2,1,0:T(8,128)(2,1)S(1)} %bitcast.315), channel_id=1, source_target_pairs={{0,136},{8,144},{16,152},{24,160},{32,168},{40,176},{48,184},{56,1... | collective-permute-start | bytes 196616 | tf_op jit(solution)/shard_map/ppermute | solution.py:18
  86.6 1.9 %collective-permute-start.5 = (bf16[2,1,2,128,128]{4,3,2,1,0:T(8,128)(2,1)S(1)}, bf16[2,1,2,128,128]{4,3,2,1,0:T(8,128)(2,1)S(1)}, u32[]{:S(2)}, u32[]{:S(2)}) collective-permute-start(bf16[2,1,2,128,128]{4,3,2,1,0:T(8,128)(2,1)S(1)} %pad_maximum_fusion.4), channel_id=1, source_target_pairs={{0,8},{8,16},{16,24},{24,32},{32,40},{40,48},{48,56},{56,64},{64,7... | collective-permute-start | bytes 393224 | tf_op jit(solution)/shard_map/ppermute | solution.py:18
  88.5 2.7 %collective-permute-start.6 = (bf16[1,2,128,128]{3,2,1,0:T(8,128)(2,1)S(1)}, bf16[1,2,128,128]{3,2,1,0:T(8,128)(2,1)S(1)}, u32[]{:S(2)}, u32[]{:S(2)}) collective-permute-start(bf16[1,2,128,128]{3,2,1,0:T(8,128)(2,1)S(1)} %bitcast.313), channel_id=1, source_target_pairs={{0,136},{8,144},{16,152},{24,160},{32,168},{40,176},{48,184},{56,1... | collective-permute-start | bytes 196616 | tf_op jit(solution)/shard_map/ppermute | solution.py:18
  96.0 1.3 %copy-done.1 = f32[4,2,32,2048]{3,2,1,0:T(8,128)} copy-done((f32[4,2,32,2048]{3,2,1,0:T(8,128)}, f32[4,2,32,2048]{3,2,1,0:T(8,128)S(1)}, u32[]{:S(2)}) %copy-start.1) | copy-done | bytes 2097176
  97.4 9.3 %collective-permute-start.13 = (bf16[4,32,2048]{2,1,0:T(8,128)(2,1)S(1)}, bf16[4,32,2048]{2,1,0:T(8,128)(2,1)S(1)}, u32[]{:S(2)}, u32[]{:S(2)}) collective-permute-start(bf16[4,32,2048]{2,1,0:T(8,128)(2,1)S(1)} %fusion.28), channel_id=1, source_target_pairs={{0,1},{1,0},{2,3},{3,2},{4,5},{5,4},{6,7},{7,6},{8,9},{9,8},{10,11... | collective-permute-start | bytes 1572872 | tf_op jit(solution)/shard_map/ppermute | solution.py:211
  106.7 1.5 %collective-permute-done.13 = bf16[4,32,2048]{2,1,0:T(8,128)(2,1)S(1)} collective-permute-done((bf16[4,32,2048]{2,1,0:T(8,128)(2,1)S(1)}, bf16[4,32,2048]{2,1,0:T(8,128)(2,1)S(1)}, u32[]{:S(2)}, u32[]{:S(2)}) %collective-permute-start.13) | collective-permute-done | bytes 524320 | tf_op jit(solution)/shard_map/ppermute | solution.py:211
  108.2 1.3 %fusion.23 = bf16[4,32,2048]{2,1,0:T(8,128)(2,1)S(1)} fusion(bf16[4,32,2048]{2,1,0:T(8,128)(2,1)S(1)} %collective-permute-done.13, f32[4,2,32,2048]{3,2,1,0:T(8,128)} %copy-done.1, s32[]{:T(128)S(6)} %select_n.339), kind=kLoop, calls=%fused_computation.61 | loop fusion | flops 786432 | bytes 2097156 | tf_op jit(solution)/shard_map/convert_element_type | solution.py:212
  109.6 2.5 %collective-permute-start.16 = (bf16[32,2048]{1,0:T(8,128)(2,1)S(1)}, bf16[32,2048]{1,0:T(8,128)(2,1)S(1)}, u32[]{:S(2)}, u32[]{:S(2)}) collective-permute-start(bf16[32,2048]{1,0:T(8,128)(2,1)S(1)} %get-tuple-element.10), channel_id=1, source_target_pairs={{0,6},{1,7},{2,0},{3,1},{4,2},{5,3},{6,4},{7,5},{8,14},{9,15},{10,... | collective-permute-start | bytes 393224 | tf_op jit(solution)/shard_map/ppermute | solution.py:217
  113.3 4.0 %collective-permute-done.16 = bf16[32,2048]{1,0:T(8,128)(2,1)S(1)} collective-permute-done((bf16[32,2048]{1,0:T(8,128)(2,1)S(1)}, bf16[32,2048]{1,0:T(8,128)(2,1)S(1)}, u32[]{:S(2)}, u32[]{:S(2)}) %collective-permute-start.16) | collective-permute-done | bytes 131104 | tf_op jit(solution)/shard_map/ppermute | solution.py:217
  118.1 3.8 %collective-permute-done.14 = bf16[32,2048]{1,0:T(8,128)(2,1)S(1)} collective-permute-done((bf16[32,2048]{1,0:T(8,128)(2,1)S(1)}, bf16[32,2048]{1,0:T(8,128)(2,1)S(1)}, u32[]{:S(2)}, u32[]{:S(2)}) %collective-permute-start.14) | collective-permute-done | bytes 131104 | tf_op jit(solution)/shard_map/ppermute | solution.py:217
  (169 shorter events, 41.7 us)
Async XLA Ops:
  0.0 95.3 %copy-start = (bf16[512,2048]{1,0:T(8,128)(2,1)S(1)}, bf16[512,2048]{1,0:T(8,128)(2,1)}, u32[]{:S(2)}) copy-start(bf16[512,2048]{1,0:T(8,128)(2,1)} %param.21) | copy-start | bytes 6291460
  2.2 9.8 %collective-permute-start = (bf16[3,1024]{1,0:T(4,128)(2,1)S(1)}, bf16[3,1024]{1,0:T(4,128)(2,1)S(1)}, u32[]{:S(2)}, u32[]{:S(2)}) collective-permute-start(bf16[3,1024]{1,0:T(4,128)(2,1)S(1)} %pad_maximum_fusion.10), channel_id=1, source_target_pairs={{0,8},{8,16},{16,24},{24,32},{32,40},{40,48},{48,56},{56,64},{64,7... | collective-permute-start | bytes 18440 | tf_op jit(solution)/shard_map/ppermute | solution.py:18
  14.9 10.2 %copy-start.5 = (f32[2,2,128,128]{3,2,1,0:T(8,128)}, f32[2,2,128,128]{3,2,1,0:T(8,128)S(1)}, u32[]{:S(2)}) copy-start(f32[2,2,128,128]{3,2,1,0:T(8,128)S(1)} %fusion.161) | copy-start | bytes 786436
  26.8 2.9 %copy-start.7 = (f32[1,512]{1,0:T(1,128)S(1)}, f32[1,512]{1,0:T(1,128)}, u32[]{:S(2)}) copy-start(f32[1,512]{1,0:T(1,128)} %get-tuple-element.28) | copy-start | bytes 6148
  26.8 2.9 %copy-start.8 = (f32[1,512]{1,0:T(1,128)S(1)}, f32[1,512]{1,0:T(1,128)}, u32[]{:S(2)}) copy-start(f32[1,512]{1,0:T(1,128)} %get-tuple-element.29) | copy-start | bytes 6148
  26.8 2.9 %copy-start.9 = (f32[1,512]{1,0:T(1,128)S(1)}, f32[1,512]{1,0:T(1,128)}, u32[]{:S(2)}) copy-start(f32[1,512]{1,0:T(1,128)} %get-tuple-element.30) | copy-start | bytes 6148
  34.8 5.7 %copy-start.2 = (f32[2,2,128,128]{3,2,1,0:T(8,128)S(1)}, f32[2,2,128,128]{3,2,1,0:T(8,128)}, u32[]{:S(2)}) copy-start(f32[2,2,128,128]{3,2,1,0:T(8,128)} %fusion.154) | copy-start | bytes 786436
  37.1 9.0 %copy-start.3 = (f32[2,128,2,128]{3,1,0,2:T(8,128)S(1)}, f32[2,128,2,128]{3,1,0,2:T(8,128)}, u32[]{:S(2)}) copy-start(f32[2,128,2,128]{3,1,0,2:T(8,128)} %copy.91) | copy-start | bytes 786436
  37.2 9.9 %collective-permute-start.7 = (bf16[2,1,2,128,128]{4,3,2,1,0:T(8,128)(2,1)S(1)}, bf16[2,1,2,128,128]{4,3,2,1,0:T(8,128)(2,1)S(1)}, u32[]{:S(2)}, u32[]{:S(2)}) collective-permute-start(bf16[2,1,2,128,128]{4,3,2,1,0:T(8,128)(2,1)S(1)} %pad_maximum_fusion.5), channel_id=1, source_target_pairs={{0,8},{8,16},{16,24},{24,32},{32,40},{40,48},{48,56},{56,64},{64,7... | collective-permute-start | bytes 393224 | tf_op jit(solution)/shard_map/ppermute | solution.py:18
  42.9 7.9 %collective-permute-start.1 = (bf16[2,1,2,128,128]{4,3,2,1,0:T(8,128)(2,1)S(1)}, bf16[2,1,2,128,128]{4,3,2,1,0:T(8,128)(2,1)S(1)}, u32[]{:S(2)}, u32[]{:S(2)}) collective-permute-start(bf16[2,1,2,128,128]{4,3,2,1,0:T(8,128)(2,1)S(1)} %pad_maximum_fusion), channel_id=1, source_target_pairs={{0,8},{8,16},{16,24},{24,32},{32,40},{40,48},{48,56},{56,64},{64,7... | collective-permute-start | bytes 393224 | tf_op jit(solution)/shard_map/ppermute | solution.py:18
  47.5 8.6 %collective-permute-start.8 = (bf16[2,1,2,128,128]{4,3,2,1,0:T(8,128)(2,1)S(1)}, bf16[2,1,2,128,128]{4,3,2,1,0:T(8,128)(2,1)S(1)}, u32[]{:S(2)}, u32[]{:S(2)}) collective-permute-start(bf16[2,1,2,128,128]{4,3,2,1,0:T(8,128)(2,1)S(1)} %pad_maximum_fusion.6), channel_id=1, source_target_pairs={{0,16},{8,24},{16,32},{24,40},{32,48},{40,56},{48,64},{56,72},{64,... | collective-permute-start | bytes 393224 | tf_op jit(solution)/shard_map/ppermute | solution.py:18
  51.3 8.9 %collective-permute-start.2 = (bf16[2,1,2,128,128]{4,3,2,1,0:T(8,128)(2,1)S(1)}, bf16[2,1,2,128,128]{4,3,2,1,0:T(8,128)(2,1)S(1)}, u32[]{:S(2)}, u32[]{:S(2)}) collective-permute-start(bf16[2,1,2,128,128]{4,3,2,1,0:T(8,128)(2,1)S(1)} %pad_maximum_fusion.1), channel_id=1, source_target_pairs={{0,16},{8,24},{16,32},{24,40},{32,48},{40,56},{48,64},{56,72},{64,... | collective-permute-start | bytes 393224 | tf_op jit(solution)/shard_map/ppermute | solution.py:18
  56.6 8.8 %collective-permute-start.9 = (bf16[2,1,2,128,128]{4,3,2,1,0:T(8,128)(2,1)S(1)}, bf16[2,1,2,128,128]{4,3,2,1,0:T(8,128)(2,1)S(1)}, u32[]{:S(2)}, u32[]{:S(2)}) collective-permute-start(bf16[2,1,2,128,128]{4,3,2,1,0:T(8,128)(2,1)S(1)} %pad_maximum_fusion.7), channel_id=1, source_target_pairs={{0,32},{8,40},{16,48},{24,56},{32,64},{40,72},{48,80},{56,88},{64,... | collective-permute-start | bytes 393224 | tf_op jit(solution)/shard_map/ppermute | solution.py:18
  60.7 8.5 %collective-permute-start.3 = (bf16[2,1,2,128,128]{4,3,2,1,0:T(8,128)(2,1)S(1)}, bf16[2,1,2,128,128]{4,3,2,1,0:T(8,128)(2,1)S(1)}, u32[]{:S(2)}, u32[]{:S(2)}) collective-permute-start(bf16[2,1,2,128,128]{4,3,2,1,0:T(8,128)(2,1)S(1)} %pad_maximum_fusion.2), channel_id=1, source_target_pairs={{0,32},{8,40},{16,48},{24,56},{32,64},{40,72},{48,80},{56,88},{64,... | collective-permute-start | bytes 393224 | tf_op jit(solution)/shard_map/ppermute | solution.py:18
  65.9 8.9 %collective-permute-start.10 = (bf16[2,1,2,128,128]{4,3,2,1,0:T(8,128)(2,1)S(1)}, bf16[2,1,2,128,128]{4,3,2,1,0:T(8,128)(2,1)S(1)}, u32[]{:S(2)}, u32[]{:S(2)}) collective-permute-start(bf16[2,1,2,128,128]{4,3,2,1,0:T(8,128)(2,1)S(1)} %pad_maximum_fusion.8), channel_id=1, source_target_pairs={{0,64},{8,72},{16,80},{24,88},{32,96},{40,104},{48,112},{56,120},{... | collective-permute-start | bytes 393224 | tf_op jit(solution)/shard_map/ppermute | solution.py:18
  69.7 16.4 %collective-permute-start.4 = (bf16[2,1,2,128,128]{4,3,2,1,0:T(8,128)(2,1)S(1)}, bf16[2,1,2,128,128]{4,3,2,1,0:T(8,128)(2,1)S(1)}, u32[]{:S(2)}, u32[]{:S(2)}) collective-permute-start(bf16[2,1,2,128,128]{4,3,2,1,0:T(8,128)(2,1)S(1)} %pad_maximum_fusion.3), channel_id=1, source_target_pairs={{0,64},{8,72},{16,80},{24,88},{32,96},{40,104},{48,112},{56,120},{... | collective-permute-start | bytes 393224 | tf_op jit(solution)/shard_map/ppermute | solution.py:18
  75.3 15.9 %collective-permute-start.11 = (bf16[2,1,2,128,128]{4,3,2,1,0:T(8,128)(2,1)S(1)}, bf16[2,1,2,128,128]{4,3,2,1,0:T(8,128)(2,1)S(1)}, u32[]{:S(2)}, u32[]{:S(2)}) collective-permute-start(bf16[2,1,2,128,128]{4,3,2,1,0:T(8,128)(2,1)S(1)} %pad_maximum_fusion.9), channel_id=1, source_target_pairs={{0,8},{8,16},{16,24},{24,32},{32,40},{40,48},{48,56},{56,64},{64,7... | collective-permute-start | bytes 393224 | tf_op jit(solution)/shard_map/ppermute | solution.py:18
  77.9 13.2 %collective-permute-start.12 = (bf16[1,2,128,128]{3,2,1,0:T(8,128)(2,1)S(1)}, bf16[1,2,128,128]{3,2,1,0:T(8,128)(2,1)S(1)}, u32[]{:S(2)}, u32[]{:S(2)}) collective-permute-start(bf16[1,2,128,128]{3,2,1,0:T(8,128)(2,1)S(1)} %bitcast.315), channel_id=1, source_target_pairs={{0,136},{8,144},{16,152},{24,160},{32,168},{40,176},{48,184},{56,1... | collective-permute-start | bytes 196616 | tf_op jit(solution)/shard_map/ppermute | solution.py:18
  86.6 5.9 %collective-permute-start.5 = (bf16[2,1,2,128,128]{4,3,2,1,0:T(8,128)(2,1)S(1)}, bf16[2,1,2,128,128]{4,3,2,1,0:T(8,128)(2,1)S(1)}, u32[]{:S(2)}, u32[]{:S(2)}) collective-permute-start(bf16[2,1,2,128,128]{4,3,2,1,0:T(8,128)(2,1)S(1)} %pad_maximum_fusion.4), channel_id=1, source_target_pairs={{0,8},{8,16},{16,24},{24,32},{32,40},{40,48},{48,56},{56,64},{64,7... | collective-permute-start | bytes 393224 | tf_op jit(solution)/shard_map/ppermute | solution.py:18
  88.5 4.0 %collective-permute-start.6 = (bf16[1,2,128,128]{3,2,1,0:T(8,128)(2,1)S(1)}, bf16[1,2,128,128]{3,2,1,0:T(8,128)(2,1)S(1)}, u32[]{:S(2)}, u32[]{:S(2)}) collective-permute-start(bf16[1,2,128,128]{3,2,1,0:T(8,128)(2,1)S(1)} %bitcast.313), channel_id=1, source_target_pairs={{0,136},{8,144},{16,152},{24,160},{32,168},{40,176},{48,184},{56,1... | collective-permute-start | bytes 196616 | tf_op jit(solution)/shard_map/ppermute | solution.py:18
  97.4 10.8 %collective-permute-start.13 = (bf16[4,32,2048]{2,1,0:T(8,128)(2,1)S(1)}, bf16[4,32,2048]{2,1,0:T(8,128)(2,1)S(1)}, u32[]{:S(2)}, u32[]{:S(2)}) collective-permute-start(bf16[4,32,2048]{2,1,0:T(8,128)(2,1)S(1)} %fusion.28), channel_id=1, source_target_pairs={{0,1},{1,0},{2,3},{3,2},{4,5},{5,4},{6,7},{7,6},{8,9},{9,8},{10,11... | collective-permute-start | bytes 1572872 | tf_op jit(solution)/shard_map/ppermute | solution.py:211
  109.6 7.7 %collective-permute-start.16 = (bf16[32,2048]{1,0:T(8,128)(2,1)S(1)}, bf16[32,2048]{1,0:T(8,128)(2,1)S(1)}, u32[]{:S(2)}, u32[]{:S(2)}) collective-permute-start(bf16[32,2048]{1,0:T(8,128)(2,1)S(1)} %get-tuple-element.10), channel_id=1, source_target_pairs={{0,6},{1,7},{2,0},{3,1},{4,2},{5,3},{6,4},{7,5},{8,14},{9,15},{10,... | collective-permute-start | bytes 393224 | tf_op jit(solution)/shard_map/ppermute | solution.py:217
  112.2 5.9 %collective-permute-start.15 = (bf16[32,2048]{1,0:T(8,128)(2,1)S(1)}, bf16[32,2048]{1,0:T(8,128)(2,1)S(1)}, u32[]{:S(2)}, u32[]{:S(2)}) collective-permute-start(bf16[32,2048]{1,0:T(8,128)(2,1)S(1)} %get-tuple-element.11), channel_id=1, source_target_pairs={{0,4},{1,5},{2,6},{3,7},{4,0},{5,1},{6,2},{7,3},{8,12},{9,13},{10,... | collective-permute-start | bytes 393224 | tf_op jit(solution)/shard_map/ppermute | solution.py:217
  112.7 9.2 %collective-permute-start.14 = (bf16[32,2048]{1,0:T(8,128)(2,1)S(1)}, bf16[32,2048]{1,0:T(8,128)(2,1)S(1)}, u32[]{:S(2)}, u32[]{:S(2)}) collective-permute-start(bf16[32,2048]{1,0:T(8,128)(2,1)S(1)} %get-tuple-element.9), channel_id=1, source_target_pairs={{0,2},{1,3},{2,4},{3,5},{4,6},{5,7},{6,0},{7,1},{8,10},{9,11},{10,... | collective-permute-start | bytes 393224 | tf_op jit(solution)/shard_map/ppermute | solution.py:217
  (5 other events, 10.3 us)

commit v11 on v10

--- a/solution.py
+++ b/solution.py
@@ -113,7 +113,7 @@
     seq_index = lax.axis_index("seq")
     prefix_map, prefix_end = total_map, local_end
     distance = 1
-    while 2 * distance < seq_size:
+    while 4 * distance < seq_size:
         earlier_map, earlier_end = shifted(
             jnp.stack([prefix_map, prefix_end]).astype(jnp.bfloat16), "seq", distance
         ).astype(jnp.float32)
@@ -122,11 +122,15 @@
             seq_index >= distance, apply_map(prefix_map, earlier_map), prefix_map
         )
         distance *= 2
-    last_map, last_end = shifted(
-        jnp.stack([prefix_map, prefix_end]).astype(jnp.bfloat16), "seq", 1
+    windows = -(-seq_size // distance)
+    incoming = shifted(
+        prefix_end.astype(jnp.bfloat16), "seq", 1 + (windows - 1) * distance
     ).astype(jnp.float32)
-    far_end = shifted(prefix_end.astype(jnp.bfloat16), "seq", distance + 1).astype(jnp.float32)
-    incoming = apply_map(last_map, far_end) + last_end
+    for window in range(windows - 2, -1, -1):
+        window_map, window_end = shifted(
+            jnp.stack([prefix_map, prefix_end]).astype(jnp.bfloat16), "seq", 1 + window * distance
+        ).astype(jnp.float32)
+        incoming = apply_map(window_map, incoming) + window_end
 
     def replay(state_now, span_in):
         transit_now, inject_now, coupling_now, local_now = span_in

time: 123 us -> 128 us (1.041)
  waiting for transfers between devices: 10.2 us -> 13.1 us
  starting transfers between devices: 62.6 us -> 64 us
    ppermute x13 -> x15, starting transfers between devices: 49.7 us -> 52.9 us  [shifted(): return lax.ppermute(array, axis, pairs)]
    ppermute x13 -> x15, waiting for transfers between devices: 0.09 us -> 2.97 us  [shifted(): return lax.ppermute(array, axis, pairs)]
    ppermute x1, starting transfers between devices: 9.29 us -> 7.33 us  [shards(): lax.ppermute(pieces[:, 1 - parity].astype(jnp.bfloat16), 'head', sibling_...]
  transfers between devices with their start and end apart: 17 -> 19, of which waited for: 5 -> 6; matrix products, arithmetic and copies ran while one was open for 12% -> 11% of each run, Pallas kernels for 0% -> 0%
where the time goes in v11:
time: 128 us
  starting transfers between devices  64 us (50%)
  matrix products  27.7 us (22%)
  waiting for transfers between devices  13.1 us (10%)
  local copies, waits for them, and re-layouts  12.1 us (9%)
  other arithmetic  9.62 us (8%)
    ppermute x15, starting transfers between devices, shifted(): return lax.ppermute(array, axis, pairs)  52.9 us
    ppermute x3, waiting for transfers between devices, shards(): summed = summed + lax.ppermute(outgoing, 'head', pairs).astype(jnp.float32)  8.58 us
    dot_general x7, matrix products, unit_lower_inverse(): jnp.einsum('...ij,...jk->...ik', inverse, coupling, precision=highest)  7.42 us
    ppermute x1, starting transfers between devices, shards(): lax.ppermute(pieces[:, 1 - parity].astype(jnp.bfloat16), 'head', sibling_...  7.33 us
    dot_general x28, matrix products, apply_map(): return jnp.einsum('hrke,hrev->hrkv', matrix, state_now, precision=highest)  6.22 us
    dot_general x7, matrix products, unit_lower_inverse(): jnp.einsum('...ij,...jk->...ik', jnp.einsum('...ij,...jk->...ik', inverse...  4.52 us
    ppermute x3, starting transfers between devices, shards(): summed = summed + lax.ppermute(outgoing, 'head', pairs).astype(jnp.float32)  3.69 us
    slice x3, local copies, waits for them, and re-layouts, conv_silu(): summed = summed + conv_taps[offset] * padded[offset:offset + length]  3.1 us
  transfers between devices with their start and end apart: 19, of which 6 were waited for; matrix products, arithmetic and copies ran while one was open for 11% of the time, Pallas kernels for 0%

profile of v11, /device:TPU:17, one launch (start us, length us, event | category | flops | bytes accessed | tf_op | source)
XLA Modules:
  0.0 127.7 jit_solution(3976452152130111406)
XLA Ops:
  2.2 2.9 %collective-permute-start = (bf16[3,1024]{1,0:T(4,128)(2,1)S(1)}, bf16[3,1024]{1,0:T(4,128)(2,1)S(1)}, u32[]{:S(2)}, u32[]{:S(2)}) collective-permute-start(bf16[3,1024]{1,0:T(4,128)(2,1)S(1)} %pad_maximum_fusion.8), channel_id=1, source_target_pairs={{0,8},{8,16},{16,24},{24,32},{32,40},{40,48},{48,56},{56,64},{64,7... | collective-permute-start | bytes 18440 | tf_op jit(solution)/shard_map/ppermute | solution.py:18
  8.8 1.4 %fusion.158 = (f32[1,512]{1,0:T(1,128)S(1)}, f32[1,512]{1,0:T(1,128)}, f32[1,512]{1,0:T(1,128)}, f32[1,512]{1,0:T(1,128)}) fusion(bf16[4,512]{1,0:T(4,128)(2,1)} %param.19), kind=kLoop, calls=%fused_computation.338 | loop fusion | bytes 16384 | tf_op jit(solution)/shard_map/slice | solution.py:27
  15.3 1.4 %fusion.154 = f32[2,2,128,128]{3,2,1,0:T(8,128)} fusion(f32[2,2,128,128]{3,2,1,0:T(8,128)S(1)} %fusion.66, f32[2,128,2,128]{3,2,1,0:T(2,128)S(1)} %reshape.1176), kind=kOutput, calls=%fused_computation.334 | convolution fusion | flops 100663296 | bytes 786432 | tf_op jit(solution)/shard_map/hxnck,hxnek->hxnce/dot_general | solution.py:64
  26.8 2.1 %fusion.37 = f32[2,2,2,128,128]{4,3,2,1,0:T(8,128)S(1)} fusion(f32[2,2,2,128,128]{4,3,2,1,0:T(8,128)S(1)} %fusion.3, f32[2,2,128,128]{3,2,1,0:T(8,128)} %copy-done.5, f32[2,2,2,128]{3,2,1,0:T(2,128)S(1)} %mul.296, f32[128,128]{1,0:T(8,128)S(1)} %fusion.141, f32[2,2,2,128]{3,2,1,0:T(2,128)S(1)} %reduce_window_sum.11, ...), kind=kOutput, calls=%fused_computation.87 | convolution fusion | flops 202375168 | bytes 1433600 | tf_op jit(solution)/shard_map/...ij,...jk->...ik/dot_general | solution.py:43
  37.1 3.3 %collective-permute-start.8 = (bf16[2,1,2,128,128]{4,3,2,1,0:T(8,128)(2,1)S(1)}, bf16[2,1,2,128,128]{4,3,2,1,0:T(8,128)(2,1)S(1)}, u32[]{:S(2)}, u32[]{:S(2)}) collective-permute-start(bf16[2,1,2,128,128]{4,3,2,1,0:T(8,128)(2,1)S(1)} %pad_maximum_fusion.4), channel_id=1, source_target_pairs={{0,8},{8,16},{16,24},{24,32},{32,40},{40,48},{48,56},{56,64},{64,7... | collective-permute-start | bytes 393224 | tf_op jit(solution)/shard_map/ppermute | solution.py:18
  42.9 3.2 %collective-permute-start.1 = (bf16[2,1,2,128,128]{4,3,2,1,0:T(8,128)(2,1)S(1)}, bf16[2,1,2,128,128]{4,3,2,1,0:T(8,128)(2,1)S(1)}, u32[]{:S(2)}, u32[]{:S(2)}) collective-permute-start(bf16[2,1,2,128,128]{4,3,2,1,0:T(8,128)(2,1)S(1)} %pad_maximum_fusion), channel_id=1, source_target_pairs={{0,8},{8,16},{16,24},{24,32},{32,40},{40,48},{48,56},{56,64},{64,7... | collective-permute-start | bytes 393224 | tf_op jit(solution)/shard_map/ppermute | solution.py:18
  47.5 3.3 %collective-permute-start.9 = (bf16[2,1,2,128,128]{4,3,2,1,0:T(8,128)(2,1)S(1)}, bf16[2,1,2,128,128]{4,3,2,1,0:T(8,128)(2,1)S(1)}, u32[]{:S(2)}, u32[]{:S(2)}) collective-permute-start(bf16[2,1,2,128,128]{4,3,2,1,0:T(8,128)(2,1)S(1)} %pad_maximum_fusion.5), channel_id=1, source_target_pairs={{0,16},{8,24},{16,32},{24,40},{32,48},{40,56},{48,64},{56,72},{64,... | collective-permute-start | bytes 393224 | tf_op jit(solution)/shard_map/ppermute | solution.py:18
  51.3 4.8 %collective-permute-start.2 = (bf16[2,1,2,128,128]{4,3,2,1,0:T(8,128)(2,1)S(1)}, bf16[2,1,2,128,128]{4,3,2,1,0:T(8,128)(2,1)S(1)}, u32[]{:S(2)}, u32[]{:S(2)}) collective-permute-start(bf16[2,1,2,128,128]{4,3,2,1,0:T(8,128)(2,1)S(1)} %pad_maximum_fusion.1), channel_id=1, source_target_pairs={{0,16},{8,24},{16,32},{24,40},{32,48},{40,56},{48,64},{56,72},{64,... | collective-permute-start | bytes 393224 | tf_op jit(solution)/shard_map/ppermute | solution.py:18
  56.6 3.6 %collective-permute-start.10 = (bf16[2,1,2,128,128]{4,3,2,1,0:T(8,128)(2,1)S(1)}, bf16[2,1,2,128,128]{4,3,2,1,0:T(8,128)(2,1)S(1)}, u32[]{:S(2)}, u32[]{:S(2)}) collective-permute-start(bf16[2,1,2,128,128]{4,3,2,1,0:T(8,128)(2,1)S(1)} %pad_maximum_fusion.6), channel_id=1, source_target_pairs={{0,32},{8,40},{16,48},{24,56},{32,64},{40,72},{48,80},{56,88},{64,... | collective-permute-start | bytes 393224 | tf_op jit(solution)/shard_map/ppermute | solution.py:18
  60.7 4.8 %collective-permute-start.3 = (bf16[2,1,2,128,128]{4,3,2,1,0:T(8,128)(2,1)S(1)}, bf16[2,1,2,128,128]{4,3,2,1,0:T(8,128)(2,1)S(1)}, u32[]{:S(2)}, u32[]{:S(2)}) collective-permute-start(bf16[2,1,2,128,128]{4,3,2,1,0:T(8,128)(2,1)S(1)} %pad_maximum_fusion.2), channel_id=1, source_target_pairs={{0,32},{8,40},{16,48},{24,56},{32,64},{40,72},{48,80},{56,88},{64,... | collective-permute-start | bytes 393224 | tf_op jit(solution)/shard_map/ppermute | solution.py:18
  65.9 6.7 %collective-permute-start.13 = (bf16[2,1,2,128,128]{4,3,2,1,0:T(8,128)(2,1)S(1)}, bf16[2,1,2,128,128]{4,3,2,1,0:T(8,128)(2,1)S(1)}, u32[]{:S(2)}, u32[]{:S(2)}) collective-permute-start(bf16[2,1,2,128,128]{4,3,2,1,0:T(8,128)(2,1)S(1)} %pad_maximum_fusion.7), channel_id=1, source_target_pairs={{0,136},{8,144},{16,152},{24,160},{32,168},{40,176},{48,184},{56,1... | collective-permute-start | bytes 393224 | tf_op jit(solution)/shard_map/ppermute | solution.py:18
  72.5 1.9 %collective-permute-start.12 = (bf16[2,1,2,128,128]{4,3,2,1,0:T(8,128)(2,1)S(1)}, bf16[2,1,2,128,128]{4,3,2,1,0:T(8,128)(2,1)S(1)}, u32[]{:S(2)}, u32[]{:S(2)}) collective-permute-start(bf16[2,1,2,128,128]{4,3,2,1,0:T(8,128)(2,1)S(1)} %pad_maximum_fusion.7), channel_id=1, source_target_pairs={{0,72},{8,80},{16,88},{24,96},{32,104},{40,112},{48,120},{56,128},... | collective-permute-start | bytes 393224 | tf_op jit(solution)/shard_map/ppermute | solution.py:18
  74.4 3.5 %collective-permute-start.11 = (bf16[2,1,2,128,128]{4,3,2,1,0:T(8,128)(2,1)S(1)}, bf16[2,1,2,128,128]{4,3,2,1,0:T(8,128)(2,1)S(1)}, u32[]{:S(2)}, u32[]{:S(2)}) collective-permute-start(bf16[2,1,2,128,128]{4,3,2,1,0:T(8,128)(2,1)S(1)} %pad_maximum_fusion.7), channel_id=1, source_target_pairs={{0,8},{8,16},{16,24},{24,32},{32,40},{40,48},{48,56},{56,64},{64,7... | collective-permute-start | bytes 393224 | tf_op jit(solution)/shard_map/ppermute | solution.py:18
  80.9 2.6 %collective-permute-done.14 = bf16[1,2,128,128]{3,2,1,0:T(8,128)(2,1)S(1)} collective-permute-done((bf16[1,2,128,128]{3,2,1,0:T(8,128)(2,1)S(1)}, bf16[1,2,128,128]{3,2,1,0:T(8,128)(2,1)S(1)}, u32[]{:S(2)}, u32[]{:S(2)}) %collective-permute-start.14) | collective-permute-done | bytes 65568 | tf_op jit(solution)/shard_map/ppermute | solution.py:18
  84.8 2.8 %collective-permute-start.4 = (bf16[2,1,2,128,128]{4,3,2,1,0:T(8,128)(2,1)S(1)}, bf16[2,1,2,128,128]{4,3,2,1,0:T(8,128)(2,1)S(1)}, u32[]{:S(2)}, u32[]{:S(2)}) collective-permute-start(bf16[2,1,2,128,128]{4,3,2,1,0:T(8,128)(2,1)S(1)} %pad_maximum_fusion.3), channel_id=1, source_target_pairs={{0,8},{8,16},{16,24},{24,32},{32,40},{40,48},{48,56},{56,64},{64,7... | collective-permute-start | bytes 393224 | tf_op jit(solution)/shard_map/ppermute | solution.py:18
  87.8 8.4 %collective-permute-start.7 = (bf16[1,2,128,128]{3,2,1,0:T(8,128)(2,1)S(1)}, bf16[1,2,128,128]{3,2,1,0:T(8,128)(2,1)S(1)}, u32[]{:S(2)}, u32[]{:S(2)}) collective-permute-start(bf16[1,2,128,128]{3,2,1,0:T(8,128)(2,1)S(1)} %bitcast.325), channel_id=1, source_target_pairs={{0,200},{8,208},{16,216},{24,224},{32,232},{40,240},{48,248},{1,20... | collective-permute-start | bytes 196616 | tf_op jit(solution)/shard_map/ppermute | solution.py:18
  103.0 1.3 %copy-done.1 = f32[4,2,32,2048]{3,2,1,0:T(8,128)} copy-done((f32[4,2,32,2048]{3,2,1,0:T(8,128)}, f32[4,2,32,2048]{3,2,1,0:T(8,128)S(1)}, u32[]{:S(2)}) %copy-start.1) | copy-done | bytes 2097176
  104.4 7.3 %collective-permute-start.15 = (bf16[4,32,2048]{2,1,0:T(8,128)(2,1)S(1)}, bf16[4,32,2048]{2,1,0:T(8,128)(2,1)S(1)}, u32[]{:S(2)}, u32[]{:S(2)}) collective-permute-start(bf16[4,32,2048]{2,1,0:T(8,128)(2,1)S(1)} %fusion.28), channel_id=1, source_target_pairs={{0,1},{1,0},{2,3},{3,2},{4,5},{5,4},{6,7},{7,6},{8,9},{9,8},{10,11... | collective-permute-start | bytes 1572872 | tf_op jit(solution)/shard_map/ppermute | solution.py:215
  111.7 1.5 %collective-permute-done.15 = bf16[4,32,2048]{2,1,0:T(8,128)(2,1)S(1)} collective-permute-done((bf16[4,32,2048]{2,1,0:T(8,128)(2,1)S(1)}, bf16[4,32,2048]{2,1,0:T(8,128)(2,1)S(1)}, u32[]{:S(2)}, u32[]{:S(2)}) %collective-permute-start.15) | collective-permute-done | bytes 524320 | tf_op jit(solution)/shard_map/ppermute | solution.py:215
  113.3 1.3 %fusion.23 = bf16[4,32,2048]{2,1,0:T(8,128)(2,1)S(1)} fusion(bf16[4,32,2048]{2,1,0:T(8,128)(2,1)S(1)} %collective-permute-done.15, f32[4,2,32,2048]{3,2,1,0:T(8,128)} %copy-done.1, s32[]{:T(128)S(6)} %select_n.324), kind=kLoop, calls=%fused_computation.61 | loop fusion | flops 786432 | bytes 2097156 | tf_op jit(solution)/shard_map/convert_element_type | solution.py:216
  114.7 2.5 %collective-permute-start.18 = (bf16[32,2048]{1,0:T(8,128)(2,1)S(1)}, bf16[32,2048]{1,0:T(8,128)(2,1)S(1)}, u32[]{:S(2)}, u32[]{:S(2)}) collective-permute-start(bf16[32,2048]{1,0:T(8,128)(2,1)S(1)} %get-tuple-element.10), channel_id=1, source_target_pairs={{0,6},{1,7},{2,0},{3,1},{4,2},{5,3},{6,4},{7,5},{8,14},{9,15},{10,... | collective-permute-start | bytes 393224 | tf_op jit(solution)/shard_map/ppermute | solution.py:221
  118.4 1.9 %collective-permute-done.18 = bf16[32,2048]{1,0:T(8,128)(2,1)S(1)} collective-permute-done((bf16[32,2048]{1,0:T(8,128)(2,1)S(1)}, bf16[32,2048]{1,0:T(8,128)(2,1)S(1)}, u32[]{:S(2)}, u32[]{:S(2)}) %collective-permute-start.18) | collective-permute-done | bytes 131104 | tf_op jit(solution)/shard_map/ppermute | solution.py:221
  120.2 2.9 %collective-permute-done.17 = bf16[32,2048]{1,0:T(8,128)(2,1)S(1)} collective-permute-done((bf16[32,2048]{1,0:T(8,128)(2,1)S(1)}, bf16[32,2048]{1,0:T(8,128)(2,1)S(1)}, u32[]{:S(2)}, u32[]{:S(2)}) %collective-permute-start.17) | collective-permute-done | bytes 131104 | tf_op jit(solution)/shard_map/ppermute | solution.py:221
  123.1 3.8 %collective-permute-done.16 = bf16[32,2048]{1,0:T(8,128)(2,1)S(1)} collective-permute-done((bf16[32,2048]{1,0:T(8,128)(2,1)S(1)}, bf16[32,2048]{1,0:T(8,128)(2,1)S(1)}, u32[]{:S(2)}, u32[]{:S(2)}) %collective-permute-start.16) | collective-permute-done | bytes 131104 | tf_op jit(solution)/shard_map/ppermute | solution.py:221
  (165 shorter events, 47.3 us)
Async XLA Ops:
  0.0 102.3 %copy-start = (bf16[512,2048]{1,0:T(8,128)(2,1)S(1)}, bf16[512,2048]{1,0:T(8,128)(2,1)}, u32[]{:S(2)}) copy-start(bf16[512,2048]{1,0:T(8,128)(2,1)} %param.21) | copy-start | bytes 6291460
  2.2 9.8 %collective-permute-start = (bf16[3,1024]{1,0:T(4,128)(2,1)S(1)}, bf16[3,1024]{1,0:T(4,128)(2,1)S(1)}, u32[]{:S(2)}, u32[]{:S(2)}) collective-permute-start(bf16[3,1024]{1,0:T(4,128)(2,1)S(1)} %pad_maximum_fusion.8), channel_id=1, source_target_pairs={{0,8},{8,16},{16,24},{24,32},{32,40},{40,48},{48,56},{56,64},{64,7... | collective-permute-start | bytes 18440 | tf_op jit(solution)/shard_map/ppermute | solution.py:18
  14.9 10.2 %copy-start.5 = (f32[2,2,128,128]{3,2,1,0:T(8,128)}, f32[2,2,128,128]{3,2,1,0:T(8,128)S(1)}, u32[]{:S(2)}) copy-start(f32[2,2,128,128]{3,2,1,0:T(8,128)S(1)} %fusion.161) | copy-start | bytes 786436
  26.7 2.9 %copy-start.6 = (f32[1,512]{1,0:T(1,128)S(1)}, f32[1,512]{1,0:T(1,128)}, u32[]{:S(2)}) copy-start(f32[1,512]{1,0:T(1,128)} %get-tuple-element.28) | copy-start | bytes 6148
  34.8 5.7 %copy-start.2 = (f32[2,2,128,128]{3,2,1,0:T(8,128)S(1)}, f32[2,2,128,128]{3,2,1,0:T(8,128)}, u32[]{:S(2)}) copy-start(f32[2,2,128,128]{3,2,1,0:T(8,128)} %fusion.154) | copy-start | bytes 786436
  37.1 9.0 %copy-start.3 = (f32[2,128,2,128]{3,1,0,2:T(8,128)S(1)}, f32[2,128,2,128]{3,1,0,2:T(8,128)}, u32[]{:S(2)}) copy-start(f32[2,128,2,128]{3,1,0,2:T(8,128)} %copy.91) | copy-start | bytes 786436
  37.1 9.8 %collective-permute-start.8 = (bf16[2,1,2,128,128]{4,3,2,1,0:T(8,128)(2,1)S(1)}, bf16[2,1,2,128,128]{4,3,2,1,0:T(8,128)(2,1)S(1)}, u32[]{:S(2)}, u32[]{:S(2)}) collective-permute-start(bf16[2,1,2,128,128]{4,3,2,1,0:T(8,128)(2,1)S(1)} %pad_maximum_fusion.4), channel_id=1, source_target_pairs={{0,8},{8,16},{16,24},{24,32},{32,40},{40,48},{48,56},{56,64},{64,7... | collective-permute-start | bytes 393224 | tf_op jit(solution)/shard_map/ppermute | solution.py:18
  42.9 7.9 %collective-permute-start.1 = (bf16[2,1,2,128,128]{4,3,2,1,0:T(8,128)(2,1)S(1)}, bf16[2,1,2,128,128]{4,3,2,1,0:T(8,128)(2,1)S(1)}, u32[]{:S(2)}, u32[]{:S(2)}) collective-permute-start(bf16[2,1,2,128,128]{4,3,2,1,0:T(8,128)(2,1)S(1)} %pad_maximum_fusion), channel_id=1, source_target_pairs={{0,8},{8,16},{16,24},{24,32},{32,40},{40,48},{48,56},{56,64},{64,7... | collective-permute-start | bytes 393224 | tf_op jit(solution)/shard_map/ppermute | solution.py:18
  47.5 8.7 %collective-permute-start.9 = (bf16[2,1,2,128,128]{4,3,2,1,0:T(8,128)(2,1)S(1)}, bf16[2,1,2,128,128]{4,3,2,1,0:T(8,128)(2,1)S(1)}, u32[]{:S(2)}, u32[]{:S(2)}) collective-permute-start(bf16[2,1,2,128,128]{4,3,2,1,0:T(8,128)(2,1)S(1)} %pad_maximum_fusion.5), channel_id=1, source_target_pairs={{0,16},{8,24},{16,32},{24,40},{32,48},{40,56},{48,64},{56,72},{64,... | collective-permute-start | bytes 393224 | tf_op jit(solution)/shard_map/ppermute | solution.py:18
  51.3 8.9 %collective-permute-start.2 = (bf16[2,1,2,128,128]{4,3,2,1,0:T(8,128)(2,1)S(1)}, bf16[2,1,2,128,128]{4,3,2,1,0:T(8,128)(2,1)S(1)}, u32[]{:S(2)}, u32[]{:S(2)}) collective-permute-start(bf16[2,1,2,128,128]{4,3,2,1,0:T(8,128)(2,1)S(1)} %pad_maximum_fusion.1), channel_id=1, source_target_pairs={{0,16},{8,24},{16,32},{24,40},{32,48},{40,56},{48,64},{56,72},{64,... | collective-permute-start | bytes 393224 | tf_op jit(solution)/shard_map/ppermute | solution.py:18
  56.6 8.8 %collective-permute-start.10 = (bf16[2,1,2,128,128]{4,3,2,1,0:T(8,128)(2,1)S(1)}, bf16[2,1,2,128,128]{4,3,2,1,0:T(8,128)(2,1)S(1)}, u32[]{:S(2)}, u32[]{:S(2)}) collective-permute-start(bf16[2,1,2,128,128]{4,3,2,1,0:T(8,128)(2,1)S(1)} %pad_maximum_fusion.6), channel_id=1, source_target_pairs={{0,32},{8,40},{16,48},{24,56},{32,64},{40,72},{48,80},{56,88},{64,... | collective-permute-start | bytes 393224 | tf_op jit(solution)/shard_map/ppermute | solution.py:18
  60.7 18.5 %collective-permute-start.3 = (bf16[2,1,2,128,128]{4,3,2,1,0:T(8,128)(2,1)S(1)}, bf16[2,1,2,128,128]{4,3,2,1,0:T(8,128)(2,1)S(1)}, u32[]{:S(2)}, u32[]{:S(2)}) collective-permute-start(bf16[2,1,2,128,128]{4,3,2,1,0:T(8,128)(2,1)S(1)} %pad_maximum_fusion.2), channel_id=1, source_target_pairs={{0,32},{8,40},{16,48},{24,56},{32,64},{40,72},{48,80},{56,88},{64,... | collective-permute-start | bytes 393224 | tf_op jit(solution)/shard_map/ppermute | solution.py:18
  65.9 18.9 %collective-permute-start.13 = (bf16[2,1,2,128,128]{4,3,2,1,0:T(8,128)(2,1)S(1)}, bf16[2,1,2,128,128]{4,3,2,1,0:T(8,128)(2,1)S(1)}, u32[]{:S(2)}, u32[]{:S(2)}) collective-permute-start(bf16[2,1,2,128,128]{4,3,2,1,0:T(8,128)(2,1)S(1)} %pad_maximum_fusion.7), channel_id=1, source_target_pairs={{0,136},{8,144},{16,152},{24,160},{32,168},{40,176},{48,184},{56,1... | collective-permute-start | bytes 393224 | tf_op jit(solution)/shard_map/ppermute | solution.py:18
  72.5 15.3 %collective-permute-start.12 = (bf16[2,1,2,128,128]{4,3,2,1,0:T(8,128)(2,1)S(1)}, bf16[2,1,2,128,128]{4,3,2,1,0:T(8,128)(2,1)S(1)}, u32[]{:S(2)}, u32[]{:S(2)}) collective-permute-start(bf16[2,1,2,128,128]{4,3,2,1,0:T(8,128)(2,1)S(1)} %pad_maximum_fusion.7), channel_id=1, source_target_pairs={{0,72},{8,80},{16,88},{24,96},{32,104},{40,112},{48,120},{56,128},... | collective-permute-start | bytes 393224 | tf_op jit(solution)/shard_map/ppermute | solution.py:18
  74.4 22.0 %collective-permute-start.11 = (bf16[2,1,2,128,128]{4,3,2,1,0:T(8,128)(2,1)S(1)}, bf16[2,1,2,128,128]{4,3,2,1,0:T(8,128)(2,1)S(1)}, u32[]{:S(2)}, u32[]{:S(2)}) collective-permute-start(bf16[2,1,2,128,128]{4,3,2,1,0:T(8,128)(2,1)S(1)} %pad_maximum_fusion.7), channel_id=1, source_target_pairs={{0,8},{8,16},{16,24},{24,32},{32,40},{40,48},{48,56},{56,64},{64,7... | collective-permute-start | bytes 393224 | tf_op jit(solution)/shard_map/ppermute | solution.py:18
  77.9 5.6 %collective-permute-start.14 = (bf16[1,2,128,128]{3,2,1,0:T(8,128)(2,1)S(1)}, bf16[1,2,128,128]{3,2,1,0:T(8,128)(2,1)S(1)}, u32[]{:S(2)}, u32[]{:S(2)}) collective-permute-start(bf16[1,2,128,128]{3,2,1,0:T(8,128)(2,1)S(1)} %bitcast.327), channel_id=1, source_target_pairs={{0,200},{8,208},{16,216},{24,224},{32,232},{40,240},{48,248},{1,20... | collective-permute-start | bytes 196616 | tf_op jit(solution)/shard_map/ppermute | solution.py:18
  79.6 17.7 %collective-permute-start.6 = (bf16[2,1,2,128,128]{4,3,2,1,0:T(8,128)(2,1)S(1)}, bf16[2,1,2,128,128]{4,3,2,1,0:T(8,128)(2,1)S(1)}, u32[]{:S(2)}, u32[]{:S(2)}) collective-permute-start(bf16[2,1,2,128,128]{4,3,2,1,0:T(8,128)(2,1)S(1)} %pad_maximum_fusion.3), channel_id=1, source_target_pairs={{0,136},{8,144},{16,152},{24,160},{32,168},{40,176},{48,184},{56,1... | collective-permute-start | bytes 393224 | tf_op jit(solution)/shard_map/ppermute | solution.py:18
  83.5 13.9 %collective-permute-start.5 = (bf16[2,1,2,128,128]{4,3,2,1,0:T(8,128)(2,1)S(1)}, bf16[2,1,2,128,128]{4,3,2,1,0:T(8,128)(2,1)S(1)}, u32[]{:S(2)}, u32[]{:S(2)}) collective-permute-start(bf16[2,1,2,128,128]{4,3,2,1,0:T(8,128)(2,1)S(1)} %pad_maximum_fusion.3), channel_id=1, source_target_pairs={{0,72},{8,80},{16,88},{24,96},{32,104},{40,112},{48,120},{56,128},... | collective-permute-start | bytes 393224 | tf_op jit(solution)/shard_map/ppermute | solution.py:18
  84.8 13.7 %collective-permute-start.4 = (bf16[2,1,2,128,128]{4,3,2,1,0:T(8,128)(2,1)S(1)}, bf16[2,1,2,128,128]{4,3,2,1,0:T(8,128)(2,1)S(1)}, u32[]{:S(2)}, u32[]{:S(2)}) collective-permute-start(bf16[2,1,2,128,128]{4,3,2,1,0:T(8,128)(2,1)S(1)} %pad_maximum_fusion.3), channel_id=1, source_target_pairs={{0,8},{8,16},{16,24},{24,32},{32,40},{40,48},{48,56},{56,64},{64,7... | collective-permute-start | bytes 393224 | tf_op jit(solution)/shard_map/ppermute | solution.py:18
  87.8 9.5 %collective-permute-start.7 = (bf16[1,2,128,128]{3,2,1,0:T(8,128)(2,1)S(1)}, bf16[1,2,128,128]{3,2,1,0:T(8,128)(2,1)S(1)}, u32[]{:S(2)}, u32[]{:S(2)}) collective-permute-start(bf16[1,2,128,128]{3,2,1,0:T(8,128)(2,1)S(1)} %bitcast.325), channel_id=1, source_target_pairs={{0,200},{8,208},{16,216},{24,224},{32,232},{40,240},{48,248},{1,20... | collective-permute-start | bytes 196616 | tf_op jit(solution)/shard_map/ppermute | solution.py:18
  104.4 8.9 %collective-permute-start.15 = (bf16[4,32,2048]{2,1,0:T(8,128)(2,1)S(1)}, bf16[4,32,2048]{2,1,0:T(8,128)(2,1)S(1)}, u32[]{:S(2)}, u32[]{:S(2)}) collective-permute-start(bf16[4,32,2048]{2,1,0:T(8,128)(2,1)S(1)} %fusion.28), channel_id=1, source_target_pairs={{0,1},{1,0},{2,3},{3,2},{4,5},{5,4},{6,7},{7,6},{8,9},{9,8},{10,11... | collective-permute-start | bytes 1572872 | tf_op jit(solution)/shard_map/ppermute | solution.py:215
  114.7 5.5 %collective-permute-start.18 = (bf16[32,2048]{1,0:T(8,128)(2,1)S(1)}, bf16[32,2048]{1,0:T(8,128)(2,1)S(1)}, u32[]{:S(2)}, u32[]{:S(2)}) collective-permute-start(bf16[32,2048]{1,0:T(8,128)(2,1)S(1)} %get-tuple-element.10), channel_id=1, source_target_pairs={{0,6},{1,7},{2,0},{3,1},{4,2},{5,3},{6,4},{7,5},{8,14},{9,15},{10,... | collective-permute-start | bytes 393224 | tf_op jit(solution)/shard_map/ppermute | solution.py:221
  117.2 5.9 %collective-permute-start.17 = (bf16[32,2048]{1,0:T(8,128)(2,1)S(1)}, bf16[32,2048]{1,0:T(8,128)(2,1)S(1)}, u32[]{:S(2)}, u32[]{:S(2)}) collective-permute-start(bf16[32,2048]{1,0:T(8,128)(2,1)S(1)} %get-tuple-element.11), channel_id=1, source_target_pairs={{0,4},{1,5},{2,6},{3,7},{4,0},{5,1},{6,2},{7,3},{8,12},{9,13},{10,... | collective-permute-start | bytes 393224 | tf_op jit(solution)/shard_map/ppermute | solution.py:221
  117.7 9.2 %collective-permute-start.16 = (bf16[32,2048]{1,0:T(8,128)(2,1)S(1)}, bf16[32,2048]{1,0:T(8,128)(2,1)S(1)}, u32[]{:S(2)}, u32[]{:S(2)}) collective-permute-start(bf16[32,2048]{1,0:T(8,128)(2,1)S(1)} %get-tuple-element.9), channel_id=1, source_target_pairs={{0,2},{1,3},{2,4},{3,5},{4,6},{5,7},{6,0},{7,1},{8,10},{9,11},{10,... | collective-permute-start | bytes 393224 | tf_op jit(solution)/shard_map/ppermute | solution.py:221
  (6 other events, 14.7 us)
